TPU v7x, 512 devices: a whole 4x4x16 slice. The times are simulated.
512 devices in a mesh: gx: 16 (over z_hi, x), gy: 8 (over y, core), gz: 4 (over z_lo).
Axes of the slice: x: 4, y: 4, z: 16 (z_hi: 4, z_lo: 4; z = z_hi * 4 + z_lo), core: 2. Of those that a mesh axis runs over, the one named last changes fastest.
Arguments:
- features: bfloat16 [16, 8, 4, 4096, 128], P('gx', 'gy', 'gz'), may hold values from -6 to 6
- output_grad: bfloat16 [16, 8, 4, 4096, 128], P('gx', 'gy', 'gz'), may hold values from -6 to 6
- kernel: bfloat16 [27, 128, 128], replicated, may hold values from -0.5 to 0.5
- inner_map: int32 [16, 8, 4, 288, 3], P('gx', 'gy', 'gz'), may hold values from 0 to 31, as said below
- outer_map: int32 [16, 8, 4, 32, 3], P('gx', 'gy', 'gz'), may hold values from 0 to 55, as said below
- face_blocks: int32 [16, 8, 4, 3, 2, 4], P('gx', 'gy', 'gz'), may hold values from 0 to 31, as said below
- inner_live: int32 [16, 8, 4], P('gx', 'gy', 'gz'), may hold values from 72 to 288, as said below
- outer_live: int32 [16, 8, 4], P('gx', 'gy', 'gz'), may hold values from 16 to 32, as said below
Outputs:
- input_grad: bfloat16 [16, 8, 4, 4096, 128], P('gx', 'gy', 'gz')
- weight_grad: bfloat16 [27, 128, 128], replicated
Inputs may be any that keep to these rules, and one draw needn't show every extreme that they name: `inner_map`: offsets lie in 0 to 26, output and input blocks in 0 to 31; every entry is valid, live or not. `outer_map`: offsets lie in 0 to 26, received blocks in 32 to 55, input blocks in 0 to 31; every entry is valid, live or not. Pairs may name a neighbour that does not exist; its blocks are zero. `face_blocks`: block indices of the brick itself; they may repeat. `inner_live`: some brick has all 288 entries live in every draw. `outer_live`: some brick has all 32 entries live in every draw.
All inputs are finite; a program needn't handle non-finite values.
Results may differ from a plain program's by a relative error of at most 0.001.
Values may be sent and summed in bfloat16 or wider, within the bound.
No kernel may reach another device: no remote copies, remote signals or barrier semaphores. Data moves between devices by JAX's collectives and lax.ppermute only.
A program may use at most 64 MiB of HBM per device.

v0:
```python
import math

import jax
import jax.numpy as jnp
from jax import lax
from jax.sharding import PartitionSpec as P

C = 128
BLOCK = 128
NB = 32
PI = 288


pair_group = 8


def extended(shard, sides, width):
    for axis, dim in sides:
        count, length = (lax.axis_size(axis), shard.shape[dim])
        up = [(i, (i + 1) % count) for i in range(count - 1)]
        down = [(j, i) for i, j in up]
        last = lax.slice_in_dim(shard, length - width, length, axis=dim)
        initial = lax.slice_in_dim(shard, 0, width, axis=dim)
        before = lax.ppermute(last, axis, up)
        after = lax.ppermute(initial, axis, down)
        shard = jnp.concatenate([before, shard, after], axis=dim)
    return shard


def run_pairs(gradient_table, local_feats, kernel, pair_list, live_count, running):
    turns = (live_count + pair_group - 1) // pair_group

    def one_group(turn_index, state_pair):
        input_acc, weight_acc = state_pair
        chosen = lax.dynamic_slice_in_dim(pair_list, turn_index * pair_group, pair_group, 0)
        offsets = chosen[:, 0]
        out_blocks = chosen[:, 1]
        in_blocks = chosen[:, 2]
        slot_index = turn_index * pair_group + jnp.arange(pair_group, dtype=jnp.int32)
        live_mask = (slot_index < live_count).astype(jnp.float32)[:, None, None]
        grad_rows = gradient_table[out_blocks]
        feat_rows = local_feats[in_blocks]
        kernels = kernel[offsets]
        backward = (
            jnp.einsum("prd,pcd->prc", grad_rows, kernels, preferred_element_type=jnp.float32)
            * live_mask
        )
        outer_terms = (
            jnp.einsum("prc,prd->pcd", feat_rows, grad_rows, preferred_element_type=jnp.float32)
            * live_mask
        )
        return (input_acc.at[in_blocks].add(backward), weight_acc.at[offsets].add(outer_terms))

    return lax.fori_loop(0, turns, one_group, running)


def build_table(local_grads, face_lists):
    got_x = extended(local_grads[face_lists[0]], (("gx", 0),), 1)
    got_y = extended(local_grads[face_lists[1]], (("gy", 0),), 1)
    got_z = extended(local_grads[face_lists[2]], (("gz", 0),), 1)
    return jnp.concatenate(
        [local_grads, got_x[0], got_x[3], got_y[0], got_y[3], got_z[0], got_z[3]], axis=0
    )


def body(features, output_grad, kernel, inner_map, outer_map, face_blocks, inner_live, outer_live):
    local_grads = output_grad[0, 0, 0].reshape(NB, BLOCK, C)
    local_feats = features[0, 0, 0].reshape(NB, BLOCK, C)
    face_lists = face_blocks[0, 0, 0]
    inner_pairs = inner_map[0, 0, 0]
    outer_pairs = outer_map[0, 0, 0]
    running = (jnp.zeros((NB, BLOCK, C), jnp.float32), jnp.zeros((27, C, C), jnp.float32))
    gradient_table = build_table(local_grads, face_lists)
    running = run_pairs(
        gradient_table, local_feats, kernel, inner_pairs, inner_live[0, 0, 0], running
    )
    running = run_pairs(
        gradient_table, local_feats, kernel, outer_pairs, outer_live[0, 0, 0], running
    )
    input_acc, weight_acc = running
    bricks_all = lax.axis_size("gx") * lax.axis_size("gy") * lax.axis_size("gz")
    grad_scale = math.sqrt(27.0 / (bricks_all * PI * BLOCK))
    summed = lax.psum(weight_acc, ("gx", "gy", "gz"))
    weight_grad = (summed * grad_scale).astype(jnp.bfloat16)
    input_grad = input_acc.astype(jnp.bfloat16).reshape(1, 1, 1, NB * BLOCK, C)
    return (input_grad, weight_grad)


def solution(mesh):
    in_specs = (
        P("gx", "gy", "gz", None, None),
        P("gx", "gy", "gz", None, None),
        P(),
        P("gx", "gy", "gz", None, None),
        P("gx", "gy", "gz", None, None),
        P("gx", "gy", "gz", None, None, None),
        P("gx", "gy", "gz"),
        P("gx", "gy", "gz"),
    )
    out_specs = (P("gx", "gy", "gz", None, None), P())
    return jax.shard_map(body, mesh=mesh, in_specs=in_specs, out_specs=out_specs, check_vma=False)
```

profile of v0, /device:TPU:1, one launch (start us, length us, event | category | flops | bytes accessed | tf_op | source)
XLA Modules:
  0.0 960.7 jit_solution(12962348174245009417)
XLA Ops:
  10.0 4.0 collective-permute-start
  17.3 4.0 collective-permute-start.2
  21.3 3.4 collective-permute-start.3
  30.4 4.7 collective-permute-done.5
  37.1 227.1 %while.24 = (s32[]{:T(128)}, f32[32,128,128]{2,1,0:T(8,128)}, f32[27,128,128]{2,1,0:T(8,128)S(1)}, s32[]{:T(128)}, s32[288,3]{0,1:T(4,128)S(1)}, /*index=5*/bf16...) while((s32[]{:T(128)}, f32[32,128,128]{2,1,0:T(8,128)}, ...), condition=%wide.region_3.4_spmd, body=%wide.region_0.3_spmd.sunk | while | flops 67636320 | bytes 6828951 | solution.py:54
  39.0 2.1 gather_fusion
  42.1 2.7 scatter_fusion
  49.8 2.1 gather_fusion
  52.8 2.7 scatter_fusion
  60.6 2.1 gather_fusion
  63.7 2.7 scatter_fusion
  71.4 2.1 gather_fusion
  74.5 2.7 scatter_fusion
  82.2 2.1 gather_fusion
  85.3 2.7 scatter_fusion
  93.1 2.1 gather_fusion
  96.1 2.7 scatter_fusion
  103.9 2.1 gather_fusion
  106.9 2.7 scatter_fusion
  114.7 2.1 gather_fusion
  117.8 2.7 scatter_fusion
  128.6 2.7 scatter_fusion
  136.3 2.1 gather_fusion
  139.4 2.7 scatter_fusion
  150.2 2.7 scatter_fusion
  158.0 2.1 gather_fusion
  161.0 2.7 scatter_fusion
  168.8 2.1 gather_fusion
  171.8 2.7 scatter_fusion
  182.7 2.7 scatter_fusion
  193.5 2.7 scatter_fusion
  201.2 2.1 gather_fusion
  204.3 2.7 scatter_fusion
  212.0 2.1 gather_fusion
  215.1 2.7 scatter_fusion
  222.8 2.1 gather_fusion
  225.9 2.7 scatter_fusion
  236.7 2.7 scatter_fusion
  244.5 2.1 gather_fusion
  247.6 2.7 scatter_fusion
  258.3 2.7 scatter_fusion
  264.2 32.5 %while.25 = (s32[]{:T(128)}, f32[32,128,128]{2,1,0:T(8,128)}, f32[27,128,128]{2,1,0:T(8,128)S(1)}, s32[]{:T(128)}, s32[32,3]{0,1:T(4,128)S(1)}, /*index=5*/bf16[...) while((s32[]{:T(128)}, f32[32,128,128]{2,1,0:T(8,128)}, ...), condition=%wide.region_7.8_spmd, body=%wide.region_4.7_spmd.sunk | while | flops 67636320 | bytes 6828951 | solution.py:54
  269.2 2.7 scatter_fusion.2
  280.0 2.7 scatter_fusion.2
  290.8 2.7 scatter_fusion.2
  298.0 2.7 convert_element_type.20
  300.7 650.5 %all-reduce.2.cloned.1.call-done = f32[27,128,128]{2,1,0:T(8,128)} async-done(((f32[27,128,128]{2,1,0:T(8,128)}), f32[27,128,128]{2,1,0:T(8,128)}) %all-reduce.2.cloned.1.call-update) | async-done | bytes 1769488 | tf_op jit(solution)/shard_map/psum | solution.py:83
  951.2 2.6 multiply_convert_fusion
  (292 shorter events, 175.0 us)
Async XLA Ops:
  7.2 17.6 %copy-start.2 = (bf16[1,1,1,4096,128]{4,3,2,1,0:T(8,128)(2,1)S(1)}, bf16[1,1,1,4096,128]{4,3,2,1,0:T(8,128)(2,1)}, u32[]{:S(2)}) copy-start(bf16[1,1,1,4096,128]{4,3,2,1,0:T(8,128)(2,1)} %param.13) | copy-start | bytes 3145732
  7.2 21.6 %copy-start.3 = (s32[1,1,1,288,3]{3,2,4,1,0:T(1,128)S(1)}, s32[1,1,1,288,3]{3,2,4,1,0:T(1,128)}, u32[]{:S(2)}) copy-start(s32[1,1,1,288,3]{3,2,4,1,0:T(1,128)} %param.15) | copy-start | bytes 10372
  7.2 21.6 %copy-start.4 = (s32[1,1,1,32,3]{3,2,4,1,0:T(1,128)S(1)}, s32[1,1,1,32,3]{3,2,4,1,0:T(1,128)}, u32[]{:S(2)}) copy-start(s32[1,1,1,32,3]{3,2,4,1,0:T(1,128)} %param.16) | copy-start | bytes 1156
  7.2 944.0 %all-reduce.2.cloned.1.call-start = ((), (), s32[]{:S(2)}) async-start(), calls=%async_computation | async-start | bytes 3538944 | tf_op jit(solution)/shard_map/psum | solution.py:83
  10.0 19.0 %collective-permute-start = (bf16[1,4,128,128]{3,2,1,0:T(8,128)(2,1)S(1)}, bf16[1,4,128,128]{3,2,1,0:T(8,128)(2,1)S(1)}, u32[]{:S(2)}, u32[]{:S(2)}) collective-permute-start(bf16[1,4,128,128]{3,2,1,0:T(8,128)(2,1)S(1)} %get-tuple-element.155), channel_id=1, source_target_pairs={{0,32},{32,64},{64,96},{96,128},{128,160},{160,192},{192,224},{224... | collective-permute-start | bytes 393224 | tf_op jit(solution)/shard_map/ppermute | solution.py:24
  13.9 16.3 %collective-permute-start.1 = (bf16[1,4,128,128]{3,2,1,0:T(8,128)(2,1)S(1)}, bf16[1,4,128,128]{3,2,1,0:T(8,128)(2,1)S(1)}, u32[]{:S(2)}, u32[]{:S(2)}) collective-permute-start(bf16[1,4,128,128]{3,2,1,0:T(8,128)(2,1)S(1)} %get-tuple-element.154), channel_id=1, source_target_pairs={{32,0},{64,32},{96,64},{128,96},{160,128},{192,160},{224,192},{256... | collective-permute-start | bytes 393224 | tf_op jit(solution)/shard_map/ppermute | solution.py:25
  17.3 13.0 %collective-permute-start.2 = (bf16[1,4,128,128]{3,2,1,0:T(8,128)(2,1)S(1)}, bf16[1,4,128,128]{3,2,1,0:T(8,128)(2,1)S(1)}, u32[]{:S(2)}, u32[]{:S(2)}) collective-permute-start(bf16[1,4,128,128]{3,2,1,0:T(8,128)(2,1)S(1)} %get-tuple-element.153), channel_id=1, source_target_pairs={{0,4},{4,8},{8,12},{12,16},{16,20},{20,24},{24,28},{1,5},{5,9},{9,... | collective-permute-start | bytes 393224 | tf_op jit(solution)/shard_map/ppermute | solution.py:24
  21.3 9.0 collective-permute-start.3
  25.4 5.0 collective-permute-start.4
  28.9 6.2 collective-permute-start.5
  35.1 1.9 copy-start.1
  296.7 1.3 copy-start
Sparse Core Ops, SparseCore 0:
  298.1 653.0 all-reduce.1
where the time goes:
time: 968 us; the launch traced here: 961 us
  waiting for transfers between devices  655 us (68%)
  local copies, waits for them, and re-layouts  146 us (15%)
  other arithmetic  112 us (12%)
  starting transfers between devices  16.1 us (2%)
  between operations  15.7 us (2%)
  matrix products  13.9 us (1%)
    psum x1, waiting for transfers between devices, body(): summed = lax.psum(weight_acc, ('gx', 'gy', 'gz'))  650 us
    scatter-add x24, other arithmetic, one_group(): input_acc.at[in_blocks].add(backward)  64.6 us
    gather x24, local copies, waits for them, and re-layouts, one_group(): grad_rows = gradient_table[out_blocks]  50.3 us
    gather x24, local copies, waits for them, and re-layouts, one_group(): feat_rows = local_feats[in_blocks]  43.7 us
    gather x24, local copies, waits for them, and re-layouts, one_group(): kernels = kernel[offsets]  42.3 us
    scatter-add x24, other arithmetic, one_group(): weight_acc.at[offsets].add(outer_terms)  24.8 us
  transfers between devices with their start and end apart: 7, of which 2 were waited for; matrix products, arithmetic and copies ran while one was open for 1% of the time, Pallas kernels for 0%

commit v1 on v0

v1 whole, which is shorter than its diff:
```python
import math

import jax
import jax.numpy as jnp
from jax import lax
from jax.experimental import pallas as pl
from jax.experimental.pallas import tpu as pltpu
from jax.sharding import PartitionSpec as P

C = 128
BLOCK = 128
NB = 32
PI = 288
PB = 32


def extended(shard, sides, width):
    for axis, dim in sides:
        count, length = (lax.axis_size(axis), shard.shape[dim])
        up = [(i, (i + 1) % count) for i in range(count - 1)]
        down = [(j, i) for i, j in up]
        last = lax.slice_in_dim(shard, length - width, length, axis=dim)
        initial = lax.slice_in_dim(shard, 0, width, axis=dim)
        before = lax.ppermute(last, axis, up)
        after = lax.ppermute(initial, axis, down)
        shard = jnp.concatenate([before, shard, after], axis=dim)
    return shard


def received_blocks(local_grads, face_lists):
    got_x = extended(local_grads[face_lists[0]], (("gx", 0),), 1)
    got_y = extended(local_grads[face_lists[1]], (("gy", 0),), 1)
    got_z = extended(local_grads[face_lists[2]], (("gz", 0),), 1)
    return jnp.concatenate(
        [got_x[0], got_x[3], got_y[0], got_y[3], got_z[0], got_z[3]], axis=0
    )


def pair_loop(pairs_ref, live_ref, table_ref, ft_ref, kt_ref, acc_in, acc_w, table_base):
    def one_pair(i, carry):
        k = pairs_ref[3 * i]
        a = pairs_ref[3 * i + 1] - table_base
        b = pairs_ref[3 * i + 2]
        g = table_ref[a]
        acc_in[b] += jnp.dot(g, kt_ref[k], preferred_element_type=jnp.float32)
        acc_w[k] += jnp.dot(ft_ref[b], g, preferred_element_type=jnp.float32)
        return carry

    lax.fori_loop(0, live_ref[0], one_pair, 0)


def inner_kernel(pairs_ref, live_ref, table_ref, ft_ref, kt_ref, acc_in, acc_w):
    acc_in[...] = jnp.zeros_like(acc_in)
    acc_w[...] = jnp.zeros_like(acc_w)
    pair_loop(pairs_ref, live_ref, table_ref, ft_ref, kt_ref, acc_in, acc_w, 0)


def outer_kernel(pairs_ref, live_ref, table_ref, ft_ref, kt_ref, in_start, w_start, grad_out, acc_w, acc_in):
    acc_in[...] = in_start[...]
    acc_w[...] = w_start[...]
    pair_loop(pairs_ref, live_ref, table_ref, ft_ref, kt_ref, acc_in, acc_w, NB)
    grad_out[...] = acc_in[...].astype(grad_out.dtype)


def vmem():
    return pl.BlockSpec(memory_space=pltpu.MemorySpace.VMEM)


def smem():
    return pl.BlockSpec(memory_space=pltpu.MemorySpace.SMEM)


def run_inner(pairs, live, table, ft, kt):
    n = pairs.shape[0] // 3
    return pl.pallas_call(
        inner_kernel,
        out_shape=(
            jax.ShapeDtypeStruct((NB, BLOCK, C), jnp.float32),
            jax.ShapeDtypeStruct((27, C, C), jnp.float32),
        ),
        in_specs=[smem(), smem(), vmem(), vmem(), vmem()],
        out_specs=(vmem(), vmem()),
        cost_estimate=pl.CostEstimate(
            flops=4 * n * BLOCK * C * C, transcendentals=0, bytes_accessed=8 * 1024 * 1024
        ),
        name="inner_pairs",
    )(pairs, live, table, ft, kt)


def run_outer(pairs, live, table, ft, kt, acc_in, acc_w):
    n = pairs.shape[0] // 3
    return pl.pallas_call(
        outer_kernel,
        out_shape=(
            jax.ShapeDtypeStruct((NB, BLOCK, C), jnp.bfloat16),
            jax.ShapeDtypeStruct((27, C, C), jnp.float32),
        ),
        in_specs=[smem(), smem(), vmem(), vmem(), vmem(), vmem(), vmem()],
        out_specs=(vmem(), vmem()),
        scratch_shapes=[pltpu.VMEM((NB, BLOCK, C), jnp.float32)],
        cost_estimate=pl.CostEstimate(
            flops=4 * n * BLOCK * C * C, transcendentals=0, bytes_accessed=8 * 1024 * 1024
        ),
        name="outer_pairs",
    )(pairs, live, table, ft, kt, acc_in, acc_w)


def reduce_weights(weight_acc, grad_scale):
    flat = weight_acc.reshape(-1)
    for axis in ("gy", "gz", "gx"):
        n = lax.axis_size(axis)
        parts = lax.all_to_all(flat.reshape(n, -1), axis, 0, 0, tiled=True)
        flat = parts.reshape(n, -1).sum(axis=0)
    piece = (flat * grad_scale).astype(jnp.bfloat16)
    n = lax.axis_size("gx")
    copies = jnp.broadcast_to(piece[None], (n,) + piece.shape)
    piece = lax.all_to_all(copies, "gx", 0, 0, tiled=True).reshape(-1)
    piece = lax.all_gather(piece, "gz", tiled=True)
    piece = lax.all_gather(piece, "gy", tiled=True)
    return piece.reshape(weight_acc.shape)


def body(features, output_grad, kernel, inner_map, outer_map, face_blocks, inner_live, outer_live):
    local_grads = output_grad[0, 0, 0].reshape(NB, BLOCK, C)
    feats_t = jnp.swapaxes(features[0, 0, 0].reshape(NB, BLOCK, C), 1, 2)
    kernel_t = jnp.swapaxes(kernel, 1, 2)
    inner_pairs = inner_map[0, 0, 0].reshape(-1)
    outer_pairs = outer_map[0, 0, 0].reshape(-1)
    inner_n = jnp.clip(inner_live[0, 0, 0], 0, PI).reshape(1)
    outer_n = jnp.clip(outer_live[0, 0, 0], 0, PB).reshape(1)
    received = received_blocks(local_grads, face_blocks[0, 0, 0])
    acc_in, acc_w = run_inner(inner_pairs, inner_n, local_grads, feats_t, kernel_t)
    input_grad, acc_w = run_outer(outer_pairs, outer_n, received, feats_t, kernel_t, acc_in, acc_w)
    bricks_all = lax.axis_size("gx") * lax.axis_size("gy") * lax.axis_size("gz")
    grad_scale = math.sqrt(27.0 / (bricks_all * PI * BLOCK))
    weight_grad = reduce_weights(acc_w, grad_scale)
    return (input_grad.reshape(1, 1, 1, NB * BLOCK, C), weight_grad)


def solution(mesh):
    in_specs = (
        P("gx", "gy", "gz", None, None),
        P("gx", "gy", "gz", None, None),
        P(),
        P("gx", "gy", "gz", None, None),
        P("gx", "gy", "gz", None, None),
        P("gx", "gy", "gz", None, None, None),
        P("gx", "gy", "gz"),
        P("gx", "gy", "gz"),
    )
    out_specs = (P("gx", "gy", "gz", None, None), P())
    return jax.shard_map(body, mesh=mesh, in_specs=in_specs, out_specs=out_specs, check_vma=False)
```

time: 968 us -> 219 us (0.23)
  waiting for transfers between devices: 655 us -> 4.26 us
  local copies, waits for them, and re-layouts: 146 us -> 13.3 us
  blocking collectives: 0 us -> 130 us
  other arithmetic: 112 us -> 4 us
  Pallas kernels: 0 us -> 49.2 us
  matrix products: 13.9 us -> 0 us
  between operations: 15.7 us -> 2.24 us
    psum x1 -> x0, waiting for transfers between devices: 650 us -> none  [body(): summed = lax.psum(weight_acc, ('gx', 'gy', 'gz'))]
    gather x75 -> x3, local copies, waits for them, and re-layouts: 141 us -> 5.46 us  [the longest x1 1.82 us: received_blocks(): got_z = extended(local_grads[face_lists[2]], (('gz', 0),), 1)]
    all_to_all x0 -> x4, blocking collectives: none -> 96.9 us  [the longest x3 80.2 us: reduce_weights(): parts = lax.all_to_all(flat.reshape(n, -1), axis, 0, 0, tiled=True)]
    scatter-add x48 -> x0, other arithmetic: 89.4 us -> none  [the longest x24 64.6 us: one_group(): input_acc.at[in_blocks].add(backward)]
    pallas_call x0 -> x2, Pallas kernels: none -> 49.2 us  [the longest x1 40.1 us: run_inner(): pl.pallas_call(inner_kernel, out_shape=(jax.ShapeDtypeStruct((NB, BLOCK,...]
    all_gather x0 -> x2, blocking collectives: none -> 32.7 us  [the longest x1 21.5 us: reduce_weights(): piece = lax.all_gather(piece, 'gy', tiled=True)]
    convert_element_type x26 -> x1, other arithmetic: 21 us -> 0.01 us  [reduce_weights(): piece = (flat * grad_scale).astype(jnp.bfloat16)]
    dot_general x48 -> x0, matrix products: 13.9 us -> none  [the longest x24 7.13 us: one_group(): jnp.einsum('prd,pcd->prc', grad_rows, kernels, preferred_element_type=jnp...]
  transfers between devices with their start and end apart: 7 -> 6, of which waited for: 2 -> 1; matrix products, arithmetic and copies ran while one was open for 1% -> 4% of each run, Pallas kernels for 0% -> 18%
where the time goes in v1:
time: 219 us
  blocking collectives  130 us (59%)
  Pallas kernels  49.2 us (22%)
  starting transfers between devices  16.2 us (7%)
  local copies, waits for them, and re-layouts  13.3 us (6%)
  waiting for transfers between devices  4.26 us (2%)
  other arithmetic  4 us (2%)
  between operations  2.24 us (1%)
    all_to_all x3, blocking collectives, reduce_weights(): parts = lax.all_to_all(flat.reshape(n, -1), axis, 0, 0, tiled=True)  80.2 us
    pallas_call x1, Pallas kernels, run_inner(): pl.pallas_call(inner_kernel, out_shape=(jax.ShapeDtypeStruct((NB, BLOCK,...  40.1 us
    all_gather x1, blocking collectives, reduce_weights(): piece = lax.all_gather(piece, 'gy', tiled=True)  21.5 us
    all_to_all x1, blocking collectives, reduce_weights(): piece = lax.all_to_all(copies, 'gx', 0, 0, tiled=True).reshape(-1)  16.7 us
    all_gather x1, blocking collectives, reduce_weights(): piece = lax.all_gather(piece, 'gz', tiled=True)  11.2 us
    ppermute x3, starting transfers between devices, extended(): before = lax.ppermute(last, axis, up)  10.2 us
    pallas_call x1, Pallas kernels, run_outer(): pl.pallas_call(outer_kernel, out_shape=(jax.ShapeDtypeStruct((NB, BLOCK,...  9.16 us
    ppermute x3, starting transfers between devices, extended(): after = lax.ppermute(initial, axis, down)  5.96 us
  transfers between devices with their start and end apart: 6, of which 1 were waited for; matrix products, arithmetic and copies ran while one was open for 4% of the time, Pallas kernels for 18%

profile of v1, /device:TPU:1, one launch (start us, length us, event | category | flops | bytes accessed | tf_op | source)
XLA Modules:
  0.0 218.9 jit_solution(7130855172426940505)
XLA Ops:
  0.6 0.8 compare_select_fusion
  1.4 0.1 reshape.148
  1.5 1.8 gather_fusion
  3.4 4.0 %collective-permute-start = (bf16[1,4,128,128]{3,2,1,0:T(8,128)(2,1)S(1)}, bf16[1,4,128,128]{3,2,1,0:T(8,128)(2,1)S(1)}, u32[]{:S(2)}, u32[]{:S(2)}) collective-permute-start(bf16[1,4,128,128]{3,2,1,0:T(8,128)(2,1)S(1)} %get-tuple-element.15), channel_id=1, source_target_pairs={{0,32},{32,64},{64,96},{96,128},{128,160},{160,192},{192,224},{224... | collective-permute-start | bytes 393224 | tf_op jit(solution)/shard_map/ppermute | solution.py:24
  7.4 1.3 collective-permute-start.1
  8.7 0.1 reshape.156
  8.7 0.1 reshape.164
  8.8 1.8 gather_fusion.1
  10.7 0.0 copy-start.2
  10.7 4.2 %collective-permute-start.2 = (bf16[1,4,128,128]{3,2,1,0:T(8,128)(2,1)S(1)}, bf16[1,4,128,128]{3,2,1,0:T(8,128)(2,1)S(1)}, u32[]{:S(2)}, u32[]{:S(2)}) collective-permute-start(bf16[1,4,128,128]{3,2,1,0:T(8,128)(2,1)S(1)} %get-tuple-element.13), channel_id=1, source_target_pairs={{0,4},{4,8},{8,12},{12,16},{16,20},{20,24},{24,28},{1,5},{5,9},{9,... | collective-permute-start | bytes 393224 | tf_op jit(solution)/shard_map/ppermute | solution.py:24
  14.9 3.4 %collective-permute-start.3 = (bf16[1,4,128,128]{3,2,1,0:T(8,128)(2,1)S(1)}, bf16[1,4,128,128]{3,2,1,0:T(8,128)(2,1)S(1)}, u32[]{:S(2)}, u32[]{:S(2)}) collective-permute-start(bf16[1,4,128,128]{3,2,1,0:T(8,128)(2,1)S(1)} %get-tuple-element.12), channel_id=1, source_target_pairs={{4,0},{8,4},{12,8},{16,12},{20,16},{24,20},{28,24},{5,1},{9,5},{13... | collective-permute-start | bytes 393224 | tf_op jit(solution)/shard_map/ppermute | solution.py:25
  18.3 1.8 gather_fusion.2
  20.1 2.1 collective-permute-start.4
  22.2 0.0 copy-start.3
  22.2 0.0 copy-start.4
  22.3 1.3 copy.27
  23.6 1.6 copy.28
  25.2 0.1 copy.29
  25.4 0.8 reshape_squeeze.15.pairs_ref
  26.8 0.1 copy.26
  26.9 0.6 reshape_squeeze.12.pairs_ref
  28.2 40.1 %inner_pairs.1 = (f32[32,128,128]{2,1,0:T(8,128)}, f32[27,128,128]{2,1,0:T(8,128)}) custom-call(s32[864]{0:T(1024)} %reshape_squeeze.15.pairs_ref, s32[1]{0:T(128)} %bitcast.20.live_ref, bf16[32,128,128]{2,1,0:T(8,128)(2,1)} %bitcast.61, bf16[32,128,128]{2,1,0:T(8,128)(2,1)} %bitcast.50, bf16[27,128,128]{2,1,0:T(8,128)(2,1)} %bitcast.53), custom_call_target="tpu_custom_call" | custom-call | flops 2415919104 | bytes 8388608 | tf_op jit(solution)/shard_map/inner_pairs/pallas_call | solution.py:75
  68.3 0.0 collective-permute-done
  68.3 1.3 collective-permute-start.5
  69.6 0.0 collective-permute-done.1
  69.6 0.0 collective-permute-done.2
  69.6 0.0 collective-permute-done.3
  69.7 0.0 collective-permute-done.4
  69.7 4.2 %collective-permute-done.5 = bf16[1,4,128,128]{3,2,1,0:T(8,128)(2,1)S(1)} collective-permute-done((bf16[1,4,128,128]{3,2,1,0:T(8,128)(2,1)S(1)}, bf16[1,4,128,128]{3,2,1,0:T(8,128)(2,1)S(1)}, u32[]{:S(2)}, u32[]{:S(2)}) %collective-permute-start.5) | collective-permute-done | bytes 131104 | tf_op jit(solution)/shard_map/ppermute | solution.py:25
  74.0 0.9 copy-done
  74.9 9.2 %outer_pairs.1 = (bf16[32,128,128]{2,1,0:T(8,128)(2,1)}, f32[27,128,128]{2,1,0:T(8,128)}) custom-call(s32[96]{0:T(128)} %reshape_squeeze.12.pairs_ref, s32[1]{0:T(128)} %bitcast.live_ref, bf16[24,128,128]{2,1,0:T(8,128)(2,1)} %copy-done, bf16[32,128,128]{2,1,0:T(8,128)(2,1)} %bitcast.51, bf16[27,128,128]{2,1,0:T(8,128)(2,1)} %bitcast.54, ...), custom_call_target="tpu_custom_call" | custom-call | flops 268435456 | bytes 8388608 | tf_op jit(solution)/shard_map/outer_pairs/pallas_call | solution.py:92
  84.0 31.1 %all_to_all.33 = f32[8,1,55296]{2,1,0:T(1,128)S(1)} all-to-all(f32[8,1,55296]{2,1,0:T(1,128)} %bitcast.55), channel_id=1, replica_groups=mesh['gx'=16,'gy'=8,'gz'=4] {'gy'}, dimensions={0} | all-to-all | bytes 3538944 | tf_op jit(solution)/shard_map/all_to_all | solution.py:112
  115.2 1.3 reduce_sum.27
  116.4 8.1 %all_to_all.34 = f32[4,1,13824]{2,1,0:T(1,128)S(1)} all-to-all(f32[4,1,13824]{2,1,0:T(1,128)S(1)} %bitcast.57), channel_id=1, replica_groups=mesh['gx'=16,'gy'=8,'gz'=4] {'gz'}, dimensions={0} | all-to-all | bytes 442368 | tf_op jit(solution)/shard_map/all_to_all | solution.py:112
  124.6 0.2 reduce_sum.28
  124.8 0.1 all_to_all.26
  124.9 40.9 %all_to_all.35 = f32[16,1,864]{2,1,0:T(1,128)S(1)} all-to-all(f32[16,1,864]{2,1,0:T(1,128)S(1)} %all_to_all.26), channel_id=1, replica_groups=mesh['gx'=16,'gy'=8,'gz'=4] {'gx'}, dimensions={0} | all-to-all | bytes 110592 | tf_op jit(solution)/shard_map/all_to_all | solution.py:112
  166.0 0.5 broadcast.78
  166.5 0.8 reduce.5
  167.3 0.1 reshape.184
  167.4 16.7 %all_to_all.36 = bf16[16,2,432]{2,1,0:T(2,128)(2,1)S(1)} all-to-all(bf16[16,2,432]{2,1,0:T(2,128)(2,1)S(1)} %reshape.184), channel_id=1, replica_groups=mesh['gx'=16,'gy'=8,'gz'=4] {'gx'}, dimensions={0} | all-to-all | bytes 55296 | tf_op jit(solution)/shard_map/all_to_all | solution.py:117
  184.1 0.1 reshape.185
  184.2 0.2 reduce.3
  184.4 0.1 reshape.179
  184.5 11.2 %all-gather = bf16[4,1,13824]{2,1,0:T(2,128)(2,1)S(1)} all-gather(bf16[1,1,13824]{2,1,0:T(2,128)(2,1)S(1)} %reshape.179), channel_id=1, replica_groups=mesh['gx'=16,'gy'=8,'gz'=4] {'gz'}, dimensions={0}, use_global_device_ids=true | all-gather | bytes 138240 | tf_op jit(solution)/shard_map/all_gather | solution.py:118
  195.7 0.7 reduce.4
  196.4 21.5 %all_gather.7 = bf16[442368]{0:T(1024)(128)(2,1)S(1)} all-gather(bf16[55296]{0:T(1024)(128)(2,1)S(1)} %reshape.180), channel_id=1, replica_groups=mesh['gx'=16,'gy'=8,'gz'=4] {'gy'}, dimensions={0}, use_global_device_ids=true | all-gather | bytes 995328 | tf_op jit(solution)/shard_map/all_gather | solution.py:119
  217.9 0.9 copy.43
  (21 shorter events, 0.3 us)
Async XLA Ops:
  0.6 21.6 %copy-start.1 = (bf16[1,1,1,4096,128]{4,3,2,1,0:T(8,128)(2,1)S(1)}, bf16[1,1,1,4096,128]{4,3,2,1,0:T(8,128)(2,1)}, u32[]{:S(2)}) copy-start(bf16[1,1,1,4096,128]{4,3,2,1,0:T(8,128)(2,1)} %param.8) | copy-start | bytes 3145732
  3.4 64.9 %collective-permute-start = (bf16[1,4,128,128]{3,2,1,0:T(8,128)(2,1)S(1)}, bf16[1,4,128,128]{3,2,1,0:T(8,128)(2,1)S(1)}, u32[]{:S(2)}, u32[]{:S(2)}) collective-permute-start(bf16[1,4,128,128]{3,2,1,0:T(8,128)(2,1)S(1)} %get-tuple-element.15), channel_id=1, source_target_pairs={{0,32},{32,64},{64,96},{96,128},{128,160},{160,192},{192,224},{224... | collective-permute-start | bytes 393224 | tf_op jit(solution)/shard_map/ppermute | solution.py:24
  7.4 62.2 %collective-permute-start.1 = (bf16[1,4,128,128]{3,2,1,0:T(8,128)(2,1)S(1)}, bf16[1,4,128,128]{3,2,1,0:T(8,128)(2,1)S(1)}, u32[]{:S(2)}, u32[]{:S(2)}) collective-permute-start(bf16[1,4,128,128]{3,2,1,0:T(8,128)(2,1)S(1)} %get-tuple-element.14), channel_id=1, source_target_pairs={{32,0},{64,32},{96,64},{128,96},{160,128},{192,160},{224,192},{256... | collective-permute-start | bytes 393224 | tf_op jit(solution)/shard_map/ppermute | solution.py:25
  10.7 12.9 %copy-start.2 = (bf16[27,128,128]{2,1,0:T(8,128)(2,1)S(1)}, bf16[27,128,128]{2,1,0:T(8,128)(2,1)}, u32[]{:S(2)}) copy-start(bf16[27,128,128]{2,1,0:T(8,128)(2,1)} %param.10) | copy-start | bytes 2654212
  10.7 58.9 %collective-permute-start.2 = (bf16[1,4,128,128]{3,2,1,0:T(8,128)(2,1)S(1)}, bf16[1,4,128,128]{3,2,1,0:T(8,128)(2,1)S(1)}, u32[]{:S(2)}, u32[]{:S(2)}) collective-permute-start(bf16[1,4,128,128]{3,2,1,0:T(8,128)(2,1)S(1)} %get-tuple-element.13), channel_id=1, source_target_pairs={{0,4},{4,8},{8,12},{12,16},{16,20},{20,24},{24,28},{1,5},{5,9},{9,... | collective-permute-start | bytes 393224 | tf_op jit(solution)/shard_map/ppermute | solution.py:24
  14.9 54.8 %collective-permute-start.3 = (bf16[1,4,128,128]{3,2,1,0:T(8,128)(2,1)S(1)}, bf16[1,4,128,128]{3,2,1,0:T(8,128)(2,1)S(1)}, u32[]{:S(2)}, u32[]{:S(2)}) collective-permute-start(bf16[1,4,128,128]{3,2,1,0:T(8,128)(2,1)S(1)} %get-tuple-element.12), channel_id=1, source_target_pairs={{4,0},{8,4},{12,8},{16,12},{20,16},{24,20},{28,24},{5,1},{9,5},{13... | collective-permute-start | bytes 393224 | tf_op jit(solution)/shard_map/ppermute | solution.py:25
  20.1 49.6 %collective-permute-start.4 = (bf16[1,4,128,128]{3,2,1,0:T(8,128)(2,1)S(1)}, bf16[1,4,128,128]{3,2,1,0:T(8,128)(2,1)S(1)}, u32[]{:S(2)}, u32[]{:S(2)}) collective-permute-start(bf16[1,4,128,128]{3,2,1,0:T(8,128)(2,1)S(1)} %get-tuple-element.11), channel_id=1, source_target_pairs={{0,1},{1,2},{2,3},{4,5},{5,6},{6,7},{8,9},{9,10},{10,11},{12,13},{... | collective-permute-start | bytes 393224 | tf_op jit(solution)/shard_map/ppermute | solution.py:24
  22.2 3.0 %copy-start.3 = (s32[1,1,1,288,3]{3,2,4,1,0:T(1,128)S(1)}, s32[1,1,1,288,3]{3,2,4,1,0:T(1,128)}, u32[]{:S(2)}) copy-start(s32[1,1,1,288,3]{3,2,4,1,0:T(1,128)} %param.11) | copy-start | bytes 10372
  22.2 4.6 %copy-start.4 = (s32[1,1,1,32,3]{3,2,4,1,0:T(1,128)S(1)}, s32[1,1,1,32,3]{3,2,4,1,0:T(1,128)}, u32[]{:S(2)}) copy-start(s32[1,1,1,32,3]{3,2,4,1,0:T(1,128)} %param.12) | copy-start | bytes 1156
  68.3 5.7 %collective-permute-start.5 = (bf16[1,4,128,128]{3,2,1,0:T(8,128)(2,1)S(1)}, bf16[1,4,128,128]{3,2,1,0:T(8,128)(2,1)S(1)}, u32[]{:S(2)}, u32[]{:S(2)}) collective-permute-start(bf16[1,4,128,128]{3,2,1,0:T(8,128)(2,1)S(1)} %get-tuple-element.10), channel_id=1, source_target_pairs={{1,0},{2,1},{3,2},{5,4},{6,5},{7,6},{9,8},{10,9},{11,10},{13,12},{... | collective-permute-start | bytes 393224 | tf_op jit(solution)/shard_map/ppermute | solution.py:25
  74.0 0.9 copy-start

commit v2 on v1

--- a/solution.py
+++ b/solution.py
@@ -12,6 +12,7 @@
 NB = 32
 PI = 288
 PB = 32
+UNROLL = 4
 
 
 def extended(shard, sides, width):
@@ -37,16 +38,36 @@
 
 
 def pair_loop(pairs_ref, live_ref, table_ref, ft_ref, kt_ref, acc_in, acc_w, table_base):
+    def pair_ids(i):
+        return (pairs_ref[3 * i], pairs_ref[3 * i + 1] - table_base, pairs_ref[3 * i + 2])
+
+    def one_group(group, carry):
+        ids = [pair_ids(group * UNROLL + j) for j in range(UNROLL)]
+        grads = [table_ref[a] for _, a, _ in ids]
+        to_in = [
+            jnp.dot(g, kt_ref[k], preferred_element_type=jnp.float32)
+            for g, (k, _, _) in zip(grads, ids)
+        ]
+        to_w = [
+            jnp.dot(ft_ref[b], g, preferred_element_type=jnp.float32)
+            for g, (_, _, b) in zip(grads, ids)
+        ]
+        for (k, _, b), p_in, p_w in zip(ids, to_in, to_w):
+            acc_in[b] += p_in
+            acc_w[k] += p_w
+        return carry
+
     def one_pair(i, carry):
-        k = pairs_ref[3 * i]
-        a = pairs_ref[3 * i + 1] - table_base
-        b = pairs_ref[3 * i + 2]
+        k, a, b = pair_ids(i)
         g = table_ref[a]
         acc_in[b] += jnp.dot(g, kt_ref[k], preferred_element_type=jnp.float32)
         acc_w[k] += jnp.dot(ft_ref[b], g, preferred_element_type=jnp.float32)
         return carry
 
-    lax.fori_loop(0, live_ref[0], one_pair, 0)
+    live = live_ref[0]
+    groups = live // UNROLL
+    lax.fori_loop(0, groups, one_group, 0)
+    lax.fori_loop(groups * UNROLL, live, one_pair, 0)
 
 
 def inner_kernel(pairs_ref, live_ref, table_ref, ft_ref, kt_ref, acc_in, acc_w):

time: 219 us -> 188 us (0.86)
  Pallas kernels: 49.2 us -> 18.3 us
  blocking collectives: 130 us -> 122 us
  waiting for transfers between devices: 4.26 us -> 12 us
    pallas_call x1, Pallas kernels: 40.1 us -> 11.5 us  [run_inner(): pl.pallas_call(inner_kernel, out_shape=(jax.ShapeDtypeStruct((NB, BLOCK,...]
    all_to_all x3, blocking collectives: 80.2 us -> 72.3 us  [reduce_weights(): parts = lax.all_to_all(flat.reshape(n, -1), axis, 0, 0, tiled=True)]
    ppermute x3, waiting for transfers between devices: 4.25 us -> 12 us  [extended(): after = lax.ppermute(initial, axis, down)]
    pallas_call x1, Pallas kernels: 9.16 us -> 6.85 us  [run_outer(): pl.pallas_call(outer_kernel, out_shape=(jax.ShapeDtypeStruct((NB, BLOCK,...]
  transfers between devices with their start and end apart: 6 -> 6, of which waited for: 1 -> 1; matrix products, arithmetic and copies ran while one was open for 4% -> 5% of each run, Pallas kernels for 18% -> 6%
where the time goes in v2:
time: 188 us
  blocking collectives  122 us (65%)
  Pallas kernels  18.3 us (10%)
  starting transfers between devices  16.2 us (9%)
  local copies, waits for them, and re-layouts  13.3 us (7%)
  waiting for transfers between devices  12 us (6%)
  other arithmetic  4 us (2%)
  between operations  2.24 us (1%)
    all_to_all x3, blocking collectives, reduce_weights(): parts = lax.all_to_all(flat.reshape(n, -1), axis, 0, 0, tiled=True)  72.3 us
    all_gather x1, blocking collectives, reduce_weights(): piece = lax.all_gather(piece, 'gy', tiled=True)  21.5 us
    all_to_all x1, blocking collectives, reduce_weights(): piece = lax.all_to_all(copies, 'gx', 0, 0, tiled=True).reshape(-1)  16.7 us
    ppermute x3, waiting for transfers between devices, extended(): after = lax.ppermute(initial, axis, down)  12 us
    pallas_call x1, Pallas kernels, run_inner(): pl.pallas_call(inner_kernel, out_shape=(jax.ShapeDtypeStruct((NB, BLOCK,...  11.5 us
    all_gather x1, blocking collectives, reduce_weights(): piece = lax.all_gather(piece, 'gz', tiled=True)  11.2 us
    ppermute x3, starting transfers between devices, extended(): before = lax.ppermute(last, axis, up)  10.2 us
    pallas_call x1, Pallas kernels, run_outer(): pl.pallas_call(outer_kernel, out_shape=(jax.ShapeDtypeStruct((NB, BLOCK,...  6.85 us
  transfers between devices with their start and end apart: 6, of which 1 were waited for; matrix products, arithmetic and copies ran while one was open for 5% of the time, Pallas kernels for 6%

profile of v2, /device:TPU:1, one launch (start us, length us, event | category | flops | bytes accessed | tf_op | source)
XLA Modules:
  0.0 187.7 jit_solution(8142783528721217595)
XLA Ops:
  0.6 0.8 compare_select_fusion
  1.4 0.1 reshape.148
  1.5 1.8 gather_fusion
  3.4 4.0 %collective-permute-start = (bf16[1,4,128,128]{3,2,1,0:T(8,128)(2,1)S(1)}, bf16[1,4,128,128]{3,2,1,0:T(8,128)(2,1)S(1)}, u32[]{:S(2)}, u32[]{:S(2)}) collective-permute-start(bf16[1,4,128,128]{3,2,1,0:T(8,128)(2,1)S(1)} %get-tuple-element.15), channel_id=1, source_target_pairs={{0,32},{32,64},{64,96},{96,128},{128,160},{160,192},{192,224},{224... | collective-permute-start | bytes 393224 | tf_op jit(solution)/shard_map/ppermute | solution.py:25
  7.4 1.3 collective-permute-start.1
  8.7 0.1 reshape.156
  8.7 0.1 reshape.164
  8.8 1.8 gather_fusion.1
  10.7 0.0 copy-start.2
  10.7 4.2 %collective-permute-start.2 = (bf16[1,4,128,128]{3,2,1,0:T(8,128)(2,1)S(1)}, bf16[1,4,128,128]{3,2,1,0:T(8,128)(2,1)S(1)}, u32[]{:S(2)}, u32[]{:S(2)}) collective-permute-start(bf16[1,4,128,128]{3,2,1,0:T(8,128)(2,1)S(1)} %get-tuple-element.13), channel_id=1, source_target_pairs={{0,4},{4,8},{8,12},{12,16},{16,20},{20,24},{24,28},{1,5},{5,9},{9,... | collective-permute-start | bytes 393224 | tf_op jit(solution)/shard_map/ppermute | solution.py:25
  14.9 3.4 %collective-permute-start.3 = (bf16[1,4,128,128]{3,2,1,0:T(8,128)(2,1)S(1)}, bf16[1,4,128,128]{3,2,1,0:T(8,128)(2,1)S(1)}, u32[]{:S(2)}, u32[]{:S(2)}) collective-permute-start(bf16[1,4,128,128]{3,2,1,0:T(8,128)(2,1)S(1)} %get-tuple-element.12), channel_id=1, source_target_pairs={{4,0},{8,4},{12,8},{16,12},{20,16},{24,20},{28,24},{5,1},{9,5},{13... | collective-permute-start | bytes 393224 | tf_op jit(solution)/shard_map/ppermute | solution.py:26
  18.3 1.8 gather_fusion.2
  20.1 2.1 %collective-permute-start.4 = (bf16[1,4,128,128]{3,2,1,0:T(8,128)(2,1)S(1)}, bf16[1,4,128,128]{3,2,1,0:T(8,128)(2,1)S(1)}, u32[]{:S(2)}, u32[]{:S(2)}) collective-permute-start(bf16[1,4,128,128]{3,2,1,0:T(8,128)(2,1)S(1)} %get-tuple-element.11), channel_id=1, source_target_pairs={{0,1},{1,2},{2,3},{4,5},{5,6},{6,7},{8,9},{9,10},{10,11},{12,13},{... | collective-permute-start | bytes 393224 | tf_op jit(solution)/shard_map/ppermute | solution.py:25
  22.2 0.0 copy-start.3
  22.2 0.0 copy-start.4
  22.3 1.3 copy.27
  23.6 1.6 copy.28
  25.2 0.1 copy.29
  25.4 0.8 reshape_squeeze.15.pairs_ref
  26.8 0.1 copy.26
  26.9 0.6 reshape_squeeze.12.pairs_ref
  28.2 11.5 %inner_pairs.1 = (f32[32,128,128]{2,1,0:T(8,128)}, f32[27,128,128]{2,1,0:T(8,128)}) custom-call(s32[864]{0:T(1024)} %reshape_squeeze.15.pairs_ref, s32[1]{0:T(128)} %bitcast.20.live_ref, bf16[32,128,128]{2,1,0:T(8,128)(2,1)} %bitcast.61, bf16[32,128,128]{2,1,0:T(8,128)(2,1)} %bitcast.50, bf16[27,128,128]{2,1,0:T(8,128)(2,1)} %bitcast.53), custom_call_target="tpu_custom_call" | custom-call | flops 2415919104 | bytes 8388608 | tf_op jit(solution)/shard_map/inner_pairs/pallas_call | solution.py:96
  39.6 0.0 collective-permute-done
  39.6 1.3 collective-permute-start.5
  41.0 0.0 collective-permute-done.1
  41.0 0.0 collective-permute-done.2
  41.0 0.0 collective-permute-done.3
  41.1 0.0 collective-permute-done.4
  41.1 12.0 %collective-permute-done.5 = bf16[1,4,128,128]{3,2,1,0:T(8,128)(2,1)S(1)} collective-permute-done((bf16[1,4,128,128]{3,2,1,0:T(8,128)(2,1)S(1)}, bf16[1,4,128,128]{3,2,1,0:T(8,128)(2,1)S(1)}, u32[]{:S(2)}, u32[]{:S(2)}) %collective-permute-start.5) | collective-permute-done | bytes 131104 | tf_op jit(solution)/shard_map/ppermute | solution.py:26
  53.1 0.9 copy-done
  54.0 6.9 %outer_pairs.1 = (bf16[32,128,128]{2,1,0:T(8,128)(2,1)}, f32[27,128,128]{2,1,0:T(8,128)}) custom-call(s32[96]{0:T(128)} %reshape_squeeze.12.pairs_ref, s32[1]{0:T(128)} %bitcast.live_ref, bf16[24,128,128]{2,1,0:T(8,128)(2,1)} %copy-done, bf16[32,128,128]{2,1,0:T(8,128)(2,1)} %bitcast.51, bf16[27,128,128]{2,1,0:T(8,128)(2,1)} %bitcast.54, ...), custom_call_target="tpu_custom_call" | custom-call | flops 268435456 | bytes 8388608 | tf_op jit(solution)/shard_map/outer_pairs/pallas_call | solution.py:113
  60.9 27.6 %all_to_all.33 = f32[8,1,55296]{2,1,0:T(1,128)S(1)} all-to-all(f32[8,1,55296]{2,1,0:T(1,128)} %bitcast.55), channel_id=1, replica_groups=mesh['gx'=16,'gy'=8,'gz'=4] {'gy'}, dimensions={0} | all-to-all | bytes 3538944 | tf_op jit(solution)/shard_map/all_to_all | solution.py:133
  88.5 1.3 reduce_sum.27
  89.8 10.6 %all_to_all.34 = f32[4,1,13824]{2,1,0:T(1,128)S(1)} all-to-all(f32[4,1,13824]{2,1,0:T(1,128)S(1)} %bitcast.57), channel_id=1, replica_groups=mesh['gx'=16,'gy'=8,'gz'=4] {'gz'}, dimensions={0} | all-to-all | bytes 442368 | tf_op jit(solution)/shard_map/all_to_all | solution.py:133
  100.4 0.2 reduce_sum.28
  100.6 0.1 all_to_all.26
  100.8 34.0 %all_to_all.35 = f32[16,1,864]{2,1,0:T(1,128)S(1)} all-to-all(f32[16,1,864]{2,1,0:T(1,128)S(1)} %all_to_all.26), channel_id=1, replica_groups=mesh['gx'=16,'gy'=8,'gz'=4] {'gx'}, dimensions={0} | all-to-all | bytes 110592 | tf_op jit(solution)/shard_map/all_to_all | solution.py:133
  134.8 0.5 broadcast.78
  135.4 0.8 reduce.5
  136.2 0.1 reshape.184
  136.3 16.7 %all_to_all.36 = bf16[16,2,432]{2,1,0:T(2,128)(2,1)S(1)} all-to-all(bf16[16,2,432]{2,1,0:T(2,128)(2,1)S(1)} %reshape.184), channel_id=1, replica_groups=mesh['gx'=16,'gy'=8,'gz'=4] {'gx'}, dimensions={0} | all-to-all | bytes 55296 | tf_op jit(solution)/shard_map/all_to_all | solution.py:138
  153.0 0.1 reshape.185
  153.1 0.2 reduce.3
  153.2 0.1 reshape.179
  153.3 11.2 %all-gather = bf16[4,1,13824]{2,1,0:T(2,128)(2,1)S(1)} all-gather(bf16[1,1,13824]{2,1,0:T(2,128)(2,1)S(1)} %reshape.179), channel_id=1, replica_groups=mesh['gx'=16,'gy'=8,'gz'=4] {'gz'}, dimensions={0}, use_global_device_ids=true | all-gather | bytes 138240 | tf_op jit(solution)/shard_map/all_gather | solution.py:139
  164.6 0.7 reduce.4
  165.3 21.5 %all_gather.7 = bf16[442368]{0:T(1024)(128)(2,1)S(1)} all-gather(bf16[55296]{0:T(1024)(128)(2,1)S(1)} %reshape.180), channel_id=1, replica_groups=mesh['gx'=16,'gy'=8,'gz'=4] {'gy'}, dimensions={0}, use_global_device_ids=true | all-gather | bytes 995328 | tf_op jit(solution)/shard_map/all_gather | solution.py:140
  186.8 0.9 copy.43
  (21 shorter events, 0.3 us)
Async XLA Ops:
  0.6 21.6 %copy-start.1 = (bf16[1,1,1,4096,128]{4,3,2,1,0:T(8,128)(2,1)S(1)}, bf16[1,1,1,4096,128]{4,3,2,1,0:T(8,128)(2,1)}, u32[]{:S(2)}) copy-start(bf16[1,1,1,4096,128]{4,3,2,1,0:T(8,128)(2,1)} %param.8) | copy-start | bytes 3145732
  3.4 36.3 %collective-permute-start = (bf16[1,4,128,128]{3,2,1,0:T(8,128)(2,1)S(1)}, bf16[1,4,128,128]{3,2,1,0:T(8,128)(2,1)S(1)}, u32[]{:S(2)}, u32[]{:S(2)}) collective-permute-start(bf16[1,4,128,128]{3,2,1,0:T(8,128)(2,1)S(1)} %get-tuple-element.15), channel_id=1, source_target_pairs={{0,32},{32,64},{64,96},{96,128},{128,160},{160,192},{192,224},{224... | collective-permute-start | bytes 393224 | tf_op jit(solution)/shard_map/ppermute | solution.py:25
  7.4 33.6 %collective-permute-start.1 = (bf16[1,4,128,128]{3,2,1,0:T(8,128)(2,1)S(1)}, bf16[1,4,128,128]{3,2,1,0:T(8,128)(2,1)S(1)}, u32[]{:S(2)}, u32[]{:S(2)}) collective-permute-start(bf16[1,4,128,128]{3,2,1,0:T(8,128)(2,1)S(1)} %get-tuple-element.14), channel_id=1, source_target_pairs={{32,0},{64,32},{96,64},{128,96},{160,128},{192,160},{224,192},{256... | collective-permute-start | bytes 393224 | tf_op jit(solution)/shard_map/ppermute | solution.py:26
  10.7 12.9 %copy-start.2 = (bf16[27,128,128]{2,1,0:T(8,128)(2,1)S(1)}, bf16[27,128,128]{2,1,0:T(8,128)(2,1)}, u32[]{:S(2)}) copy-start(bf16[27,128,128]{2,1,0:T(8,128)(2,1)} %param.10) | copy-start | bytes 2654212
  10.7 30.3 %collective-permute-start.2 = (bf16[1,4,128,128]{3,2,1,0:T(8,128)(2,1)S(1)}, bf16[1,4,128,128]{3,2,1,0:T(8,128)(2,1)S(1)}, u32[]{:S(2)}, u32[]{:S(2)}) collective-permute-start(bf16[1,4,128,128]{3,2,1,0:T(8,128)(2,1)S(1)} %get-tuple-element.13), channel_id=1, source_target_pairs={{0,4},{4,8},{8,12},{12,16},{16,20},{20,24},{24,28},{1,5},{5,9},{9,... | collective-permute-start | bytes 393224 | tf_op jit(solution)/shard_map/ppermute | solution.py:25
  14.9 26.2 %collective-permute-start.3 = (bf16[1,4,128,128]{3,2,1,0:T(8,128)(2,1)S(1)}, bf16[1,4,128,128]{3,2,1,0:T(8,128)(2,1)S(1)}, u32[]{:S(2)}, u32[]{:S(2)}) collective-permute-start(bf16[1,4,128,128]{3,2,1,0:T(8,128)(2,1)S(1)} %get-tuple-element.12), channel_id=1, source_target_pairs={{4,0},{8,4},{12,8},{16,12},{20,16},{24,20},{28,24},{5,1},{9,5},{13... | collective-permute-start | bytes 393224 | tf_op jit(solution)/shard_map/ppermute | solution.py:26
  20.1 20.9 %collective-permute-start.4 = (bf16[1,4,128,128]{3,2,1,0:T(8,128)(2,1)S(1)}, bf16[1,4,128,128]{3,2,1,0:T(8,128)(2,1)S(1)}, u32[]{:S(2)}, u32[]{:S(2)}) collective-permute-start(bf16[1,4,128,128]{3,2,1,0:T(8,128)(2,1)S(1)} %get-tuple-element.11), channel_id=1, source_target_pairs={{0,1},{1,2},{2,3},{4,5},{5,6},{6,7},{8,9},{9,10},{10,11},{12,13},{... | collective-permute-start | bytes 393224 | tf_op jit(solution)/shard_map/ppermute | solution.py:25
  22.2 3.0 %copy-start.3 = (s32[1,1,1,288,3]{3,2,4,1,0:T(1,128)S(1)}, s32[1,1,1,288,3]{3,2,4,1,0:T(1,128)}, u32[]{:S(2)}) copy-start(s32[1,1,1,288,3]{3,2,4,1,0:T(1,128)} %param.11) | copy-start | bytes 10372
  22.2 4.6 %copy-start.4 = (s32[1,1,1,32,3]{3,2,4,1,0:T(1,128)S(1)}, s32[1,1,1,32,3]{3,2,4,1,0:T(1,128)}, u32[]{:S(2)}) copy-start(s32[1,1,1,32,3]{3,2,4,1,0:T(1,128)} %param.12) | copy-start | bytes 1156
  39.6 13.4 %collective-permute-start.5 = (bf16[1,4,128,128]{3,2,1,0:T(8,128)(2,1)S(1)}, bf16[1,4,128,128]{3,2,1,0:T(8,128)(2,1)S(1)}, u32[]{:S(2)}, u32[]{:S(2)}) collective-permute-start(bf16[1,4,128,128]{3,2,1,0:T(8,128)(2,1)S(1)} %get-tuple-element.10), channel_id=1, source_target_pairs={{1,0},{2,1},{3,2},{5,4},{6,5},{7,6},{9,8},{10,9},{11,10},{13,12},{... | collective-permute-start | bytes 393224 | tf_op jit(solution)/shard_map/ppermute | solution.py:26
  53.1 0.9 copy-start

commit v3 on v2

v3 whole, which is shorter than its diff:
```python
import math

import jax
import jax.numpy as jnp
from jax import lax
from jax.experimental import pallas as pl
from jax.experimental.pallas import tpu as pltpu
from jax.sharding import PartitionSpec as P

C = 128
BLOCK = 128
NB = 32
PI = 288
PB = 32
UNROLL = 4


def extended(shard, sides, width):
    for axis, dim in sides:
        count, length = (lax.axis_size(axis), shard.shape[dim])
        up = [(i, (i + 1) % count) for i in range(count - 1)]
        down = [(j, i) for i, j in up]
        last = lax.slice_in_dim(shard, length - width, length, axis=dim)
        initial = lax.slice_in_dim(shard, 0, width, axis=dim)
        before = lax.ppermute(last, axis, up)
        after = lax.ppermute(initial, axis, down)
        shard = jnp.concatenate([before, shard, after], axis=dim)
    return shard


def received_blocks(local_grads, face_lists):
    got_x = extended(local_grads[face_lists[0]], (("gx", 0),), 1)
    got_y = extended(local_grads[face_lists[1]], (("gy", 0),), 1)
    got_z = extended(local_grads[face_lists[2]], (("gz", 0),), 1)
    return jnp.concatenate(
        [got_x[0], got_x[3], got_y[0], got_y[3], got_z[0], got_z[3]], axis=0
    )


def pair_loop(pairs_ref, live_ref, table_ref, table_base, update):
    def pair_ids(i):
        return (pairs_ref[3 * i], pairs_ref[3 * i + 1] - table_base, pairs_ref[3 * i + 2])

    def one_group(group, carry):
        ids = [pair_ids(group * UNROLL + j) for j in range(UNROLL)]
        grads = [table_ref[a] for _, a, _ in ids]
        update(ids, grads)
        return carry

    def one_pair(i, carry):
        k, a, b = pair_ids(i)
        update([(k, a, b)], [table_ref[a]])
        return carry

    live = live_ref[0]
    groups = live // UNROLL
    lax.fori_loop(0, groups, one_group, 0)
    lax.fori_loop(groups * UNROLL, live, one_pair, 0)


def weight_updater(ft_ref, acc_w):
    def update(ids, grads):
        terms = [
            jnp.dot(ft_ref[b], g, preferred_element_type=jnp.float32)
            for g, (_, _, b) in zip(grads, ids)
        ]
        for (k, _, _), term in zip(ids, terms):
            acc_w[k] += term

    return update


def input_updater(kt_ref, acc_in):
    def update(ids, grads):
        terms = [
            jnp.dot(g, kt_ref[k], preferred_element_type=jnp.float32)
            for g, (k, _, _) in zip(grads, ids)
        ]
        for (_, _, b), term in zip(ids, terms):
            acc_in[b] += term

    return update


def inner_weight_kernel(pairs_ref, live_ref, table_ref, ft_ref, acc_w):
    acc_w[...] = jnp.zeros_like(acc_w)
    pair_loop(pairs_ref, live_ref, table_ref, 0, weight_updater(ft_ref, acc_w))


def outer_weight_kernel(pairs_ref, live_ref, table_ref, ft_ref, w_start, acc_w):
    acc_w[...] = w_start[...]
    pair_loop(pairs_ref, live_ref, table_ref, NB, weight_updater(ft_ref, acc_w))


def input_kernel(inner_ref, inner_live_ref, outer_ref, outer_live_ref, local_ref, received_ref, kt_ref, after_ref, grad_out, acc_in):
    acc_in[...] = jnp.zeros_like(acc_in)
    update = input_updater(kt_ref, acc_in)
    pair_loop(inner_ref, inner_live_ref, local_ref, 0, update)
    pair_loop(outer_ref, outer_live_ref, received_ref, NB, update)
    grad_out[...] = acc_in[...].astype(grad_out.dtype)


def vmem():
    return pl.BlockSpec(memory_space=pltpu.MemorySpace.VMEM)


def smem():
    return pl.BlockSpec(memory_space=pltpu.MemorySpace.SMEM)


def cost(pairs):
    return pl.CostEstimate(
        flops=2 * pairs * BLOCK * C * C, transcendentals=0, bytes_accessed=6 * 1024 * 1024
    )


def run_inner_weights(pairs, live, table, ft):
    return pl.pallas_call(
        inner_weight_kernel,
        out_shape=jax.ShapeDtypeStruct((27, C, C), jnp.float32),
        in_specs=[smem(), smem(), vmem(), vmem()],
        out_specs=vmem(),
        cost_estimate=cost(PI),
        name="inner_weight_pairs",
    )(pairs, live, table, ft)


def run_outer_weights(pairs, live, table, ft, acc_w):
    return pl.pallas_call(
        outer_weight_kernel,
        out_shape=jax.ShapeDtypeStruct((27, C, C), jnp.float32),
        in_specs=[smem(), smem(), vmem(), vmem(), vmem()],
        out_specs=vmem(),
        input_output_aliases={4: 0},
        cost_estimate=cost(PB),
        name="outer_weight_pairs",
    )(pairs, live, table, ft, acc_w)


def run_inputs(inner_pairs, inner_n, outer_pairs, outer_n, local, received, kt, after):
    return pl.pallas_call(
        input_kernel,
        out_shape=jax.ShapeDtypeStruct((NB, BLOCK, C), jnp.bfloat16),
        in_specs=[smem(), smem(), smem(), smem(), vmem(), vmem(), vmem(), vmem()],
        out_specs=vmem(),
        scratch_shapes=[pltpu.VMEM((NB, BLOCK, C), jnp.float32)],
        cost_estimate=cost(PI + PB),
        name="input_pairs",
    )(inner_pairs, inner_n, outer_pairs, outer_n, local, received, kt, after)


def reduce_weights(weight_acc, grad_scale):
    flat = weight_acc.reshape(-1)
    for axis in ("gy", "gz", "gx"):
        n = lax.axis_size(axis)
        parts = lax.all_to_all(flat.reshape(n, -1), axis, 0, 0, tiled=True)
        flat = parts.reshape(n, -1).sum(axis=0)
    after = flat
    piece = (flat * grad_scale).astype(jnp.bfloat16)
    n = lax.axis_size("gx")
    copies = jnp.broadcast_to(piece[None], (n,) + piece.shape)
    piece = lax.all_to_all(copies, "gx", 0, 0, tiled=True).reshape(-1)
    piece = lax.all_gather(piece, "gz", tiled=True)
    piece = lax.all_gather(piece, "gy", tiled=True)
    return piece.reshape(weight_acc.shape), after


def body(features, output_grad, kernel, inner_map, outer_map, face_blocks, inner_live, outer_live):
    local_grads = output_grad[0, 0, 0].reshape(NB, BLOCK, C)
    feats_t = jnp.swapaxes(features[0, 0, 0].reshape(NB, BLOCK, C), 1, 2)
    kernel_t = jnp.swapaxes(kernel, 1, 2)
    inner_pairs = inner_map[0, 0, 0].reshape(-1)
    outer_pairs = outer_map[0, 0, 0].reshape(-1)
    inner_n = jnp.clip(inner_live[0, 0, 0], 0, PI).reshape(1)
    outer_n = jnp.clip(outer_live[0, 0, 0], 0, PB).reshape(1)
    received = received_blocks(local_grads, face_blocks[0, 0, 0])
    acc_w = run_inner_weights(inner_pairs, inner_n, local_grads, feats_t)
    acc_w = run_outer_weights(outer_pairs, outer_n, received, feats_t, acc_w)
    bricks_all = lax.axis_size("gx") * lax.axis_size("gy") * lax.axis_size("gz")
    grad_scale = math.sqrt(27.0 / (bricks_all * PI * BLOCK))
    weight_grad, after = reduce_weights(acc_w, grad_scale)
    input_grad = run_inputs(
        inner_pairs, inner_n, outer_pairs, outer_n, local_grads, received, kernel_t, after
    )
    return (input_grad.reshape(1, 1, 1, NB * BLOCK, C), weight_grad)


def solution(mesh):
    in_specs = (
        P("gx", "gy", "gz", None, None),
        P("gx", "gy", "gz", None, None),
        P(),
        P("gx", "gy", "gz", None, None),
        P("gx", "gy", "gz", None, None),
        P("gx", "gy", "gz", None, None, None),
        P("gx", "gy", "gz"),
        P("gx", "gy", "gz"),
    )
    out_specs = (P("gx", "gy", "gz", None, None), P())
    return jax.shard_map(body, mesh=mesh, in_specs=in_specs, out_specs=out_specs, check_vma=False)
```

time: 188 us -> 184 us (0.979)
  blocking collectives: 122 us -> 65 us
  starting transfers between devices: 16.2 us -> 41.8 us
  Pallas kernels: 18.3 us -> 38.9 us
  waiting for transfers between devices: 12 us -> 16.5 us
    all_to_all x3 -> x2, blocking collectives: 72.3 us -> 35.7 us  [reduce_weights(): parts = lax.all_to_all(flat.reshape(n, -1), axis, 0, 0, tiled=True)]
    all_to_all x0 -> x2, starting transfers between devices: none -> 25.8 us  [the longest x1 22.3 us: reduce_weights(): parts = lax.all_to_all(flat.reshape(n, -1), axis, 0, 0, tiled=True)]
    pallas_call x2 -> x3, Pallas kernels: 18.3 us -> 38.9 us  [the longest x1 17.7 us: run_inputs(): pl.pallas_call(input_kernel, out_shape=jax.ShapeDtypeStruct((NB, BLOCK, C...]
    all_to_all x1 -> x0, blocking collectives: 16.7 us -> none  [reduce_weights(): piece = lax.all_to_all(copies, 'gx', 0, 0, tiled=True).reshape(-1)]
    all_to_all x0 -> x2, waiting for transfers between devices: none -> 12.3 us  [the longest x1 12.3 us: reduce_weights(): parts = lax.all_to_all(flat.reshape(n, -1), axis, 0, 0, tiled=True)]
    ppermute x3, waiting for transfers between devices: 12 us -> 4.25 us  [extended(): after = lax.ppermute(initial, axis, down)]
    all_gather x1, blocking collectives: 21.5 us -> 18.2 us  [reduce_weights(): piece = lax.all_gather(piece, 'gy', tiled=True)]
    unnamed x23 -> x25, local copies, waits for them, and re-layouts: 4.13 us -> 4.74 us
  transfers between devices with their start and end apart: 6 -> 8, of which waited for: 1 -> 2; matrix products, arithmetic and copies ran while one was open for 5% -> 5% of each run, Pallas kernels for 6% -> 19%
where the time goes in v3:
time: 184 us; the launch traced here: 183 us
  blocking collectives  65 us (35%)
  starting transfers between devices  41.8 us (23%)
  Pallas kernels  38.9 us (21%)
  waiting for transfers between devices  16.5 us (9%)
  local copies, waits for them, and re-layouts  14.5 us (8%)
  other arithmetic  3.99 us (2%)
  between operations  2.27 us (1%)
    all_to_all x2, blocking collectives, reduce_weights(): parts = lax.all_to_all(flat.reshape(n, -1), axis, 0, 0, tiled=True)  35.7 us
    all_to_all x1, starting transfers between devices, reduce_weights(): parts = lax.all_to_all(flat.reshape(n, -1), axis, 0, 0, tiled=True)  22.3 us
    all_gather x1, blocking collectives, reduce_weights(): piece = lax.all_gather(piece, 'gy', tiled=True)  18.2 us
    pallas_call x1, Pallas kernels, run_inputs(): pl.pallas_call(input_kernel, out_shape=jax.ShapeDtypeStruct((NB, BLOCK, C...  17.7 us
    pallas_call x1, Pallas kernels, run_inner_weights(): pl.pallas_call(inner_weight_kernel, out_shape=jax.ShapeDtypeStruct((27, C...  16.2 us
    all_to_all x1, waiting for transfers between devices, reduce_weights(): parts = lax.all_to_all(flat.reshape(n, -1), axis, 0, 0, tiled=True)  12.3 us
    all_gather x1, blocking collectives, reduce_weights(): piece = lax.all_gather(piece, 'gz', tiled=True)  11 us
    ppermute x3, starting transfers between devices, extended(): before = lax.ppermute(last, axis, up)  10.1 us
  transfers between devices with their start and end apart: 8, of which 2 were waited for; matrix products, arithmetic and copies ran while one was open for 5% of the time, Pallas kernels for 19%

profile of v3, /device:TPU:1, one launch (start us, length us, event | category | flops | bytes accessed | tf_op | source)
XLA Modules:
  0.0 183.0 jit_solution(5783268758752151509)
XLA Ops:
  0.6 0.8 compare_select_fusion
  1.4 0.1 reshape.148
  1.5 1.8 gather_fusion
  3.4 4.0 %collective-permute-start = (bf16[1,4,128,128]{3,2,1,0:T(8,128)(2,1)S(1)}, bf16[1,4,128,128]{3,2,1,0:T(8,128)(2,1)S(1)}, u32[]{:S(2)}, u32[]{:S(2)}) collective-permute-start(bf16[1,4,128,128]{3,2,1,0:T(8,128)(2,1)S(1)} %get-tuple-element.7), channel_id=1, source_target_pairs={{0,32},{32,64},{64,96},{96,128},{128,160},{160,192},{192,224},{224... | collective-permute-start | bytes 393224 | tf_op jit(solution)/shard_map/ppermute | solution.py:25
  7.4 1.3 collective-permute-start.1
  8.7 0.1 reshape.156
  8.7 0.1 reshape.164
  8.8 1.8 gather_fusion.1
  10.7 0.0 copy-start.4
  10.7 0.0 copy-start.5
  10.7 4.0 %collective-permute-start.2 = (bf16[1,4,128,128]{3,2,1,0:T(8,128)(2,1)S(1)}, bf16[1,4,128,128]{3,2,1,0:T(8,128)(2,1)S(1)}, u32[]{:S(2)}, u32[]{:S(2)}) collective-permute-start(bf16[1,4,128,128]{3,2,1,0:T(8,128)(2,1)S(1)} %get-tuple-element.5), channel_id=1, source_target_pairs={{0,4},{4,8},{8,12},{12,16},{16,20},{20,24},{24,28},{1,5},{5,9},{9,... | collective-permute-start | bytes 393224 | tf_op jit(solution)/shard_map/ppermute | solution.py:25
  14.8 3.4 %collective-permute-start.3 = (bf16[1,4,128,128]{3,2,1,0:T(8,128)(2,1)S(1)}, bf16[1,4,128,128]{3,2,1,0:T(8,128)(2,1)S(1)}, u32[]{:S(2)}, u32[]{:S(2)}) collective-permute-start(bf16[1,4,128,128]{3,2,1,0:T(8,128)(2,1)S(1)} %get-tuple-element.4), channel_id=1, source_target_pairs={{4,0},{8,4},{12,8},{16,12},{20,16},{24,20},{28,24},{5,1},{9,5},{13... | collective-permute-start | bytes 393224 | tf_op jit(solution)/shard_map/ppermute | solution.py:26
  18.1 1.8 gather_fusion.2
  20.0 2.1 %collective-permute-start.4 = (bf16[1,4,128,128]{3,2,1,0:T(8,128)(2,1)S(1)}, bf16[1,4,128,128]{3,2,1,0:T(8,128)(2,1)S(1)}, u32[]{:S(2)}, u32[]{:S(2)}) collective-permute-start(bf16[1,4,128,128]{3,2,1,0:T(8,128)(2,1)S(1)} %get-tuple-element.3), channel_id=1, source_target_pairs={{0,1},{1,2},{2,3},{4,5},{5,6},{6,7},{8,9},{9,10},{10,11},{12,13},{... | collective-permute-start | bytes 393224 | tf_op jit(solution)/shard_map/ppermute | solution.py:25
  22.1 1.3 copy.30
  23.4 0.1 copy.27
  23.6 0.8 reshape_squeeze.12.pairs_ref.inner_ref
  25.0 0.1 copy.28
  25.1 0.6 reshape_squeeze.13.pairs_ref.outer_ref
  26.4 16.2 %inner_weight_pairs.1.w_start = f32[27,128,128]{2,1,0:T(8,128)} custom-call(s32[864]{0:T(1024)} %reshape_squeeze.12.pairs_ref.inner_ref, s32[1]{0:T(128)} %bitcast.live_ref.inner_live_ref, bf16[32,128,128]{2,1,0:T(8,128)(2,1)} %bitcast.60, bf16[32,128,128]{2,1,0:T(8,128)(2,1)} %bitcast.51), custom_call_target="tpu_custom_call" | custom-call | flops 1207959552 | bytes 6291456 | tf_op jit(solution)/shard_map/inner_weight_pairs/pallas_call | solution.py:118
  42.6 1.3 collective-permute-start.5
  43.9 0.0 collective-permute-done.1
  43.9 0.0 collective-permute-done.3
  44.0 0.0 collective-permute-done.4
  44.0 4.2 %collective-permute-done.5 = bf16[1,4,128,128]{3,2,1,0:T(8,128)(2,1)S(1)} collective-permute-done((bf16[1,4,128,128]{3,2,1,0:T(8,128)(2,1)S(1)}, bf16[1,4,128,128]{3,2,1,0:T(8,128)(2,1)S(1)}, u32[]{:S(2)}, u32[]{:S(2)}) %collective-permute-start.5) | collective-permute-done | bytes 131104 | tf_op jit(solution)/shard_map/ppermute | solution.py:26
  48.3 0.9 copy-done
  49.2 5.0 %outer_weight_pairs.1 = f32[27,128,128]{2,1,0:T(8,128)} custom-call(s32[96]{0:T(128)} %reshape_squeeze.13.pairs_ref.outer_ref, s32[1]{0:T(128)} %bitcast.1.live_ref.outer_live_ref, bf16[24,128,128]{2,1,0:T(8,128)(2,1)} %copy-done, bf16[32,128,128]{2,1,0:T(8,128)(2,1)} %bitcast.52, ...), custom_call_target="tpu_custom_call", output_to_operand_aliasing={{}: (4, {})} | custom-call | flops 134217728 | bytes 6291456 | tf_op jit(solution)/shard_map/outer_weight_pairs/pallas_call | solution.py:129
  54.1 26.5 %all_to_all.33 = f32[8,1,55296]{2,1,0:T(1,128)S(1)} all-to-all(f32[8,1,55296]{2,1,0:T(1,128)} %bitcast.50), channel_id=1, replica_groups=mesh['gx'=16,'gy'=8,'gz'=4] {'gy'}, dimensions={0} | all-to-all | bytes 3538944 | tf_op jit(solution)/shard_map/all_to_all | solution.py:156
  80.6 1.3 reduce_sum.27
  81.9 9.2 %all_to_all.34 = f32[4,1,13824]{2,1,0:T(1,128)S(1)} all-to-all(f32[4,1,13824]{2,1,0:T(1,128)S(1)} %bitcast.55), channel_id=1, replica_groups=mesh['gx'=16,'gy'=8,'gz'=4] {'gz'}, dimensions={0} | all-to-all | bytes 442368 | tf_op jit(solution)/shard_map/all_to_all | solution.py:156
  91.1 0.2 reduce_sum.28
  91.3 0.7 all_to_all.26
  92.1 22.3 %all-to-all-start.2 = ((f32[16,1,864]{2,1,0:T(1,128)}), f32[16,1,864]{2,1,0:T(1,128)S(1)}, u32[]{:S(2)}, u32[]{:S(2)}) async-start(f32[16,1,864]{2,1,0:T(1,128)} %all_to_all.26), calls=%async_computation.2 | async-start | bytes 114688 | tf_op jit(solution)/shard_map/all_to_all | solution.py:156
  114.4 1.6 copy.29
  116.1 12.3 %all-to-all-done.2 = f32[16,1,864]{2,1,0:T(1,128)S(1)} async-done(((f32[16,1,864]{2,1,0:T(1,128)}), f32[16,1,864]{2,1,0:T(1,128)S(1)}, u32[]{:S(2)}, u32[]{:S(2)}) %all-to-all-start.2) | async-done | bytes 55328 | tf_op jit(solution)/shard_map/all_to_all | solution.py:156
  128.4 0.5 broadcast.78
  128.9 0.8 reduce.5
  129.8 0.7 reshape.184
  130.5 3.5 %all-to-all-start.3 = ((bf16[16,2,432]{2,1,0:T(2,128)(2,1)}), bf16[16,2,432]{2,1,0:T(2,128)(2,1)S(1)}, u32[]{:S(2)}, u32[]{:S(2)}) async-start(bf16[16,2,432]{2,1,0:T(2,128)(2,1)} %reshape.184), calls=%async_computation.3 | async-start | bytes 65536 | tf_op jit(solution)/shard_map/all_to_all | solution.py:162
  134.0 17.7 %input_pairs.1 = bf16[32,128,128]{2,1,0:T(8,128)(2,1)} custom-call(s32[864]{0:T(1024)} %reshape_squeeze.12.pairs_ref.inner_ref, s32[1]{0:T(128)} %bitcast.live_ref.inner_live_ref, s32[96]{0:T(128)} %reshape_squeeze.13.pairs_ref.outer_ref, s32[1]{0:T(128)} %bitcast.1.live_ref.outer_live_ref, bf16[32,128,128]{2,1,0:T(8,128)(2,1)} %bitcast.61, ...), custom_call_target="tpu_custom_call" | custom-call | flops 1342177280 | bytes 6291456 | tf_op jit(solution)/shard_map/input_pairs/pallas_call | solution.py:141
  151.7 0.0 all-to-all-done.3
  151.7 0.1 reshape.185
  151.8 0.2 reduce.3
  152.0 0.1 reshape.179
  152.1 11.0 %all-gather = bf16[4,1,13824]{2,1,0:T(2,128)(2,1)S(1)} all-gather(bf16[1,1,13824]{2,1,0:T(2,128)(2,1)S(1)} %reshape.179), channel_id=1, replica_groups=mesh['gx'=16,'gy'=8,'gz'=4] {'gz'}, dimensions={0}, use_global_device_ids=true | all-gather | bytes 138240 | tf_op jit(solution)/shard_map/all_gather | solution.py:163
  163.1 0.7 reduce.4
  163.9 18.2 %all_gather.7 = bf16[442368]{0:T(1024)(128)(2,1)S(1)} all-gather(bf16[55296]{0:T(1024)(128)(2,1)S(1)} %reshape.180), channel_id=1, replica_groups=mesh['gx'=16,'gy'=8,'gz'=4] {'gy'}, dimensions={0}, use_global_device_ids=true | all-gather | bytes 995328 | tf_op jit(solution)/shard_map/all_gather | solution.py:164
  182.1 0.9 copy.45
  (26 shorter events, 0.3 us)
Async XLA Ops:
  0.6 21.5 %copy-start.1 = (bf16[1,1,1,4096,128]{4,3,2,1,0:T(8,128)(2,1)S(1)}, bf16[1,1,1,4096,128]{4,3,2,1,0:T(8,128)(2,1)}, u32[]{:S(2)}) copy-start(bf16[1,1,1,4096,128]{4,3,2,1,0:T(8,128)(2,1)} %param.8) | copy-start | bytes 3145732
  3.4 39.2 %collective-permute-start = (bf16[1,4,128,128]{3,2,1,0:T(8,128)(2,1)S(1)}, bf16[1,4,128,128]{3,2,1,0:T(8,128)(2,1)S(1)}, u32[]{:S(2)}, u32[]{:S(2)}) collective-permute-start(bf16[1,4,128,128]{3,2,1,0:T(8,128)(2,1)S(1)} %get-tuple-element.7), channel_id=1, source_target_pairs={{0,32},{32,64},{64,96},{96,128},{128,160},{160,192},{192,224},{224... | collective-permute-start | bytes 393224 | tf_op jit(solution)/shard_map/ppermute | solution.py:25
  7.4 36.5 %collective-permute-start.1 = (bf16[1,4,128,128]{3,2,1,0:T(8,128)(2,1)S(1)}, bf16[1,4,128,128]{3,2,1,0:T(8,128)(2,1)S(1)}, u32[]{:S(2)}, u32[]{:S(2)}) collective-permute-start(bf16[1,4,128,128]{3,2,1,0:T(8,128)(2,1)S(1)} %get-tuple-element.6), channel_id=1, source_target_pairs={{32,0},{64,32},{96,64},{128,96},{160,128},{192,160},{224,192},{256... | collective-permute-start | bytes 393224 | tf_op jit(solution)/shard_map/ppermute | solution.py:26
  10.7 12.8 %copy-start.4 = (s32[1,1,1,288,3]{3,2,4,1,0:T(1,128)S(1)}, s32[1,1,1,288,3]{3,2,4,1,0:T(1,128)}, u32[]{:S(2)}) copy-start(s32[1,1,1,288,3]{3,2,4,1,0:T(1,128)} %param.11) | copy-start | bytes 10372
  10.7 14.3 %copy-start.5 = (s32[1,1,1,32,3]{3,2,4,1,0:T(1,128)S(1)}, s32[1,1,1,32,3]{3,2,4,1,0:T(1,128)}, u32[]{:S(2)}) copy-start(s32[1,1,1,32,3]{3,2,4,1,0:T(1,128)} %param.12) | copy-start | bytes 1156
  10.7 33.2 %collective-permute-start.2 = (bf16[1,4,128,128]{3,2,1,0:T(8,128)(2,1)S(1)}, bf16[1,4,128,128]{3,2,1,0:T(8,128)(2,1)S(1)}, u32[]{:S(2)}, u32[]{:S(2)}) collective-permute-start(bf16[1,4,128,128]{3,2,1,0:T(8,128)(2,1)S(1)} %get-tuple-element.5), channel_id=1, source_target_pairs={{0,4},{4,8},{8,12},{12,16},{16,20},{20,24},{24,28},{1,5},{5,9},{9,... | collective-permute-start | bytes 393224 | tf_op jit(solution)/shard_map/ppermute | solution.py:25
  14.8 29.2 %collective-permute-start.3 = (bf16[1,4,128,128]{3,2,1,0:T(8,128)(2,1)S(1)}, bf16[1,4,128,128]{3,2,1,0:T(8,128)(2,1)S(1)}, u32[]{:S(2)}, u32[]{:S(2)}) collective-permute-start(bf16[1,4,128,128]{3,2,1,0:T(8,128)(2,1)S(1)} %get-tuple-element.4), channel_id=1, source_target_pairs={{4,0},{8,4},{12,8},{16,12},{20,16},{24,20},{28,24},{5,1},{9,5},{13... | collective-permute-start | bytes 393224 | tf_op jit(solution)/shard_map/ppermute | solution.py:26
  20.0 24.0 %collective-permute-start.4 = (bf16[1,4,128,128]{3,2,1,0:T(8,128)(2,1)S(1)}, bf16[1,4,128,128]{3,2,1,0:T(8,128)(2,1)S(1)}, u32[]{:S(2)}, u32[]{:S(2)}) collective-permute-start(bf16[1,4,128,128]{3,2,1,0:T(8,128)(2,1)S(1)} %get-tuple-element.3), channel_id=1, source_target_pairs={{0,1},{1,2},{2,3},{4,5},{5,6},{6,7},{8,9},{9,10},{10,11},{12,13},{... | collective-permute-start | bytes 393224 | tf_op jit(solution)/shard_map/ppermute | solution.py:25
  42.6 5.7 %collective-permute-start.5 = (bf16[1,4,128,128]{3,2,1,0:T(8,128)(2,1)S(1)}, bf16[1,4,128,128]{3,2,1,0:T(8,128)(2,1)S(1)}, u32[]{:S(2)}, u32[]{:S(2)}) collective-permute-start(bf16[1,4,128,128]{3,2,1,0:T(8,128)(2,1)S(1)} %get-tuple-element.2), channel_id=1, source_target_pairs={{1,0},{2,1},{3,2},{5,4},{6,5},{7,6},{9,8},{10,9},{11,10},{13,12},{... | collective-permute-start | bytes 393224 | tf_op jit(solution)/shard_map/ppermute | solution.py:26
  48.3 0.9 copy-start
  80.6 33.8 %copy-start.2 = (bf16[27,128,128]{2,1,0:T(8,128)(2,1)S(1)}, bf16[27,128,128]{2,1,0:T(8,128)(2,1)}, u32[]{:S(2)}) copy-start(bf16[27,128,128]{2,1,0:T(8,128)(2,1)} %param.10) | copy-start | bytes 2654212
  92.1 36.2 %all-to-all-start.2 = ((f32[16,1,864]{2,1,0:T(1,128)}), f32[16,1,864]{2,1,0:T(1,128)S(1)}, u32[]{:S(2)}, u32[]{:S(2)}) async-start(f32[16,1,864]{2,1,0:T(1,128)} %all_to_all.26), calls=%async_computation.2 | async-start | bytes 114688 | tf_op jit(solution)/shard_map/all_to_all | solution.py:156
  128.4 5.6 %copy-start.3 = (f32[864]{0:T(1024)}, f32[864]{0:T(1024)S(1)}, u32[]{:S(2)}) copy-start(f32[864]{0:T(1024)S(1)} %reduce_sum.29.after_ref) | copy-start | bytes 10372
  130.5 21.2 %all-to-all-start.3 = ((bf16[16,2,432]{2,1,0:T(2,128)(2,1)}), bf16[16,2,432]{2,1,0:T(2,128)(2,1)S(1)}, u32[]{:S(2)}, u32[]{:S(2)}) async-start(bf16[16,2,432]{2,1,0:T(2,128)(2,1)} %reshape.184), calls=%async_computation.3 | async-start | bytes 65536 | tf_op jit(solution)/shard_map/all_to_all | solution.py:162

commit v4 on v3

--- a/solution.py
+++ b/solution.py
@@ -156,13 +156,12 @@
         parts = lax.all_to_all(flat.reshape(n, -1), axis, 0, 0, tiled=True)
         flat = parts.reshape(n, -1).sum(axis=0)
     after = flat
-    piece = (flat * grad_scale).astype(jnp.bfloat16)
+    piece = flat * grad_scale
     n = lax.axis_size("gx")
     copies = jnp.broadcast_to(piece[None], (n,) + piece.shape)
     piece = lax.all_to_all(copies, "gx", 0, 0, tiled=True).reshape(-1)
-    piece = lax.all_gather(piece, "gz", tiled=True)
-    piece = lax.all_gather(piece, "gy", tiled=True)
-    return piece.reshape(weight_acc.shape), after
+    piece = lax.optimization_barrier(lax.all_gather(piece, ("gy", "gz"), tiled=True))
+    return piece.astype(jnp.bfloat16).reshape(weight_acc.shape), after
 
 
 def body(features, output_grad, kernel, inner_map, outer_map, face_blocks, inner_live, outer_live):

time: 184 us -> 245 us (1.33)
  waiting for transfers between devices: 16.5 us -> 73.9 us
  blocking collectives: 65 us -> 92.8 us
  starting transfers between devices: 41.8 us -> 16.1 us
  between operations: 2.27 us -> 15.6 us
  Pallas kernels: 38.9 us -> 28.7 us
    all_gather x0 -> x1, waiting for transfers between devices: none -> 69.6 us  [reduce_weights(): lax.all_gather(piece, ('gy', 'gz'), tiled=True)]
    all_to_all x2 -> x3, blocking collectives: 35.7 us -> 76.3 us  [reduce_weights(): parts = lax.all_to_all(flat.reshape(n, -1), axis, 0, 0, tiled=True)]
    all_gather x2 -> x0, blocking collectives: 29.3 us -> none  [the longest x1 18.2 us: reduce_weights(): piece = lax.all_gather(piece, 'gy', tiled=True)]
    all_to_all x2 -> x0, starting transfers between devices: 25.8 us -> none  [the longest x1 22.3 us: reduce_weights(): parts = lax.all_to_all(flat.reshape(n, -1), axis, 0, 0, tiled=True)]
    all_to_all x0 -> x1, blocking collectives: none -> 16.5 us  [reduce_weights(): piece = lax.all_to_all(copies, 'gx', 0, 0, tiled=True).reshape(-1)]
    all_to_all x2 -> x0, waiting for transfers between devices: 12.3 us -> none  [the longest x1 12.3 us: reduce_weights(): parts = lax.all_to_all(flat.reshape(n, -1), axis, 0, 0, tiled=True)]
    pallas_call x1, Pallas kernels: 17.7 us -> 12.7 us  [run_inputs(): pl.pallas_call(input_kernel, out_shape=jax.ShapeDtypeStruct((NB, BLOCK, C...]
    pallas_call x1, Pallas kernels: 16.2 us -> 11.3 us  [run_inner_weights(): pl.pallas_call(inner_weight_kernel, out_shape=jax.ShapeDtypeStruct((27, C...]
  transfers between devices with their start and end apart: 8 -> 7, of which waited for: 2 -> 2; matrix products, arithmetic and copies ran while one was open for 5% -> 4% of each run, Pallas kernels for 19% -> 10%
where the time goes in v4:
time: 245 us; the launch traced here: 244 us
  blocking collectives  92.8 us (38%)
  waiting for transfers between devices  73.9 us (30%)
  Pallas kernels  28.7 us (12%)
  starting transfers between devices  16.1 us (7%)
  between operations  15.6 us (6%)
  local copies, waits for them, and re-layouts  12.3 us (5%)
  other arithmetic  4.96 us (2%)
    all_to_all x3, blocking collectives, reduce_weights(): parts = lax.all_to_all(flat.reshape(n, -1), axis, 0, 0, tiled=True)  76.3 us
    all_gather x1, waiting for transfers between devices, reduce_weights(): lax.all_gather(piece, ('gy', 'gz'), tiled=True)  69.6 us
    all_to_all x1, blocking collectives, reduce_weights(): piece = lax.all_to_all(copies, 'gx', 0, 0, tiled=True).reshape(-1)  16.5 us
    pallas_call x1, Pallas kernels, run_inputs(): pl.pallas_call(input_kernel, out_shape=jax.ShapeDtypeStruct((NB, BLOCK, C...  12.7 us
    pallas_call x1, Pallas kernels, run_inner_weights(): pl.pallas_call(inner_weight_kernel, out_shape=jax.ShapeDtypeStruct((27, C...  11.3 us
    ppermute x3, starting transfers between devices, extended(): before = lax.ppermute(last, axis, up)  10.1 us
    ppermute x3, starting transfers between devices, extended(): after = lax.ppermute(initial, axis, down)  5.96 us
  transfers between devices with their start and end apart: 7, of which 2 were waited for; matrix products, arithmetic and copies ran while one was open for 4% of the time, Pallas kernels for 10%

profile of v4, /device:TPU:1, one launch (start us, length us, event | category | flops | bytes accessed | tf_op | source)
XLA Modules:
  0.0 244.4 jit_solution(8958927546200884261)
XLA Ops:
  7.2 0.0 copy-start.1
  7.2 0.0 all-gather.3.cloned.1.call-start
  7.2 0.8 compare_select_fusion
  8.0 0.1 reshape.147
  8.1 1.8 gather_fusion
  10.0 4.0 %collective-permute-start = (bf16[1,4,128,128]{3,2,1,0:T(8,128)(2,1)S(1)}, bf16[1,4,128,128]{3,2,1,0:T(8,128)(2,1)S(1)}, u32[]{:S(2)}, u32[]{:S(2)}) collective-permute-start(bf16[1,4,128,128]{3,2,1,0:T(8,128)(2,1)S(1)} %get-tuple-element.7), channel_id=1, source_target_pairs={{0,32},{32,64},{64,96},{96,128},{128,160},{160,192},{192,224},{224... | collective-permute-start | bytes 393224 | tf_op jit(solution)/shard_map/ppermute | solution.py:25
  13.9 1.3 collective-permute-start.1
  15.2 0.1 reshape.155
  15.3 0.1 reshape.163
  15.4 1.8 gather_fusion.1
  17.2 0.0 copy-start.4
  17.3 0.0 copy-start.5
  17.3 4.0 %collective-permute-start.2 = (bf16[1,4,128,128]{3,2,1,0:T(8,128)(2,1)S(1)}, bf16[1,4,128,128]{3,2,1,0:T(8,128)(2,1)S(1)}, u32[]{:S(2)}, u32[]{:S(2)}) collective-permute-start(bf16[1,4,128,128]{3,2,1,0:T(8,128)(2,1)S(1)} %get-tuple-element.5), channel_id=1, source_target_pairs={{0,4},{4,8},{8,12},{12,16},{16,20},{20,24},{24,28},{1,5},{5,9},{9,... | collective-permute-start | bytes 393224 | tf_op jit(solution)/shard_map/ppermute | solution.py:25
  21.3 3.4 %collective-permute-start.3 = (bf16[1,4,128,128]{3,2,1,0:T(8,128)(2,1)S(1)}, bf16[1,4,128,128]{3,2,1,0:T(8,128)(2,1)S(1)}, u32[]{:S(2)}, u32[]{:S(2)}) collective-permute-start(bf16[1,4,128,128]{3,2,1,0:T(8,128)(2,1)S(1)} %get-tuple-element.4), channel_id=1, source_target_pairs={{4,0},{8,4},{12,8},{16,12},{20,16},{24,20},{28,24},{5,1},{9,5},{13... | collective-permute-start | bytes 393224 | tf_op jit(solution)/shard_map/ppermute | solution.py:26
  24.7 1.8 gather_fusion.2
  26.6 2.1 collective-permute-start.4
  28.7 0.0 copy-done.1
  28.7 1.3 copy.35
  30.0 0.1 copy.32
  30.1 0.8 reshape_squeeze.12.pairs_ref.inner_ref
  31.6 0.1 copy.33
  31.7 0.7 reshape_squeeze.13.pairs_ref.outer_ref
  33.0 11.3 %inner_weight_pairs.1.w_start = f32[27,128,128]{2,1,0:T(8,128)} custom-call(s32[864]{0:T(1024)} %reshape_squeeze.12.pairs_ref.inner_ref, s32[1]{0:T(128)} %bitcast.live_ref.inner_live_ref, bf16[32,128,128]{2,1,0:T(8,128)(2,1)} %bitcast.62, bf16[32,128,128]{2,1,0:T(8,128)(2,1)} %bitcast.52), custom_call_target="tpu_custom_call" | custom-call | flops 1207959552 | bytes 6291456 | tf_op jit(solution)/shard_map/inner_weight_pairs/pallas_call | solution.py:118
  44.3 0.0 collective-permute-done
  44.3 1.3 collective-permute-start.5
  45.6 0.0 collective-permute-done.1
  45.6 0.0 collective-permute-done.2
  45.7 0.0 collective-permute-done.3
  45.7 0.0 collective-permute-done.4
  45.7 4.2 %collective-permute-done.5 = bf16[1,4,128,128]{3,2,1,0:T(8,128)(2,1)S(1)} collective-permute-done((bf16[1,4,128,128]{3,2,1,0:T(8,128)(2,1)S(1)}, bf16[1,4,128,128]{3,2,1,0:T(8,128)(2,1)S(1)}, u32[]{:S(2)}, u32[]{:S(2)}) %collective-permute-start.5) | collective-permute-done | bytes 131104 | tf_op jit(solution)/shard_map/ppermute | solution.py:26
  50.0 0.0 copy-start
  50.0 0.9 copy-done
  50.9 4.8 %outer_weight_pairs.1 = f32[27,128,128]{2,1,0:T(8,128)} custom-call(s32[96]{0:T(128)} %reshape_squeeze.13.pairs_ref.outer_ref, s32[1]{0:T(128)} %bitcast.1.live_ref.outer_live_ref, bf16[24,128,128]{2,1,0:T(8,128)(2,1)} %copy-done, bf16[32,128,128]{2,1,0:T(8,128)(2,1)} %bitcast.53, ...), custom_call_target="tpu_custom_call", output_to_operand_aliasing={{}: (4, {})} | custom-call | flops 134217728 | bytes 6291456 | tf_op jit(solution)/shard_map/outer_weight_pairs/pallas_call | solution.py:129
  55.6 32.7 %all_to_all.33 = f32[8,1,55296]{2,1,0:T(1,128)S(1)} all-to-all(f32[8,1,55296]{2,1,0:T(1,128)} %bitcast.51), channel_id=1, replica_groups=mesh['gx'=16,'gy'=8,'gz'=4] {'gy'}, dimensions={0} | all-to-all | bytes 3538944 | tf_op jit(solution)/shard_map/all_to_all | solution.py:156
  88.3 1.3 reduce_sum.27
  89.6 9.6 %all_to_all.34 = f32[4,1,13824]{2,1,0:T(1,128)S(1)} all-to-all(f32[4,1,13824]{2,1,0:T(1,128)S(1)} %bitcast.56), channel_id=1, replica_groups=mesh['gx'=16,'gy'=8,'gz'=4] {'gz'}, dimensions={0} | all-to-all | bytes 442368 | tf_op jit(solution)/shard_map/all_to_all | solution.py:156
  99.2 0.2 reduce_sum.28
  99.4 0.1 all_to_all.26
  99.5 34.1 %all_to_all.35 = f32[16,1,864]{2,1,0:T(1,128)S(1)} all-to-all(f32[16,1,864]{2,1,0:T(1,128)S(1)} %all_to_all.26), channel_id=1, replica_groups=mesh['gx'=16,'gy'=8,'gz'=4] {'gx'}, dimensions={0} | all-to-all | bytes 110592 | tf_op jit(solution)/shard_map/all_to_all | solution.py:156
  133.7 16.5 %all_to_all.36 = f32[16,1,864]{2,1,0:T(1,128)S(1)} all-to-all(f32[16,1,864]{2,1,0:T(1,128)S(1)} %broadcast_in_dim.2), channel_id=1, replica_groups=mesh['gx'=16,'gy'=8,'gz'=4] {'gx'}, dimensions={0} | all-to-all | bytes 110592 | tf_op jit(solution)/shard_map/all_to_all | solution.py:162
  150.2 0.1 reduce.3
  150.3 0.8 reshape.178
  151.1 0.0 all-gather.3.cloned.1.call-update
  151.1 0.0 copy-done.2
  151.1 1.6 copy.34
  152.8 12.7 %input_pairs.1 = bf16[32,128,128]{2,1,0:T(8,128)(2,1)} custom-call(s32[864]{0:T(1024)} %reshape_squeeze.12.pairs_ref.inner_ref, s32[1]{0:T(128)} %bitcast.live_ref.inner_live_ref, s32[96]{0:T(128)} %reshape_squeeze.13.pairs_ref.outer_ref, s32[1]{0:T(128)} %bitcast.1.live_ref.outer_live_ref, bf16[32,128,128]{2,1,0:T(8,128)(2,1)} %bitcast.63, ...), custom_call_target="tpu_custom_call" | custom-call | flops 1342177280 | bytes 6291456 | tf_op jit(solution)/shard_map/input_pairs/pallas_call | solution.py:141
  165.4 69.6 %all-gather.3.cloned.1.call-done = f32[32,1,13824]{2,1,0:T(1,128)} async-done(((f32[1,1,13824]{2,1,0:T(1,128)}), f32[32,1,13824]{2,1,0:T(1,128)}) %all-gather.3.cloned.1.call-update) | async-done | bytes 1769488 | tf_op jit(solution)/shard_map/all_gather | solution.py:163
  235.1 2.5 %convert_element_type.3 = bf16[442368]{0:T(1024)(128)(2,1)} convert(f32[442368]{0:T(1024)} %bitcast.54) | non-fusion elementwise | flops 442368 | bytes 2654208 | tf_op jit(solution)/shard_map/convert_element_type | solution.py:164
  (19 shorter events, 0.3 us)
Async XLA Ops:
  7.2 21.5 %copy-start.1 = (bf16[1,1,1,4096,128]{4,3,2,1,0:T(8,128)(2,1)S(1)}, bf16[1,1,1,4096,128]{4,3,2,1,0:T(8,128)(2,1)}, u32[]{:S(2)}) copy-start(bf16[1,1,1,4096,128]{4,3,2,1,0:T(8,128)(2,1)} %param.8) | copy-start | bytes 3145732
  7.2 227.9 %all-gather.3.cloned.1.call-start = ((), (), s32[]{:S(2)}) async-start(), calls=%async_computation.4 | async-start | bytes 1824768 | tf_op jit(solution)/shard_map/all_gather | solution.py:163
  10.0 34.3 %collective-permute-start = (bf16[1,4,128,128]{3,2,1,0:T(8,128)(2,1)S(1)}, bf16[1,4,128,128]{3,2,1,0:T(8,128)(2,1)S(1)}, u32[]{:S(2)}, u32[]{:S(2)}) collective-permute-start(bf16[1,4,128,128]{3,2,1,0:T(8,128)(2,1)S(1)} %get-tuple-element.7), channel_id=1, source_target_pairs={{0,32},{32,64},{64,96},{96,128},{128,160},{160,192},{192,224},{224... | collective-permute-start | bytes 393224 | tf_op jit(solution)/shard_map/ppermute | solution.py:25
  13.9 31.7 %collective-permute-start.1 = (bf16[1,4,128,128]{3,2,1,0:T(8,128)(2,1)S(1)}, bf16[1,4,128,128]{3,2,1,0:T(8,128)(2,1)S(1)}, u32[]{:S(2)}, u32[]{:S(2)}) collective-permute-start(bf16[1,4,128,128]{3,2,1,0:T(8,128)(2,1)S(1)} %get-tuple-element.6), channel_id=1, source_target_pairs={{32,0},{64,32},{96,64},{128,96},{160,128},{192,160},{224,192},{256... | collective-permute-start | bytes 393224 | tf_op jit(solution)/shard_map/ppermute | solution.py:26
  17.2 12.8 %copy-start.4 = (s32[1,1,1,288,3]{3,2,4,1,0:T(1,128)S(1)}, s32[1,1,1,288,3]{3,2,4,1,0:T(1,128)}, u32[]{:S(2)}) copy-start(s32[1,1,1,288,3]{3,2,4,1,0:T(1,128)} %param.11) | copy-start | bytes 10372
  17.3 14.3 %copy-start.5 = (s32[1,1,1,32,3]{3,2,4,1,0:T(1,128)S(1)}, s32[1,1,1,32,3]{3,2,4,1,0:T(1,128)}, u32[]{:S(2)}) copy-start(s32[1,1,1,32,3]{3,2,4,1,0:T(1,128)} %param.12) | copy-start | bytes 1156
  17.3 28.3 %collective-permute-start.2 = (bf16[1,4,128,128]{3,2,1,0:T(8,128)(2,1)S(1)}, bf16[1,4,128,128]{3,2,1,0:T(8,128)(2,1)S(1)}, u32[]{:S(2)}, u32[]{:S(2)}) collective-permute-start(bf16[1,4,128,128]{3,2,1,0:T(8,128)(2,1)S(1)} %get-tuple-element.5), channel_id=1, source_target_pairs={{0,4},{4,8},{8,12},{12,16},{16,20},{20,24},{24,28},{1,5},{5,9},{9,... | collective-permute-start | bytes 393224 | tf_op jit(solution)/shard_map/ppermute | solution.py:25
  21.3 24.3 %collective-permute-start.3 = (bf16[1,4,128,128]{3,2,1,0:T(8,128)(2,1)S(1)}, bf16[1,4,128,128]{3,2,1,0:T(8,128)(2,1)S(1)}, u32[]{:S(2)}, u32[]{:S(2)}) collective-permute-start(bf16[1,4,128,128]{3,2,1,0:T(8,128)(2,1)S(1)} %get-tuple-element.4), channel_id=1, source_target_pairs={{4,0},{8,4},{12,8},{16,12},{20,16},{24,20},{28,24},{5,1},{9,5},{13... | collective-permute-start | bytes 393224 | tf_op jit(solution)/shard_map/ppermute | solution.py:26
  26.6 19.1 %collective-permute-start.4 = (bf16[1,4,128,128]{3,2,1,0:T(8,128)(2,1)S(1)}, bf16[1,4,128,128]{3,2,1,0:T(8,128)(2,1)S(1)}, u32[]{:S(2)}, u32[]{:S(2)}) collective-permute-start(bf16[1,4,128,128]{3,2,1,0:T(8,128)(2,1)S(1)} %get-tuple-element.3), channel_id=1, source_target_pairs={{0,1},{1,2},{2,3},{4,5},{5,6},{6,7},{8,9},{9,10},{10,11},{12,13},{... | collective-permute-start | bytes 393224 | tf_op jit(solution)/shard_map/ppermute | solution.py:25
  44.3 5.7 %collective-permute-start.5 = (bf16[1,4,128,128]{3,2,1,0:T(8,128)(2,1)S(1)}, bf16[1,4,128,128]{3,2,1,0:T(8,128)(2,1)S(1)}, u32[]{:S(2)}, u32[]{:S(2)}) collective-permute-start(bf16[1,4,128,128]{3,2,1,0:T(8,128)(2,1)S(1)} %get-tuple-element.2), channel_id=1, source_target_pairs={{1,0},{2,1},{3,2},{5,4},{6,5},{7,6},{9,8},{10,9},{11,10},{13,12},{... | collective-permute-start | bytes 393224 | tf_op jit(solution)/shard_map/ppermute | solution.py:26
  50.0 0.9 copy-start
  88.3 62.8 %copy-start.2 = (bf16[27,128,128]{2,1,0:T(8,128)(2,1)S(1)}, bf16[27,128,128]{2,1,0:T(8,128)(2,1)}, u32[]{:S(2)}) copy-start(bf16[27,128,128]{2,1,0:T(8,128)(2,1)} %param.10) | copy-start | bytes 2654212
  133.6 19.1 %copy-start.3 = (f32[864]{0:T(1024)}, f32[864]{0:T(1024)S(1)}, u32[]{:S(2)}) copy-start(f32[864]{0:T(1024)S(1)} %reduce_sum.29.after_ref) | copy-start | bytes 10372
Sparse Core Ops, SparseCore 0:
  151.2 83.7 all-gather.2

commit v5 on v3

--- a/solution.py
+++ b/solution.py
@@ -29,9 +29,10 @@
 
 
 def received_blocks(local_grads, face_lists):
-    got_x = extended(local_grads[face_lists[0]], (("gx", 0),), 1)
-    got_y = extended(local_grads[face_lists[1]], (("gy", 0),), 1)
-    got_z = extended(local_grads[face_lists[2]], (("gz", 0),), 1)
+    faces = local_grads[face_lists.reshape(-1)].reshape(3, 2, 4, BLOCK, C)
+    got_x = extended(faces[0], (("gx", 0),), 1)
+    got_y = extended(faces[1], (("gy", 0),), 1)
+    got_z = extended(faces[2], (("gz", 0),), 1)
     return jnp.concatenate(
         [got_x[0], got_x[3], got_y[0], got_y[3], got_z[0], got_z[3]], axis=0
     )
@@ -39,7 +40,7 @@
 
 def pair_loop(pairs_ref, live_ref, table_ref, table_base, update):
     def pair_ids(i):
-        return (pairs_ref[3 * i], pairs_ref[3 * i + 1] - table_base, pairs_ref[3 * i + 2])
+        return (pairs_ref[i, 0], pairs_ref[i, 1] - table_base, pairs_ref[i, 2])
 
     def one_group(group, carry):
         ids = [pair_ids(group * UNROLL + j) for j in range(UNROLL)]
@@ -52,7 +53,7 @@
         update([(k, a, b)], [table_ref[a]])
         return carry
 
-    live = live_ref[0]
+    live = jnp.clip(live_ref[0], 0, pairs_ref.shape[0])
     groups = live // UNROLL
     lax.fori_loop(0, groups, one_group, 0)
     lax.fori_loop(groups * UNROLL, live, one_pair, 0)
@@ -169,10 +170,10 @@
     local_grads = output_grad[0, 0, 0].reshape(NB, BLOCK, C)
     feats_t = jnp.swapaxes(features[0, 0, 0].reshape(NB, BLOCK, C), 1, 2)
     kernel_t = jnp.swapaxes(kernel, 1, 2)
-    inner_pairs = inner_map[0, 0, 0].reshape(-1)
-    outer_pairs = outer_map[0, 0, 0].reshape(-1)
-    inner_n = jnp.clip(inner_live[0, 0, 0], 0, PI).reshape(1)
-    outer_n = jnp.clip(outer_live[0, 0, 0], 0, PB).reshape(1)
+    inner_pairs = inner_map[0, 0, 0]
+    outer_pairs = outer_map[0, 0, 0]
+    inner_n = inner_live[0, 0]
+    outer_n = outer_live[0, 0]
     received = received_blocks(local_grads, face_blocks[0, 0, 0])
     acc_w = run_inner_weights(inner_pairs, inner_n, local_grads, feats_t)
     acc_w = run_outer_weights(outer_pairs, outer_n, received, feats_t, acc_w)

time: 184 us -> 183 us (level)
  the two profiles are of different devices: /device:TPU:1 before, /device:TPU:3 now
where the time goes in v5:
time: 183 us
  blocking collectives  67.8 us (37%)
  starting transfers between devices  41.2 us (23%)
  Pallas kernels  40 us (22%)
  waiting for transfers between devices  16.7 us (9%)
  local copies, waits for them, and re-layouts  11.5 us (6%)
  other arithmetic  3.19 us (2%)
  between operations  2.19 us (1%)
    all_to_all x2, blocking collectives, reduce_weights(): parts = lax.all_to_all(flat.reshape(n, -1), axis, 0, 0, tiled=True)  35.3 us
    all_gather x1, blocking collectives, reduce_weights(): piece = lax.all_gather(piece, 'gy', tiled=True)  20.9 us
    all_to_all x1, starting transfers between devices, reduce_weights(): parts = lax.all_to_all(flat.reshape(n, -1), axis, 0, 0, tiled=True)  20.4 us
    pallas_call x1, Pallas kernels, run_inputs(): pl.pallas_call(input_kernel, out_shape=jax.ShapeDtypeStruct((NB, BLOCK, C...  18.5 us
    pallas_call x1, Pallas kernels, run_inner_weights(): pl.pallas_call(inner_weight_kernel, out_shape=jax.ShapeDtypeStruct((27, C...  16.5 us
    all_gather x1, blocking collectives, reduce_weights(): piece = lax.all_gather(piece, 'gz', tiled=True)  11.6 us
    all_to_all x1, waiting for transfers between devices, reduce_weights(): parts = lax.all_to_all(flat.reshape(n, -1), axis, 0, 0, tiled=True)  11.2 us
    ppermute x3, starting transfers between devices, extended(): before = lax.ppermute(last, axis, up)  9.53 us
  transfers between devices with their start and end apart: 8, of which 2 were waited for; matrix products, arithmetic and copies ran while one was open for 2% of the time, Pallas kernels for 19%

profile of v5, /device:TPU:3, one launch (start us, length us, event | category | flops | bytes accessed | tf_op | source)
XLA Modules:
  0.0 182.6 jit_solution(162184488749907177)
XLA Ops:
  0.6 0.0 copy-start.1
  0.6 0.9 reshape_squeeze.10
  1.5 1.9 %gather_fusion = bf16[24,128,128]{2,1,0:T(8,128)(2,1)S(1)} fusion(bf16[32,128,128]{2,1,0:T(8,128)(2,1)} %bitcast.49, s32[1024]{0:T(1024)S(1)} %pad_clamp_fusion), kind=kCustom, calls=%fused_computation | custom fusion | bytes 1572960 | tf_op jit(solution)/shard_map/gather | solution.py:32
  3.4 0.0 copy-start.4
  3.5 0.0 copy-start.5
  3.5 0.1 slice_bitcast_fusion
  3.5 3.1 %collective-permute-start = (bf16[1,4,128,128]{3,2,1,0:T(8,128)(2,1)S(1)}, bf16[1,4,128,128]{3,2,1,0:T(8,128)(2,1)S(1)}, u32[]{:S(2)}, u32[]{:S(2)}) collective-permute-start(bf16[1,4,128,128]{3,2,1,0:T(8,128)(2,1)S(1)} %get-tuple-element.7), channel_id=1, source_target_pairs={{0,32},{32,64},{64,96},{96,128},{128,160},{160,192},{192,224},{224... | collective-permute-start | bytes 393224 | tf_op jit(solution)/shard_map/ppermute | solution.py:25
  6.7 2.2 %collective-permute-start.1 = (bf16[1,4,128,128]{3,2,1,0:T(8,128)(2,1)S(1)}, bf16[1,4,128,128]{3,2,1,0:T(8,128)(2,1)S(1)}, u32[]{:S(2)}, u32[]{:S(2)}) collective-permute-start(bf16[1,4,128,128]{3,2,1,0:T(8,128)(2,1)S(1)} %get-tuple-element.6), channel_id=1, source_target_pairs={{32,0},{64,32},{96,64},{128,96},{160,128},{192,160},{224,192},{256... | collective-permute-start | bytes 393224 | tf_op jit(solution)/shard_map/ppermute | solution.py:26
  8.8 4.3 %collective-permute-start.2 = (bf16[1,4,128,128]{3,2,1,0:T(8,128)(2,1)S(1)}, bf16[1,4,128,128]{3,2,1,0:T(8,128)(2,1)S(1)}, u32[]{:S(2)}, u32[]{:S(2)}) collective-permute-start(bf16[1,4,128,128]{3,2,1,0:T(8,128)(2,1)S(1)} %get-tuple-element.5), channel_id=1, source_target_pairs={{0,4},{4,8},{8,12},{12,16},{16,20},{20,24},{24,28},{1,5},{5,9},{9,... | collective-permute-start | bytes 393224 | tf_op jit(solution)/shard_map/ppermute | solution.py:25
  13.2 3.4 %collective-permute-start.3 = (bf16[1,4,128,128]{3,2,1,0:T(8,128)(2,1)S(1)}, bf16[1,4,128,128]{3,2,1,0:T(8,128)(2,1)S(1)}, u32[]{:S(2)}, u32[]{:S(2)}) collective-permute-start(bf16[1,4,128,128]{3,2,1,0:T(8,128)(2,1)S(1)} %get-tuple-element.4), channel_id=1, source_target_pairs={{4,0},{8,4},{12,8},{16,12},{20,16},{24,20},{28,24},{5,1},{9,5},{13... | collective-permute-start | bytes 393224 | tf_op jit(solution)/shard_map/ppermute | solution.py:26
  16.6 2.1 %collective-permute-start.4 = (bf16[1,4,128,128]{3,2,1,0:T(8,128)(2,1)S(1)}, bf16[1,4,128,128]{3,2,1,0:T(8,128)(2,1)S(1)}, u32[]{:S(2)}, u32[]{:S(2)}) collective-permute-start(bf16[1,4,128,128]{3,2,1,0:T(8,128)(2,1)S(1)} %get-tuple-element.3), channel_id=1, source_target_pairs={{0,1},{1,2},{2,3},{4,5},{5,6},{6,7},{8,9},{9,10},{10,11},{12,13},{... | collective-permute-start | bytes 393224 | tf_op jit(solution)/shard_map/ppermute | solution.py:25
  18.7 0.0 copy-done.1
  18.7 1.3 copy.34
  20.0 0.0 copy-done.4
  20.0 0.8 copy.32
  21.4 0.7 copy.40
  22.8 16.5 %inner_weight_pairs.1.w_start = f32[27,128,128]{2,1,0:T(8,128)} custom-call(s32[288,3]{1,0:T(8,128)} %bitcast.52, s32[1]{0:T(128)} %bitcast.38.live_ref, bf16[32,128,128]{2,1,0:T(8,128)(2,1)} %bitcast.50, bf16[32,128,128]{2,1,0:T(8,128)(2,1)} %bitcast.43), custom_call_target="tpu_custom_call" | custom-call | flops 1207959552 | bytes 6291456 | tf_op jit(solution)/shard_map/inner_weight_pairs/pallas_call | solution.py:119
  39.3 0.0 collective-permute-done
  39.3 1.3 collective-permute-start.5
  40.6 0.0 collective-permute-done.1
  40.6 0.0 collective-permute-done.2
  40.7 0.0 collective-permute-done.3
  40.7 0.0 collective-permute-done.4
  40.7 5.5 %collective-permute-done.5 = bf16[1,4,128,128]{3,2,1,0:T(8,128)(2,1)S(1)} collective-permute-done((bf16[1,4,128,128]{3,2,1,0:T(8,128)(2,1)S(1)}, bf16[1,4,128,128]{3,2,1,0:T(8,128)(2,1)S(1)}, u32[]{:S(2)}, u32[]{:S(2)}) %collective-permute-start.5) | collective-permute-done | bytes 131104 | tf_op jit(solution)/shard_map/ppermute | solution.py:26
  46.3 0.9 copy-done
  47.2 5.1 %outer_weight_pairs.1 = f32[27,128,128]{2,1,0:T(8,128)} custom-call(s32[32,3]{1,0:T(8,128)} %bitcast.54, s32[1]{0:T(128)} %bitcast.40.live_ref, bf16[24,128,128]{2,1,0:T(8,128)(2,1)} %copy-done, bf16[32,128,128]{2,1,0:T(8,128)(2,1)} %bitcast.44, f32[27,128,128]{2,1,0:T(8,128)} %inner_weight_pairs.1.w_start), custom_call_target="tpu_custom_call", output_to_operand_aliasing={{}: (4, {})} | custom-call | flops 134217728 | bytes 6291456 | tf_op jit(solution)/shard_map/outer_weight_pairs/pallas_call | solution.py:130
  52.2 27.1 %all_to_all.33 = f32[8,1,55296]{2,1,0:T(1,128)S(1)} all-to-all(f32[8,1,55296]{2,1,0:T(1,128)} %bitcast.42), channel_id=1, replica_groups=mesh['gx'=16,'gy'=8,'gz'=4] {'gy'}, dimensions={0} | all-to-all | bytes 3538944 | tf_op jit(solution)/shard_map/all_to_all | solution.py:157
  79.4 1.3 reduce_sum.27
  80.6 8.1 %all_to_all.34 = f32[4,1,13824]{2,1,0:T(1,128)S(1)} all-to-all(f32[4,1,13824]{2,1,0:T(1,128)S(1)} %bitcast.47), channel_id=1, replica_groups=mesh['gx'=16,'gy'=8,'gz'=4] {'gz'}, dimensions={0} | all-to-all | bytes 442368 | tf_op jit(solution)/shard_map/all_to_all | solution.py:157
  88.8 0.2 reduce_sum.28
  89.0 0.7 all_to_all.26
  89.7 20.4 %all-to-all-start.2 = ((f32[16,1,864]{2,1,0:T(1,128)}), f32[16,1,864]{2,1,0:T(1,128)S(1)}, u32[]{:S(2)}, u32[]{:S(2)}) async-start(f32[16,1,864]{2,1,0:T(1,128)} %all_to_all.26), calls=%async_computation.2 | async-start | bytes 114688 | tf_op jit(solution)/shard_map/all_to_all | solution.py:157
  110.1 0.0 copy-done.2
  110.1 1.6 copy.33
  111.8 11.2 %all-to-all-done.2 = f32[16,1,864]{2,1,0:T(1,128)S(1)} async-done(((f32[16,1,864]{2,1,0:T(1,128)}), f32[16,1,864]{2,1,0:T(1,128)S(1)}, u32[]{:S(2)}, u32[]{:S(2)}) %all-to-all-start.2) | async-done | bytes 55328 | tf_op jit(solution)/shard_map/all_to_all | solution.py:157
  123.1 0.5 broadcast.38
  123.6 0.8 reduce.5
  124.4 0.7 reshape.92
  125.1 4.5 %all-to-all-start.3 = ((bf16[16,2,432]{2,1,0:T(2,128)(2,1)}), bf16[16,2,432]{2,1,0:T(2,128)(2,1)S(1)}, u32[]{:S(2)}, u32[]{:S(2)}) async-start(bf16[16,2,432]{2,1,0:T(2,128)(2,1)} %reshape.92), calls=%async_computation.3 | async-start | bytes 65536 | tf_op jit(solution)/shard_map/all_to_all | solution.py:163
  129.6 18.5 %input_pairs.1 = bf16[32,128,128]{2,1,0:T(8,128)(2,1)} custom-call(s32[288,3]{1,0:T(8,128)} %bitcast.53, s32[1]{0:T(128)} %bitcast.39.inner_live_ref, s32[32,3]{1,0:T(8,128)} %bitcast.55, s32[1]{0:T(128)} %bitcast.41.outer_live_ref, bf16[32,128,128]{2,1,0:T(8,128)(2,1)} %bitcast.51, bf16[24,128,128]{2,1,0:T(8,128)(2,1)} %copy-done, ...), custom_call_target="tpu_custom_call" | custom-call | flops 1342177280 | bytes 6291456 | tf_op jit(solution)/shard_map/input_pairs/pallas_call | solution.py:142
  148.0 0.0 all-to-all-done.3
  148.0 0.1 reshape.93
  148.2 0.2 reduce.3
  148.3 0.1 reshape.87
  148.4 11.6 %all-gather = bf16[4,1,13824]{2,1,0:T(2,128)(2,1)S(1)} all-gather(bf16[1,1,13824]{2,1,0:T(2,128)(2,1)S(1)} %reshape.87), channel_id=1, replica_groups=mesh['gx'=16,'gy'=8,'gz'=4] {'gz'}, dimensions={0}, use_global_device_ids=true | all-gather | bytes 138240 | tf_op jit(solution)/shard_map/all_gather | solution.py:164
  160.0 0.7 reduce.4
  160.8 20.9 %all_gather.7 = bf16[442368]{0:T(1024)(128)(2,1)S(1)} all-gather(bf16[55296]{0:T(1024)(128)(2,1)S(1)} %reshape.88), channel_id=1, replica_groups=mesh['gx'=16,'gy'=8,'gz'=4] {'gy'}, dimensions={0}, use_global_device_ids=true | all-gather | bytes 995328 | tf_op jit(solution)/shard_map/all_gather | solution.py:165
  181.7 0.9 copy.52
  (17 shorter events, 0.3 us)
Async XLA Ops:
  0.6 18.0 %copy-start.1 = (bf16[1,1,1,4096,128]{4,3,2,1,0:T(8,128)(2,1)S(1)}, bf16[1,1,1,4096,128]{4,3,2,1,0:T(8,128)(2,1)}, u32[]{:S(2)}) copy-start(bf16[1,1,1,4096,128]{4,3,2,1,0:T(8,128)(2,1)} %param.8) | copy-start | bytes 3145732
  3.4 16.5 %copy-start.4 = (s32[1,1,1,288,3]{3,2,4,1,0:T(1,128)S(1)}, s32[1,1,1,288,3]{3,2,4,1,0:T(1,128)}, u32[]{:S(2)}) copy-start(s32[1,1,1,288,3]{3,2,4,1,0:T(1,128)} %param.11) | copy-start | bytes 10372
  3.5 18.0 %copy-start.5 = (s32[1,1,1,32,3]{3,2,4,1,0:T(1,128)S(1)}, s32[1,1,1,32,3]{3,2,4,1,0:T(1,128)}, u32[]{:S(2)}) copy-start(s32[1,1,1,32,3]{3,2,4,1,0:T(1,128)} %param.12) | copy-start | bytes 1156
  3.5 35.7 %collective-permute-start = (bf16[1,4,128,128]{3,2,1,0:T(8,128)(2,1)S(1)}, bf16[1,4,128,128]{3,2,1,0:T(8,128)(2,1)S(1)}, u32[]{:S(2)}, u32[]{:S(2)}) collective-permute-start(bf16[1,4,128,128]{3,2,1,0:T(8,128)(2,1)S(1)} %get-tuple-element.7), channel_id=1, source_target_pairs={{0,32},{32,64},{64,96},{96,128},{128,160},{160,192},{192,224},{224... | collective-permute-start | bytes 393224 | tf_op jit(solution)/shard_map/ppermute | solution.py:25
  6.7 33.9 %collective-permute-start.1 = (bf16[1,4,128,128]{3,2,1,0:T(8,128)(2,1)S(1)}, bf16[1,4,128,128]{3,2,1,0:T(8,128)(2,1)S(1)}, u32[]{:S(2)}, u32[]{:S(2)}) collective-permute-start(bf16[1,4,128,128]{3,2,1,0:T(8,128)(2,1)S(1)} %get-tuple-element.6), channel_id=1, source_target_pairs={{32,0},{64,32},{96,64},{128,96},{160,128},{192,160},{224,192},{256... | collective-permute-start | bytes 393224 | tf_op jit(solution)/shard_map/ppermute | solution.py:26
  8.8 31.8 %collective-permute-start.2 = (bf16[1,4,128,128]{3,2,1,0:T(8,128)(2,1)S(1)}, bf16[1,4,128,128]{3,2,1,0:T(8,128)(2,1)S(1)}, u32[]{:S(2)}, u32[]{:S(2)}) collective-permute-start(bf16[1,4,128,128]{3,2,1,0:T(8,128)(2,1)S(1)} %get-tuple-element.5), channel_id=1, source_target_pairs={{0,4},{4,8},{8,12},{12,16},{16,20},{20,24},{24,28},{1,5},{5,9},{9,... | collective-permute-start | bytes 393224 | tf_op jit(solution)/shard_map/ppermute | solution.py:25
  13.2 27.5 %collective-permute-start.3 = (bf16[1,4,128,128]{3,2,1,0:T(8,128)(2,1)S(1)}, bf16[1,4,128,128]{3,2,1,0:T(8,128)(2,1)S(1)}, u32[]{:S(2)}, u32[]{:S(2)}) collective-permute-start(bf16[1,4,128,128]{3,2,1,0:T(8,128)(2,1)S(1)} %get-tuple-element.4), channel_id=1, source_target_pairs={{4,0},{8,4},{12,8},{16,12},{20,16},{24,20},{28,24},{5,1},{9,5},{13... | collective-permute-start | bytes 393224 | tf_op jit(solution)/shard_map/ppermute | solution.py:26
  16.6 24.1 %collective-permute-start.4 = (bf16[1,4,128,128]{3,2,1,0:T(8,128)(2,1)S(1)}, bf16[1,4,128,128]{3,2,1,0:T(8,128)(2,1)S(1)}, u32[]{:S(2)}, u32[]{:S(2)}) collective-permute-start(bf16[1,4,128,128]{3,2,1,0:T(8,128)(2,1)S(1)} %get-tuple-element.3), channel_id=1, source_target_pairs={{0,1},{1,2},{2,3},{4,5},{5,6},{6,7},{8,9},{9,10},{10,11},{12,13},{... | collective-permute-start | bytes 393224 | tf_op jit(solution)/shard_map/ppermute | solution.py:25
  39.3 7.0 %collective-permute-start.5 = (bf16[1,4,128,128]{3,2,1,0:T(8,128)(2,1)S(1)}, bf16[1,4,128,128]{3,2,1,0:T(8,128)(2,1)S(1)}, u32[]{:S(2)}, u32[]{:S(2)}) collective-permute-start(bf16[1,4,128,128]{3,2,1,0:T(8,128)(2,1)S(1)} %get-tuple-element.2), channel_id=1, source_target_pairs={{1,0},{2,1},{3,2},{5,4},{6,5},{7,6},{9,8},{10,9},{11,10},{13,12},{... | collective-permute-start | bytes 393224 | tf_op jit(solution)/shard_map/ppermute | solution.py:26
  46.3 0.9 copy-start
  79.4 30.8 %copy-start.2 = (bf16[27,128,128]{2,1,0:T(8,128)(2,1)S(1)}, bf16[27,128,128]{2,1,0:T(8,128)(2,1)}, u32[]{:S(2)}) copy-start(bf16[27,128,128]{2,1,0:T(8,128)(2,1)} %param.10) | copy-start | bytes 2654212
  89.7 33.2 %all-to-all-start.2 = ((f32[16,1,864]{2,1,0:T(1,128)}), f32[16,1,864]{2,1,0:T(1,128)S(1)}, u32[]{:S(2)}, u32[]{:S(2)}) async-start(f32[16,1,864]{2,1,0:T(1,128)} %all_to_all.26), calls=%async_computation.2 | async-start | bytes 114688 | tf_op jit(solution)/shard_map/all_to_all | solution.py:157
  123.0 6.6 %copy-start.3 = (f32[864]{0:T(1024)}, f32[864]{0:T(1024)S(1)}, u32[]{:S(2)}) copy-start(f32[864]{0:T(1024)S(1)} %reduce_sum.29.after_ref) | copy-start | bytes 10372
  125.1 22.9 %all-to-all-start.3 = ((bf16[16,2,432]{2,1,0:T(2,128)(2,1)}), bf16[16,2,432]{2,1,0:T(2,128)(2,1)S(1)}, u32[]{:S(2)}, u32[]{:S(2)}) async-start(bf16[16,2,432]{2,1,0:T(2,128)(2,1)} %reshape.92), calls=%async_computation.3 | async-start | bytes 65536 | tf_op jit(solution)/shard_map/all_to_all | solution.py:163

commit v6 on v5

--- a/solution.py
+++ b/solution.py
@@ -12,7 +12,7 @@
 NB = 32
 PI = 288
 PB = 32
-UNROLL = 4
+UNROLL = 8
 
 
 def extended(shard, sides, width):

time: 183 us -> 175 us (0.956)
  the two profiles are of different devices: /device:TPU:3 before, /device:TPU:1 now
where the time goes in v6:
time: 175 us; the launch traced here: 174 us
  blocking collectives  69.6 us (40%)
  starting transfers between devices  40.3 us (23%)
  waiting for transfers between devices  24.9 us (14%)
  Pallas kernels  22.8 us (13%)
  local copies, waits for them, and re-layouts  11.4 us (7%)
  other arithmetic  3.19 us (2%)
  between operations  2.22 us (1%)
    all_to_all x2, blocking collectives, reduce_weights(): parts = lax.all_to_all(flat.reshape(n, -1), axis, 0, 0, tiled=True)  36.9 us
    all_gather x1, blocking collectives, reduce_weights(): piece = lax.all_gather(piece, 'gy', tiled=True)  21.5 us
    all_to_all x1, starting transfers between devices, reduce_weights(): parts = lax.all_to_all(flat.reshape(n, -1), axis, 0, 0, tiled=True)  20.8 us
    all_to_all x1, waiting for transfers between devices, reduce_weights(): parts = lax.all_to_all(flat.reshape(n, -1), axis, 0, 0, tiled=True)  12.3 us
    all_gather x1, blocking collectives, reduce_weights(): piece = lax.all_gather(piece, 'gz', tiled=True)  11.2 us
    ppermute x3, starting transfers between devices, extended(): before = lax.ppermute(last, axis, up)  10.1 us
    pallas_call x1, Pallas kernels, run_inputs(): pl.pallas_call(input_kernel, out_shape=jax.ShapeDtypeStruct((NB, BLOCK, C...  9.83 us
    ppermute x3, waiting for transfers between devices, extended(): after = lax.ppermute(initial, axis, down)  8.73 us
  transfers between devices with their start and end apart: 8, of which 3 were waited for; matrix products, arithmetic and copies ran while one was open for 3% of the time, Pallas kernels for 10%

profile of v6, /device:TPU:1, one launch (start us, length us, event | category | flops | bytes accessed | tf_op | source)
XLA Modules:
  0.0 174.4 jit_solution(10171169057984507770)
XLA Ops:
  0.6 0.0 copy-start.1
  0.6 0.9 reshape_squeeze.10
  1.5 1.9 %gather_fusion = bf16[24,128,128]{2,1,0:T(8,128)(2,1)S(1)} fusion(bf16[32,128,128]{2,1,0:T(8,128)(2,1)} %bitcast.49, s32[1024]{0:T(1024)S(1)} %pad_clamp_fusion), kind=kCustom, calls=%fused_computation | custom fusion | bytes 1572960 | tf_op jit(solution)/shard_map/gather | solution.py:32
  3.4 0.0 copy-start.4
  3.5 0.0 copy-start.5
  3.5 0.1 slice_bitcast_fusion
  3.5 4.0 %collective-permute-start = (bf16[1,4,128,128]{3,2,1,0:T(8,128)(2,1)S(1)}, bf16[1,4,128,128]{3,2,1,0:T(8,128)(2,1)S(1)}, u32[]{:S(2)}, u32[]{:S(2)}) collective-permute-start(bf16[1,4,128,128]{3,2,1,0:T(8,128)(2,1)S(1)} %get-tuple-element.7), channel_id=1, source_target_pairs={{0,32},{32,64},{64,96},{96,128},{128,160},{160,192},{192,224},{224... | collective-permute-start | bytes 393224 | tf_op jit(solution)/shard_map/ppermute | solution.py:25
  7.5 1.3 collective-permute-start.1
  8.8 4.0 %collective-permute-start.2 = (bf16[1,4,128,128]{3,2,1,0:T(8,128)(2,1)S(1)}, bf16[1,4,128,128]{3,2,1,0:T(8,128)(2,1)S(1)}, u32[]{:S(2)}, u32[]{:S(2)}) collective-permute-start(bf16[1,4,128,128]{3,2,1,0:T(8,128)(2,1)S(1)} %get-tuple-element.5), channel_id=1, source_target_pairs={{0,4},{4,8},{8,12},{12,16},{16,20},{20,24},{24,28},{1,5},{5,9},{9,... | collective-permute-start | bytes 393224 | tf_op jit(solution)/shard_map/ppermute | solution.py:25
  12.9 3.4 %collective-permute-start.3 = (bf16[1,4,128,128]{3,2,1,0:T(8,128)(2,1)S(1)}, bf16[1,4,128,128]{3,2,1,0:T(8,128)(2,1)S(1)}, u32[]{:S(2)}, u32[]{:S(2)}) collective-permute-start(bf16[1,4,128,128]{3,2,1,0:T(8,128)(2,1)S(1)} %get-tuple-element.4), channel_id=1, source_target_pairs={{4,0},{8,4},{12,8},{16,12},{20,16},{24,20},{28,24},{5,1},{9,5},{13... | collective-permute-start | bytes 393224 | tf_op jit(solution)/shard_map/ppermute | solution.py:26
  16.2 2.1 %collective-permute-start.4 = (bf16[1,4,128,128]{3,2,1,0:T(8,128)(2,1)S(1)}, bf16[1,4,128,128]{3,2,1,0:T(8,128)(2,1)S(1)}, u32[]{:S(2)}, u32[]{:S(2)}) collective-permute-start(bf16[1,4,128,128]{3,2,1,0:T(8,128)(2,1)S(1)} %get-tuple-element.3), channel_id=1, source_target_pairs={{0,1},{1,2},{2,3},{4,5},{5,6},{6,7},{8,9},{9,10},{10,11},{12,13},{... | collective-permute-start | bytes 393224 | tf_op jit(solution)/shard_map/ppermute | solution.py:25
  18.3 0.0 copy-done.1
  18.4 1.3 copy.34
  19.7 0.0 copy-done.4
  19.7 0.8 copy.32
  21.1 0.0 copy-done.5
  21.1 0.7 copy.40
  22.5 8.1 %inner_weight_pairs.1.w_start = f32[27,128,128]{2,1,0:T(8,128)} custom-call(s32[288,3]{1,0:T(8,128)} %bitcast.52, s32[1]{0:T(128)} %bitcast.38.live_ref, bf16[32,128,128]{2,1,0:T(8,128)(2,1)} %bitcast.50, bf16[32,128,128]{2,1,0:T(8,128)(2,1)} %bitcast.43), custom_call_target="tpu_custom_call" | custom-call | flops 1207959552 | bytes 6291456 | tf_op jit(solution)/shard_map/inner_weight_pairs/pallas_call | solution.py:119
  30.6 0.0 collective-permute-done
  30.6 1.3 collective-permute-start.5
  31.9 0.0 collective-permute-done.1
  31.9 0.0 collective-permute-done.2
  32.0 0.0 collective-permute-done.3
  32.0 0.0 collective-permute-done.4
  32.0 8.7 %collective-permute-done.5 = bf16[1,4,128,128]{3,2,1,0:T(8,128)(2,1)S(1)} collective-permute-done((bf16[1,4,128,128]{3,2,1,0:T(8,128)(2,1)S(1)}, bf16[1,4,128,128]{3,2,1,0:T(8,128)(2,1)S(1)}, u32[]{:S(2)}, u32[]{:S(2)}) %collective-permute-start.5) | collective-permute-done | bytes 131104 | tf_op jit(solution)/shard_map/ppermute | solution.py:26
  40.8 0.9 copy-done
  41.7 4.8 %outer_weight_pairs.1 = f32[27,128,128]{2,1,0:T(8,128)} custom-call(s32[32,3]{1,0:T(8,128)} %bitcast.54, s32[1]{0:T(128)} %bitcast.40.live_ref, bf16[24,128,128]{2,1,0:T(8,128)(2,1)} %copy-done, bf16[32,128,128]{2,1,0:T(8,128)(2,1)} %bitcast.44, f32[27,128,128]{2,1,0:T(8,128)} %inner_weight_pairs.1.w_start), custom_call_target="tpu_custom_call", output_to_operand_aliasing={{}: (4, {})} | custom-call | flops 134217728 | bytes 6291456 | tf_op jit(solution)/shard_map/outer_weight_pairs/pallas_call | solution.py:130
  46.5 28.5 %all_to_all.33 = f32[8,1,55296]{2,1,0:T(1,128)S(1)} all-to-all(f32[8,1,55296]{2,1,0:T(1,128)} %bitcast.42), channel_id=1, replica_groups=mesh['gx'=16,'gy'=8,'gz'=4] {'gy'}, dimensions={0} | all-to-all | bytes 3538944 | tf_op jit(solution)/shard_map/all_to_all | solution.py:157
  74.9 1.3 reduce_sum.27
  76.2 8.4 %all_to_all.34 = f32[4,1,13824]{2,1,0:T(1,128)S(1)} all-to-all(f32[4,1,13824]{2,1,0:T(1,128)S(1)} %bitcast.47), channel_id=1, replica_groups=mesh['gx'=16,'gy'=8,'gz'=4] {'gz'}, dimensions={0} | all-to-all | bytes 442368 | tf_op jit(solution)/shard_map/all_to_all | solution.py:157
  84.6 0.2 reduce_sum.28
  84.8 0.7 all_to_all.26
  85.6 20.8 %all-to-all-start.2 = ((f32[16,1,864]{2,1,0:T(1,128)}), f32[16,1,864]{2,1,0:T(1,128)S(1)}, u32[]{:S(2)}, u32[]{:S(2)}) async-start(f32[16,1,864]{2,1,0:T(1,128)} %all_to_all.26), calls=%async_computation.2 | async-start | bytes 114688 | tf_op jit(solution)/shard_map/all_to_all | solution.py:157
  106.4 1.6 copy.33
  108.0 12.3 %all-to-all-done.2 = f32[16,1,864]{2,1,0:T(1,128)S(1)} async-done(((f32[16,1,864]{2,1,0:T(1,128)}), f32[16,1,864]{2,1,0:T(1,128)S(1)}, u32[]{:S(2)}, u32[]{:S(2)}) %all-to-all-start.2) | async-done | bytes 55328 | tf_op jit(solution)/shard_map/all_to_all | solution.py:157
  120.4 0.5 broadcast.38
  120.9 0.8 reduce.5
  121.7 0.7 reshape.92
  122.5 3.5 %all-to-all-start.3 = ((bf16[16,2,432]{2,1,0:T(2,128)(2,1)}), bf16[16,2,432]{2,1,0:T(2,128)(2,1)S(1)}, u32[]{:S(2)}, u32[]{:S(2)}) async-start(bf16[16,2,432]{2,1,0:T(2,128)(2,1)} %reshape.92), calls=%async_computation.3 | async-start | bytes 65536 | tf_op jit(solution)/shard_map/all_to_all | solution.py:163
  126.0 9.8 %input_pairs.1 = bf16[32,128,128]{2,1,0:T(8,128)(2,1)} custom-call(s32[288,3]{1,0:T(8,128)} %bitcast.53, s32[1]{0:T(128)} %bitcast.39.inner_live_ref, s32[32,3]{1,0:T(8,128)} %bitcast.55, s32[1]{0:T(128)} %bitcast.41.outer_live_ref, bf16[32,128,128]{2,1,0:T(8,128)(2,1)} %bitcast.51, bf16[24,128,128]{2,1,0:T(8,128)(2,1)} %copy-done, ...), custom_call_target="tpu_custom_call" | custom-call | flops 1342177280 | bytes 6291456 | tf_op jit(solution)/shard_map/input_pairs/pallas_call | solution.py:142
  135.8 3.9 %all-to-all-done.3 = bf16[16,2,432]{2,1,0:T(2,128)(2,1)S(1)} async-done(((bf16[16,2,432]{2,1,0:T(2,128)(2,1)}), bf16[16,2,432]{2,1,0:T(2,128)(2,1)S(1)}, u32[]{:S(2)}, u32[]{:S(2)}) %all-to-all-start.3) | async-done | bytes 27680 | tf_op jit(solution)/shard_map/all_to_all | solution.py:163
  139.7 0.1 reshape.93
  139.8 0.2 reduce.3
  140.0 0.1 reshape.87
  140.1 11.2 %all-gather = bf16[4,1,13824]{2,1,0:T(2,128)(2,1)S(1)} all-gather(bf16[1,1,13824]{2,1,0:T(2,128)(2,1)S(1)} %reshape.87), channel_id=1, replica_groups=mesh['gx'=16,'gy'=8,'gz'=4] {'gz'}, dimensions={0}, use_global_device_ids=true | all-gather | bytes 138240 | tf_op jit(solution)/shard_map/all_gather | solution.py:164
  151.3 0.7 reduce.4
  152.0 21.5 %all_gather.7 = bf16[442368]{0:T(1024)(128)(2,1)S(1)} all-gather(bf16[55296]{0:T(1024)(128)(2,1)S(1)} %reshape.88), channel_id=1, replica_groups=mesh['gx'=16,'gy'=8,'gz'=4] {'gy'}, dimensions={0}, use_global_device_ids=true | all-gather | bytes 995328 | tf_op jit(solution)/shard_map/all_gather | solution.py:165
  173.5 0.9 copy.52
  (17 shorter events, 0.3 us)
Async XLA Ops:
  0.6 17.7 %copy-start.1 = (bf16[1,1,1,4096,128]{4,3,2,1,0:T(8,128)(2,1)S(1)}, bf16[1,1,1,4096,128]{4,3,2,1,0:T(8,128)(2,1)}, u32[]{:S(2)}) copy-start(bf16[1,1,1,4096,128]{4,3,2,1,0:T(8,128)(2,1)} %param.8) | copy-start | bytes 3145732
  3.4 16.2 %copy-start.4 = (s32[1,1,1,288,3]{3,2,4,1,0:T(1,128)S(1)}, s32[1,1,1,288,3]{3,2,4,1,0:T(1,128)}, u32[]{:S(2)}) copy-start(s32[1,1,1,288,3]{3,2,4,1,0:T(1,128)} %param.11) | copy-start | bytes 10372
  3.5 17.7 %copy-start.5 = (s32[1,1,1,32,3]{3,2,4,1,0:T(1,128)S(1)}, s32[1,1,1,32,3]{3,2,4,1,0:T(1,128)}, u32[]{:S(2)}) copy-start(s32[1,1,1,32,3]{3,2,4,1,0:T(1,128)} %param.12) | copy-start | bytes 1156
  3.5 27.0 %collective-permute-start = (bf16[1,4,128,128]{3,2,1,0:T(8,128)(2,1)S(1)}, bf16[1,4,128,128]{3,2,1,0:T(8,128)(2,1)S(1)}, u32[]{:S(2)}, u32[]{:S(2)}) collective-permute-start(bf16[1,4,128,128]{3,2,1,0:T(8,128)(2,1)S(1)} %get-tuple-element.7), channel_id=1, source_target_pairs={{0,32},{32,64},{64,96},{96,128},{128,160},{160,192},{192,224},{224... | collective-permute-start | bytes 393224 | tf_op jit(solution)/shard_map/ppermute | solution.py:25
  7.5 24.4 %collective-permute-start.1 = (bf16[1,4,128,128]{3,2,1,0:T(8,128)(2,1)S(1)}, bf16[1,4,128,128]{3,2,1,0:T(8,128)(2,1)S(1)}, u32[]{:S(2)}, u32[]{:S(2)}) collective-permute-start(bf16[1,4,128,128]{3,2,1,0:T(8,128)(2,1)S(1)} %get-tuple-element.6), channel_id=1, source_target_pairs={{32,0},{64,32},{96,64},{128,96},{160,128},{192,160},{224,192},{256... | collective-permute-start | bytes 393224 | tf_op jit(solution)/shard_map/ppermute | solution.py:26
  8.8 23.1 %collective-permute-start.2 = (bf16[1,4,128,128]{3,2,1,0:T(8,128)(2,1)S(1)}, bf16[1,4,128,128]{3,2,1,0:T(8,128)(2,1)S(1)}, u32[]{:S(2)}, u32[]{:S(2)}) collective-permute-start(bf16[1,4,128,128]{3,2,1,0:T(8,128)(2,1)S(1)} %get-tuple-element.5), channel_id=1, source_target_pairs={{0,4},{4,8},{8,12},{12,16},{16,20},{20,24},{24,28},{1,5},{5,9},{9,... | collective-permute-start | bytes 393224 | tf_op jit(solution)/shard_map/ppermute | solution.py:25
  12.9 19.1 %collective-permute-start.3 = (bf16[1,4,128,128]{3,2,1,0:T(8,128)(2,1)S(1)}, bf16[1,4,128,128]{3,2,1,0:T(8,128)(2,1)S(1)}, u32[]{:S(2)}, u32[]{:S(2)}) collective-permute-start(bf16[1,4,128,128]{3,2,1,0:T(8,128)(2,1)S(1)} %get-tuple-element.4), channel_id=1, source_target_pairs={{4,0},{8,4},{12,8},{16,12},{20,16},{24,20},{28,24},{5,1},{9,5},{13... | collective-permute-start | bytes 393224 | tf_op jit(solution)/shard_map/ppermute | solution.py:26
  16.2 15.8 %collective-permute-start.4 = (bf16[1,4,128,128]{3,2,1,0:T(8,128)(2,1)S(1)}, bf16[1,4,128,128]{3,2,1,0:T(8,128)(2,1)S(1)}, u32[]{:S(2)}, u32[]{:S(2)}) collective-permute-start(bf16[1,4,128,128]{3,2,1,0:T(8,128)(2,1)S(1)} %get-tuple-element.3), channel_id=1, source_target_pairs={{0,1},{1,2},{2,3},{4,5},{5,6},{6,7},{8,9},{9,10},{10,11},{12,13},{... | collective-permute-start | bytes 393224 | tf_op jit(solution)/shard_map/ppermute | solution.py:25
  30.6 10.2 %collective-permute-start.5 = (bf16[1,4,128,128]{3,2,1,0:T(8,128)(2,1)S(1)}, bf16[1,4,128,128]{3,2,1,0:T(8,128)(2,1)S(1)}, u32[]{:S(2)}, u32[]{:S(2)}) collective-permute-start(bf16[1,4,128,128]{3,2,1,0:T(8,128)(2,1)S(1)} %get-tuple-element.2), channel_id=1, source_target_pairs={{1,0},{2,1},{3,2},{5,4},{6,5},{7,6},{9,8},{10,9},{11,10},{13,12},{... | collective-permute-start | bytes 393224 | tf_op jit(solution)/shard_map/ppermute | solution.py:26
  40.8 0.9 copy-start
  74.9 31.5 %copy-start.2 = (bf16[27,128,128]{2,1,0:T(8,128)(2,1)S(1)}, bf16[27,128,128]{2,1,0:T(8,128)(2,1)}, u32[]{:S(2)}) copy-start(bf16[27,128,128]{2,1,0:T(8,128)(2,1)} %param.10) | copy-start | bytes 2654212
  85.6 34.7 %all-to-all-start.2 = ((f32[16,1,864]{2,1,0:T(1,128)}), f32[16,1,864]{2,1,0:T(1,128)S(1)}, u32[]{:S(2)}, u32[]{:S(2)}) async-start(f32[16,1,864]{2,1,0:T(1,128)} %all_to_all.26), calls=%async_computation.2 | async-start | bytes 114688 | tf_op jit(solution)/shard_map/all_to_all | solution.py:157
  120.4 5.6 %copy-start.3 = (f32[864]{0:T(1024)}, f32[864]{0:T(1024)S(1)}, u32[]{:S(2)}) copy-start(f32[864]{0:T(1024)S(1)} %reduce_sum.29.after_ref) | copy-start | bytes 10372
  122.5 17.2 %all-to-all-start.3 = ((bf16[16,2,432]{2,1,0:T(2,128)(2,1)}), bf16[16,2,432]{2,1,0:T(2,128)(2,1)S(1)}, u32[]{:S(2)}, u32[]{:S(2)}) async-start(bf16[16,2,432]{2,1,0:T(2,128)(2,1)} %reshape.92), calls=%async_computation.3 | async-start | bytes 65536 | tf_op jit(solution)/shard_map/all_to_all | solution.py:163

commit v7 on v6

--- a/solution.py
+++ b/solution.py
@@ -12,7 +12,7 @@
 NB = 32
 PI = 288
 PB = 32
-UNROLL = 8
+UNROLL = 16
 
 
 def extended(shard, sides, width):

time: 175 us -> 175 us (level)
  waiting for transfers between devices: 24.9 us -> 21.5 us
  blocking collectives: 69.6 us -> 71.5 us
    ppermute x3, waiting for transfers between devices: 8.73 us -> 5.83 us  [extended(): after = lax.ppermute(initial, axis, down)]
  transfers between devices with their start and end apart: 8 -> 8, of which waited for: 3 -> 3; matrix products, arithmetic and copies ran while one was open for 3% -> 3% of each run, Pallas kernels for 10% -> 11%
where the time goes in v7:
time: 175 us; the launch traced here: 174 us
  blocking collectives  71.5 us (41%)
  starting transfers between devices  40.6 us (23%)
  Pallas kernels  23.5 us (13%)
  waiting for transfers between devices  21.5 us (12%)
  local copies, waits for them, and re-layouts  11.5 us (7%)
  other arithmetic  3.19 us (2%)
  between operations  2.22 us (1%)
    all_to_all x2, blocking collectives, reduce_weights(): parts = lax.all_to_all(flat.reshape(n, -1), axis, 0, 0, tiled=True)  38.5 us
    all_gather x1, blocking collectives, reduce_weights(): piece = lax.all_gather(piece, 'gy', tiled=True)  21.3 us
    all_to_all x1, starting transfers between devices, reduce_weights(): parts = lax.all_to_all(flat.reshape(n, -1), axis, 0, 0, tiled=True)  21.1 us
    all_to_all x1, waiting for transfers between devices, reduce_weights(): parts = lax.all_to_all(flat.reshape(n, -1), axis, 0, 0, tiled=True)  12.3 us
    all_gather x1, blocking collectives, reduce_weights(): piece = lax.all_gather(piece, 'gz', tiled=True)  11.6 us
    pallas_call x1, Pallas kernels, run_inputs(): pl.pallas_call(input_kernel, out_shape=jax.ShapeDtypeStruct((NB, BLOCK, C...  10.2 us
    ppermute x3, starting transfers between devices, extended(): before = lax.ppermute(last, axis, up)  10.1 us
    pallas_call x1, Pallas kernels, run_inner_weights(): pl.pallas_call(inner_weight_kernel, out_shape=jax.ShapeDtypeStruct((27, C...  8.9 us
  transfers between devices with their start and end apart: 8, of which 3 were waited for; matrix products, arithmetic and copies ran while one was open for 3% of the time, Pallas kernels for 11%

profile of v7, /device:TPU:1, one launch (start us, length us, event | category | flops | bytes accessed | tf_op | source)
XLA Modules:
  0.0 173.9 jit_solution(5579802978042053283)
XLA Ops:
  0.6 0.0 copy-start.1
  0.6 0.9 reshape_squeeze.10
  1.5 1.9 %gather_fusion = bf16[24,128,128]{2,1,0:T(8,128)(2,1)S(1)} fusion(bf16[32,128,128]{2,1,0:T(8,128)(2,1)} %bitcast.49, s32[1024]{0:T(1024)S(1)} %pad_clamp_fusion), kind=kCustom, calls=%fused_computation | custom fusion | bytes 1572960 | tf_op jit(solution)/shard_map/gather | solution.py:32
  3.4 0.0 copy-start.4
  3.5 0.0 copy-start.5
  3.5 0.1 slice_bitcast_fusion
  3.5 4.0 %collective-permute-start = (bf16[1,4,128,128]{3,2,1,0:T(8,128)(2,1)S(1)}, bf16[1,4,128,128]{3,2,1,0:T(8,128)(2,1)S(1)}, u32[]{:S(2)}, u32[]{:S(2)}) collective-permute-start(bf16[1,4,128,128]{3,2,1,0:T(8,128)(2,1)S(1)} %get-tuple-element.7), channel_id=1, source_target_pairs={{0,32},{32,64},{64,96},{96,128},{128,160},{160,192},{192,224},{224... | collective-permute-start | bytes 393224 | tf_op jit(solution)/shard_map/ppermute | solution.py:25
  7.5 1.3 collective-permute-start.1
  8.8 4.0 %collective-permute-start.2 = (bf16[1,4,128,128]{3,2,1,0:T(8,128)(2,1)S(1)}, bf16[1,4,128,128]{3,2,1,0:T(8,128)(2,1)S(1)}, u32[]{:S(2)}, u32[]{:S(2)}) collective-permute-start(bf16[1,4,128,128]{3,2,1,0:T(8,128)(2,1)S(1)} %get-tuple-element.5), channel_id=1, source_target_pairs={{0,4},{4,8},{8,12},{12,16},{16,20},{20,24},{24,28},{1,5},{5,9},{9,... | collective-permute-start | bytes 393224 | tf_op jit(solution)/shard_map/ppermute | solution.py:25
  12.9 3.4 %collective-permute-start.3 = (bf16[1,4,128,128]{3,2,1,0:T(8,128)(2,1)S(1)}, bf16[1,4,128,128]{3,2,1,0:T(8,128)(2,1)S(1)}, u32[]{:S(2)}, u32[]{:S(2)}) collective-permute-start(bf16[1,4,128,128]{3,2,1,0:T(8,128)(2,1)S(1)} %get-tuple-element.4), channel_id=1, source_target_pairs={{4,0},{8,4},{12,8},{16,12},{20,16},{24,20},{28,24},{5,1},{9,5},{13... | collective-permute-start | bytes 393224 | tf_op jit(solution)/shard_map/ppermute | solution.py:26
  16.2 2.1 %collective-permute-start.4 = (bf16[1,4,128,128]{3,2,1,0:T(8,128)(2,1)S(1)}, bf16[1,4,128,128]{3,2,1,0:T(8,128)(2,1)S(1)}, u32[]{:S(2)}, u32[]{:S(2)}) collective-permute-start(bf16[1,4,128,128]{3,2,1,0:T(8,128)(2,1)S(1)} %get-tuple-element.3), channel_id=1, source_target_pairs={{0,1},{1,2},{2,3},{4,5},{5,6},{6,7},{8,9},{9,10},{10,11},{12,13},{... | collective-permute-start | bytes 393224 | tf_op jit(solution)/shard_map/ppermute | solution.py:25
  18.3 0.0 copy-done.1
  18.4 1.3 copy.34
  19.7 0.0 copy-done.4
  19.7 0.8 copy.32
  21.1 0.0 copy-done.5
  21.1 0.7 copy.40
  22.5 8.9 %inner_weight_pairs.1.w_start = f32[27,128,128]{2,1,0:T(8,128)} custom-call(s32[288,3]{1,0:T(8,128)} %bitcast.52, s32[1]{0:T(128)} %bitcast.38.live_ref, bf16[32,128,128]{2,1,0:T(8,128)(2,1)} %bitcast.50, bf16[32,128,128]{2,1,0:T(8,128)(2,1)} %bitcast.43), custom_call_target="tpu_custom_call" | custom-call | flops 1207959552 | bytes 6291456 | tf_op jit(solution)/shard_map/inner_weight_pairs/pallas_call | solution.py:119
  31.4 0.0 collective-permute-done
  31.4 1.3 collective-permute-start.5
  32.7 0.0 collective-permute-done.1
  32.7 0.0 collective-permute-done.2
  32.8 0.0 collective-permute-done.3
  32.8 0.0 collective-permute-done.4
  32.8 5.8 %collective-permute-done.5 = bf16[1,4,128,128]{3,2,1,0:T(8,128)(2,1)S(1)} collective-permute-done((bf16[1,4,128,128]{3,2,1,0:T(8,128)(2,1)S(1)}, bf16[1,4,128,128]{3,2,1,0:T(8,128)(2,1)S(1)}, u32[]{:S(2)}, u32[]{:S(2)}) %collective-permute-start.5) | collective-permute-done | bytes 131104 | tf_op jit(solution)/shard_map/ppermute | solution.py:26
  38.7 0.9 copy-done
  39.5 4.4 %outer_weight_pairs.1 = f32[27,128,128]{2,1,0:T(8,128)} custom-call(s32[32,3]{1,0:T(8,128)} %bitcast.54, s32[1]{0:T(128)} %bitcast.40.live_ref, bf16[24,128,128]{2,1,0:T(8,128)(2,1)} %copy-done, bf16[32,128,128]{2,1,0:T(8,128)(2,1)} %bitcast.44, f32[27,128,128]{2,1,0:T(8,128)} %inner_weight_pairs.1.w_start), custom_call_target="tpu_custom_call", output_to_operand_aliasing={{}: (4, {})} | custom-call | flops 134217728 | bytes 6291456 | tf_op jit(solution)/shard_map/outer_weight_pairs/pallas_call | solution.py:130
  43.9 29.7 %all_to_all.33 = f32[8,1,55296]{2,1,0:T(1,128)S(1)} all-to-all(f32[8,1,55296]{2,1,0:T(1,128)} %bitcast.42), channel_id=1, replica_groups=mesh['gx'=16,'gy'=8,'gz'=4] {'gy'}, dimensions={0} | all-to-all | bytes 3538944 | tf_op jit(solution)/shard_map/all_to_all | solution.py:157
  73.6 1.3 reduce_sum.27
  74.9 8.9 %all_to_all.34 = f32[4,1,13824]{2,1,0:T(1,128)S(1)} all-to-all(f32[4,1,13824]{2,1,0:T(1,128)S(1)} %bitcast.47), channel_id=1, replica_groups=mesh['gx'=16,'gy'=8,'gz'=4] {'gz'}, dimensions={0} | all-to-all | bytes 442368 | tf_op jit(solution)/shard_map/all_to_all | solution.py:157
  83.7 0.2 reduce_sum.28
  83.9 0.7 all_to_all.26
  84.7 21.1 %all-to-all-start.2 = ((f32[16,1,864]{2,1,0:T(1,128)}), f32[16,1,864]{2,1,0:T(1,128)S(1)}, u32[]{:S(2)}, u32[]{:S(2)}) async-start(f32[16,1,864]{2,1,0:T(1,128)} %all_to_all.26), calls=%async_computation.2 | async-start | bytes 114688 | tf_op jit(solution)/shard_map/all_to_all | solution.py:157
  105.8 1.6 copy.33
  107.4 12.3 %all-to-all-done.2 = f32[16,1,864]{2,1,0:T(1,128)S(1)} async-done(((f32[16,1,864]{2,1,0:T(1,128)}), f32[16,1,864]{2,1,0:T(1,128)S(1)}, u32[]{:S(2)}, u32[]{:S(2)}) %all-to-all-start.2) | async-done | bytes 55328 | tf_op jit(solution)/shard_map/all_to_all | solution.py:157
  119.8 0.5 broadcast.38
  120.3 0.8 reduce.5
  121.1 0.7 reshape.92
  121.8 3.5 %all-to-all-start.3 = ((bf16[16,2,432]{2,1,0:T(2,128)(2,1)}), bf16[16,2,432]{2,1,0:T(2,128)(2,1)S(1)}, u32[]{:S(2)}, u32[]{:S(2)}) async-start(bf16[16,2,432]{2,1,0:T(2,128)(2,1)} %reshape.92), calls=%async_computation.3 | async-start | bytes 65536 | tf_op jit(solution)/shard_map/all_to_all | solution.py:163
  125.3 10.2 %input_pairs.1 = bf16[32,128,128]{2,1,0:T(8,128)(2,1)} custom-call(s32[288,3]{1,0:T(8,128)} %bitcast.53, s32[1]{0:T(128)} %bitcast.39.inner_live_ref, s32[32,3]{1,0:T(8,128)} %bitcast.55, s32[1]{0:T(128)} %bitcast.41.outer_live_ref, bf16[32,128,128]{2,1,0:T(8,128)(2,1)} %bitcast.51, bf16[24,128,128]{2,1,0:T(8,128)(2,1)} %copy-done, ...), custom_call_target="tpu_custom_call" | custom-call | flops 1342177280 | bytes 6291456 | tf_op jit(solution)/shard_map/input_pairs/pallas_call | solution.py:142
  135.5 3.4 %all-to-all-done.3 = bf16[16,2,432]{2,1,0:T(2,128)(2,1)S(1)} async-done(((bf16[16,2,432]{2,1,0:T(2,128)(2,1)}), bf16[16,2,432]{2,1,0:T(2,128)(2,1)S(1)}, u32[]{:S(2)}, u32[]{:S(2)}) %all-to-all-start.3) | async-done | bytes 27680 | tf_op jit(solution)/shard_map/all_to_all | solution.py:163
  139.0 0.1 reshape.93
  139.1 0.2 reduce.3
  139.2 0.1 reshape.87
  139.4 11.6 %all-gather = bf16[4,1,13824]{2,1,0:T(2,128)(2,1)S(1)} all-gather(bf16[1,1,13824]{2,1,0:T(2,128)(2,1)S(1)} %reshape.87), channel_id=1, replica_groups=mesh['gx'=16,'gy'=8,'gz'=4] {'gz'}, dimensions={0}, use_global_device_ids=true | all-gather | bytes 138240 | tf_op jit(solution)/shard_map/all_gather | solution.py:164
  151.0 0.7 reduce.4
  151.7 21.3 %all_gather.7 = bf16[442368]{0:T(1024)(128)(2,1)S(1)} all-gather(bf16[55296]{0:T(1024)(128)(2,1)S(1)} %reshape.88), channel_id=1, replica_groups=mesh['gx'=16,'gy'=8,'gz'=4] {'gy'}, dimensions={0}, use_global_device_ids=true | all-gather | bytes 995328 | tf_op jit(solution)/shard_map/all_gather | solution.py:165
  173.0 0.9 copy.52
  (17 shorter events, 0.3 us)
Async XLA Ops:
  0.6 17.7 %copy-start.1 = (bf16[1,1,1,4096,128]{4,3,2,1,0:T(8,128)(2,1)S(1)}, bf16[1,1,1,4096,128]{4,3,2,1,0:T(8,128)(2,1)}, u32[]{:S(2)}) copy-start(bf16[1,1,1,4096,128]{4,3,2,1,0:T(8,128)(2,1)} %param.8) | copy-start | bytes 3145732
  3.4 16.2 %copy-start.4 = (s32[1,1,1,288,3]{3,2,4,1,0:T(1,128)S(1)}, s32[1,1,1,288,3]{3,2,4,1,0:T(1,128)}, u32[]{:S(2)}) copy-start(s32[1,1,1,288,3]{3,2,4,1,0:T(1,128)} %param.11) | copy-start | bytes 10372
  3.5 17.7 %copy-start.5 = (s32[1,1,1,32,3]{3,2,4,1,0:T(1,128)S(1)}, s32[1,1,1,32,3]{3,2,4,1,0:T(1,128)}, u32[]{:S(2)}) copy-start(s32[1,1,1,32,3]{3,2,4,1,0:T(1,128)} %param.12) | copy-start | bytes 1156
  3.5 27.8 %collective-permute-start = (bf16[1,4,128,128]{3,2,1,0:T(8,128)(2,1)S(1)}, bf16[1,4,128,128]{3,2,1,0:T(8,128)(2,1)S(1)}, u32[]{:S(2)}, u32[]{:S(2)}) collective-permute-start(bf16[1,4,128,128]{3,2,1,0:T(8,128)(2,1)S(1)} %get-tuple-element.7), channel_id=1, source_target_pairs={{0,32},{32,64},{64,96},{96,128},{128,160},{160,192},{192,224},{224... | collective-permute-start | bytes 393224 | tf_op jit(solution)/shard_map/ppermute | solution.py:25
  7.5 25.2 %collective-permute-start.1 = (bf16[1,4,128,128]{3,2,1,0:T(8,128)(2,1)S(1)}, bf16[1,4,128,128]{3,2,1,0:T(8,128)(2,1)S(1)}, u32[]{:S(2)}, u32[]{:S(2)}) collective-permute-start(bf16[1,4,128,128]{3,2,1,0:T(8,128)(2,1)S(1)} %get-tuple-element.6), channel_id=1, source_target_pairs={{32,0},{64,32},{96,64},{128,96},{160,128},{192,160},{224,192},{256... | collective-permute-start | bytes 393224 | tf_op jit(solution)/shard_map/ppermute | solution.py:26
  8.8 23.9 %collective-permute-start.2 = (bf16[1,4,128,128]{3,2,1,0:T(8,128)(2,1)S(1)}, bf16[1,4,128,128]{3,2,1,0:T(8,128)(2,1)S(1)}, u32[]{:S(2)}, u32[]{:S(2)}) collective-permute-start(bf16[1,4,128,128]{3,2,1,0:T(8,128)(2,1)S(1)} %get-tuple-element.5), channel_id=1, source_target_pairs={{0,4},{4,8},{8,12},{12,16},{16,20},{20,24},{24,28},{1,5},{5,9},{9,... | collective-permute-start | bytes 393224 | tf_op jit(solution)/shard_map/ppermute | solution.py:25
  12.9 19.9 %collective-permute-start.3 = (bf16[1,4,128,128]{3,2,1,0:T(8,128)(2,1)S(1)}, bf16[1,4,128,128]{3,2,1,0:T(8,128)(2,1)S(1)}, u32[]{:S(2)}, u32[]{:S(2)}) collective-permute-start(bf16[1,4,128,128]{3,2,1,0:T(8,128)(2,1)S(1)} %get-tuple-element.4), channel_id=1, source_target_pairs={{4,0},{8,4},{12,8},{16,12},{20,16},{24,20},{28,24},{5,1},{9,5},{13... | collective-permute-start | bytes 393224 | tf_op jit(solution)/shard_map/ppermute | solution.py:26
  16.2 16.5 %collective-permute-start.4 = (bf16[1,4,128,128]{3,2,1,0:T(8,128)(2,1)S(1)}, bf16[1,4,128,128]{3,2,1,0:T(8,128)(2,1)S(1)}, u32[]{:S(2)}, u32[]{:S(2)}) collective-permute-start(bf16[1,4,128,128]{3,2,1,0:T(8,128)(2,1)S(1)} %get-tuple-element.3), channel_id=1, source_target_pairs={{0,1},{1,2},{2,3},{4,5},{5,6},{6,7},{8,9},{9,10},{10,11},{12,13},{... | collective-permute-start | bytes 393224 | tf_op jit(solution)/shard_map/ppermute | solution.py:25
  31.4 7.3 %collective-permute-start.5 = (bf16[1,4,128,128]{3,2,1,0:T(8,128)(2,1)S(1)}, bf16[1,4,128,128]{3,2,1,0:T(8,128)(2,1)S(1)}, u32[]{:S(2)}, u32[]{:S(2)}) collective-permute-start(bf16[1,4,128,128]{3,2,1,0:T(8,128)(2,1)S(1)} %get-tuple-element.2), channel_id=1, source_target_pairs={{1,0},{2,1},{3,2},{5,4},{6,5},{7,6},{9,8},{10,9},{11,10},{13,12},{... | collective-permute-start | bytes 393224 | tf_op jit(solution)/shard_map/ppermute | solution.py:26
  38.7 0.9 copy-start
  73.6 32.2 %copy-start.2 = (bf16[27,128,128]{2,1,0:T(8,128)(2,1)S(1)}, bf16[27,128,128]{2,1,0:T(8,128)(2,1)}, u32[]{:S(2)}) copy-start(bf16[27,128,128]{2,1,0:T(8,128)(2,1)} %param.10) | copy-start | bytes 2654212
  84.7 35.0 %all-to-all-start.2 = ((f32[16,1,864]{2,1,0:T(1,128)}), f32[16,1,864]{2,1,0:T(1,128)S(1)}, u32[]{:S(2)}, u32[]{:S(2)}) async-start(f32[16,1,864]{2,1,0:T(1,128)} %all_to_all.26), calls=%async_computation.2 | async-start | bytes 114688 | tf_op jit(solution)/shard_map/all_to_all | solution.py:157
  119.7 5.6 %copy-start.3 = (f32[864]{0:T(1024)}, f32[864]{0:T(1024)S(1)}, u32[]{:S(2)}) copy-start(f32[864]{0:T(1024)S(1)} %reduce_sum.29.after_ref) | copy-start | bytes 10372
  121.8 17.1 %all-to-all-start.3 = ((bf16[16,2,432]{2,1,0:T(2,128)(2,1)}), bf16[16,2,432]{2,1,0:T(2,128)(2,1)S(1)}, u32[]{:S(2)}, u32[]{:S(2)}) async-start(bf16[16,2,432]{2,1,0:T(2,128)(2,1)} %reshape.92), calls=%async_computation.3 | async-start | bytes 65536 | tf_op jit(solution)/shard_map/all_to_all | solution.py:163

commit v8 on v7

--- a/solution.py
+++ b/solution.py
@@ -83,14 +83,11 @@
     return update
 
 
-def inner_weight_kernel(pairs_ref, live_ref, table_ref, ft_ref, acc_w):
+def weight_kernel(inner_ref, inner_live_ref, outer_ref, outer_live_ref, local_ref, received_ref, ft_ref, acc_w):
     acc_w[...] = jnp.zeros_like(acc_w)
-    pair_loop(pairs_ref, live_ref, table_ref, 0, weight_updater(ft_ref, acc_w))
-
-
-def outer_weight_kernel(pairs_ref, live_ref, table_ref, ft_ref, w_start, acc_w):
-    acc_w[...] = w_start[...]
-    pair_loop(pairs_ref, live_ref, table_ref, NB, weight_updater(ft_ref, acc_w))
+    update = weight_updater(ft_ref, acc_w)
+    pair_loop(inner_ref, inner_live_ref, local_ref, 0, update)
+    pair_loop(outer_ref, outer_live_ref, received_ref, NB, update)
 
 
 def input_kernel(inner_ref, inner_live_ref, outer_ref, outer_live_ref, local_ref, received_ref, kt_ref, after_ref, grad_out, acc_in):
@@ -115,27 +112,15 @@
     )
 
 
-def run_inner_weights(pairs, live, table, ft):
+def run_weights(inner_pairs, inner_n, outer_pairs, outer_n, local, received, ft):
     return pl.pallas_call(
-        inner_weight_kernel,
+        weight_kernel,
         out_shape=jax.ShapeDtypeStruct((27, C, C), jnp.float32),
-        in_specs=[smem(), smem(), vmem(), vmem()],
+        in_specs=[smem(), smem(), smem(), smem(), vmem(), vmem(), vmem()],
         out_specs=vmem(),
-        cost_estimate=cost(PI),
-        name="inner_weight_pairs",
-    )(pairs, live, table, ft)
-
-
-def run_outer_weights(pairs, live, table, ft, acc_w):
-    return pl.pallas_call(
-        outer_weight_kernel,
-        out_shape=jax.ShapeDtypeStruct((27, C, C), jnp.float32),
-        in_specs=[smem(), smem(), vmem(), vmem(), vmem()],
-        out_specs=vmem(),
-        input_output_aliases={4: 0},
-        cost_estimate=cost(PB),
-        name="outer_weight_pairs",
-    )(pairs, live, table, ft, acc_w)
+        cost_estimate=cost(PI + PB),
+        name="weight_pairs",
+    )(inner_pairs, inner_n, outer_pairs, outer_n, local, received, ft)
 
 
 def run_inputs(inner_pairs, inner_n, outer_pairs, outer_n, local, received, kt, after):
@@ -175,8 +160,7 @@
     inner_n = inner_live[0, 0]
     outer_n = outer_live[0, 0]
     received = received_blocks(local_grads, face_blocks[0, 0, 0])
-    acc_w = run_inner_weights(inner_pairs, inner_n, local_grads, feats_t)
-    acc_w = run_outer_weights(outer_pairs, outer_n, received, feats_t, acc_w)
+    acc_w = run_weights(inner_pairs, inner_n, outer_pairs, outer_n, local_grads, received, feats_t)
     bricks_all = lax.axis_size("gx") * lax.axis_size("gy") * lax.axis_size("gz")
     grad_scale = math.sqrt(27.0 / (bricks_all * PI * BLOCK))
     weight_grad, after = reduce_weights(acc_w, grad_scale)

time: 175 us -> 171 us (0.977)
  blocking collectives: 71.5 us -> 79.9 us
  starting transfers between devices: 40.6 us -> 33.4 us
  Pallas kernels: 23.5 us -> 18.3 us
    all_to_all x2, blocking collectives: 38.5 us -> 47.2 us  [reduce_weights(): parts = lax.all_to_all(flat.reshape(n, -1), axis, 0, 0, tiled=True)]
    all_to_all x1, starting transfers between devices: 21.1 us -> 13.9 us  [reduce_weights(): parts = lax.all_to_all(flat.reshape(n, -1), axis, 0, 0, tiled=True)]
    pallas_call x2 -> x1, Pallas kernels: 13.3 us -> 9.18 us  [run_weights(): pl.pallas_call(weight_kernel, out_shape=jax.ShapeDtypeStruct((27, C, C),...]
  transfers between devices with their start and end apart: 8 -> 8, of which waited for: 3 -> 3; matrix products, arithmetic and copies ran while one was open for 3% -> 3% of each run, Pallas kernels for 11% -> 5%
where the time goes in v8:
time: 171 us; the launch traced here: 170 us
  blocking collectives  79.9 us (47%)
  starting transfers between devices  33.4 us (20%)
  waiting for transfers between devices  21.6 us (13%)
  Pallas kernels  18.3 us (11%)
  local copies, waits for them, and re-layouts  11.4 us (7%)
  other arithmetic  3.19 us (2%)
  between operations  2.21 us (1%)
    all_to_all x2, blocking collectives, reduce_weights(): parts = lax.all_to_all(flat.reshape(n, -1), axis, 0, 0, tiled=True)  47.2 us
    all_gather x1, blocking collectives, reduce_weights(): piece = lax.all_gather(piece, 'gy', tiled=True)  21.5 us
    all_to_all x1, starting transfers between devices, reduce_weights(): parts = lax.all_to_all(flat.reshape(n, -1), axis, 0, 0, tiled=True)  13.9 us
    all_to_all x1, waiting for transfers between devices, reduce_weights(): parts = lax.all_to_all(flat.reshape(n, -1), axis, 0, 0, tiled=True)  12.3 us
    all_gather x1, blocking collectives, reduce_weights(): piece = lax.all_gather(piece, 'gz', tiled=True)  11.2 us
    ppermute x3, starting transfers between devices, extended(): before = lax.ppermute(last, axis, up)  10.1 us
    pallas_call x1, Pallas kernels, run_weights(): pl.pallas_call(weight_kernel, out_shape=jax.ShapeDtypeStruct((27, C, C),...  9.18 us
    pallas_call x1, Pallas kernels, run_inputs(): pl.pallas_call(input_kernel, out_shape=jax.ShapeDtypeStruct((NB, BLOCK, C...  9.08 us
  transfers between devices with their start and end apart: 8, of which 3 were waited for; matrix products, arithmetic and copies ran while one was open for 3% of the time, Pallas kernels for 5%

profile of v8, /device:TPU:1, one launch (start us, length us, event | category | flops | bytes accessed | tf_op | source)
XLA Modules:
  0.0 170.0 jit_solution(5339591636242444120)
XLA Ops:
  0.6 0.0 copy-start.4
  0.6 0.0 copy-start.5
  0.7 0.0 copy-start
  0.7 0.9 reshape_squeeze.10
  1.5 1.9 %gather_fusion = bf16[24,128,128]{2,1,0:T(8,128)(2,1)S(1)} fusion(bf16[32,128,128]{2,1,0:T(8,128)(2,1)} %bitcast.48, s32[1024]{0:T(1024)S(1)} %pad_clamp_fusion), kind=kCustom, calls=%fused_computation | custom fusion | bytes 1572960 | tf_op jit(solution)/shard_map/gather | solution.py:32
  3.5 0.1 slice_bitcast_fusion
  3.5 4.0 %collective-permute-start = (bf16[1,4,128,128]{3,2,1,0:T(8,128)(2,1)S(1)}, bf16[1,4,128,128]{3,2,1,0:T(8,128)(2,1)S(1)}, u32[]{:S(2)}, u32[]{:S(2)}) collective-permute-start(bf16[1,4,128,128]{3,2,1,0:T(8,128)(2,1)S(1)} %get-tuple-element.7), channel_id=1, source_target_pairs={{0,32},{32,64},{64,96},{96,128},{128,160},{160,192},{192,224},{224... | collective-permute-start | bytes 393224 | tf_op jit(solution)/shard_map/ppermute | solution.py:25
  7.5 1.3 collective-permute-start.1
  8.8 4.0 %collective-permute-start.2 = (bf16[1,4,128,128]{3,2,1,0:T(8,128)(2,1)S(1)}, bf16[1,4,128,128]{3,2,1,0:T(8,128)(2,1)S(1)}, u32[]{:S(2)}, u32[]{:S(2)}) collective-permute-start(bf16[1,4,128,128]{3,2,1,0:T(8,128)(2,1)S(1)} %get-tuple-element.5), channel_id=1, source_target_pairs={{0,4},{4,8},{8,12},{12,16},{16,20},{20,24},{24,28},{1,5},{5,9},{9,... | collective-permute-start | bytes 393224 | tf_op jit(solution)/shard_map/ppermute | solution.py:25
  12.9 3.4 %collective-permute-start.3 = (bf16[1,4,128,128]{3,2,1,0:T(8,128)(2,1)S(1)}, bf16[1,4,128,128]{3,2,1,0:T(8,128)(2,1)S(1)}, u32[]{:S(2)}, u32[]{:S(2)}) collective-permute-start(bf16[1,4,128,128]{3,2,1,0:T(8,128)(2,1)S(1)} %get-tuple-element.4), channel_id=1, source_target_pairs={{4,0},{8,4},{12,8},{16,12},{20,16},{24,20},{28,24},{5,1},{9,5},{13... | collective-permute-start | bytes 393224 | tf_op jit(solution)/shard_map/ppermute | solution.py:26
  16.2 2.1 %collective-permute-start.4 = (bf16[1,4,128,128]{3,2,1,0:T(8,128)(2,1)S(1)}, bf16[1,4,128,128]{3,2,1,0:T(8,128)(2,1)S(1)}, u32[]{:S(2)}, u32[]{:S(2)}) collective-permute-start(bf16[1,4,128,128]{3,2,1,0:T(8,128)(2,1)S(1)} %get-tuple-element.3), channel_id=1, source_target_pairs={{0,1},{1,2},{2,3},{4,5},{5,6},{6,7},{8,9},{9,10},{10,11},{12,13},{... | collective-permute-start | bytes 393224 | tf_op jit(solution)/shard_map/ppermute | solution.py:25
  18.3 0.0 copy-done.4
  18.3 0.8 copy.31
  19.1 0.0 copy-done.5
  19.2 0.7 copy.39
  21.1 0.0 copy-done
  21.1 1.3 copy.33
  22.5 0.0 collective-permute-done
  22.5 1.3 collective-permute-start.5
  23.8 0.0 collective-permute-done.1
  23.8 0.0 collective-permute-done.2
  23.8 0.0 collective-permute-done.3
  23.9 0.0 collective-permute-done.4
  23.9 4.7 %collective-permute-done.5 = bf16[1,4,128,128]{3,2,1,0:T(8,128)(2,1)S(1)} collective-permute-done((bf16[1,4,128,128]{3,2,1,0:T(8,128)(2,1)S(1)}, bf16[1,4,128,128]{3,2,1,0:T(8,128)(2,1)S(1)}, u32[]{:S(2)}, u32[]{:S(2)}) %collective-permute-start.5) | collective-permute-done | bytes 131104 | tf_op jit(solution)/shard_map/ppermute | solution.py:26
  28.6 0.0 copy-start.2
  28.7 0.9 copy-done.2
  29.5 9.2 %weight_pairs.1 = f32[27,128,128]{2,1,0:T(8,128)} custom-call(s32[288,3]{1,0:T(8,128)} %bitcast.51, s32[1]{0:T(128)} %bitcast.38.inner_live_ref, s32[32,3]{1,0:T(8,128)} %bitcast.53, s32[1]{0:T(128)} %bitcast.40.outer_live_ref, bf16[32,128,128]{2,1,0:T(8,128)(2,1)} %bitcast.49, bf16[24,128,128]{2,1,0:T(8,128)(2,1)} %copy-done.2, bf16[32,128,128]{2,1,0:T(8,128)(2,1)} %bitcast.45), custom_call_target="tpu_custom_call" | custom-call | flops 1342177280 | bytes 6291456 | tf_op jit(solution)/shard_map/weight_pairs/pallas_call | solution.py:116
  38.7 31.6 %all_to_all.33 = f32[8,1,55296]{2,1,0:T(1,128)S(1)} all-to-all(f32[8,1,55296]{2,1,0:T(1,128)} %bitcast.43), channel_id=1, replica_groups=mesh['gx'=16,'gy'=8,'gz'=4] {'gy'}, dimensions={0} | all-to-all | bytes 3538944 | tf_op jit(solution)/shard_map/all_to_all | solution.py:142
  70.3 1.3 reduce_sum.27
  71.5 15.6 %all_to_all.34 = f32[4,1,13824]{2,1,0:T(1,128)S(1)} all-to-all(f32[4,1,13824]{2,1,0:T(1,128)S(1)} %bitcast.46), channel_id=1, replica_groups=mesh['gx'=16,'gy'=8,'gz'=4] {'gz'}, dimensions={0} | all-to-all | bytes 442368 | tf_op jit(solution)/shard_map/all_to_all | solution.py:142
  87.1 0.2 reduce_sum.28
  87.4 0.7 all_to_all.26
  88.1 13.9 %all-to-all-start.2 = ((f32[16,1,864]{2,1,0:T(1,128)}), f32[16,1,864]{2,1,0:T(1,128)S(1)}, u32[]{:S(2)}, u32[]{:S(2)}) async-start(f32[16,1,864]{2,1,0:T(1,128)} %all_to_all.26), calls=%async_computation.2 | async-start | bytes 114688 | tf_op jit(solution)/shard_map/all_to_all | solution.py:142
  102.0 1.6 copy.32
  103.6 12.3 %all-to-all-done.2 = f32[16,1,864]{2,1,0:T(1,128)S(1)} async-done(((f32[16,1,864]{2,1,0:T(1,128)}), f32[16,1,864]{2,1,0:T(1,128)S(1)}, u32[]{:S(2)}, u32[]{:S(2)}) %all-to-all-start.2) | async-done | bytes 55328 | tf_op jit(solution)/shard_map/all_to_all | solution.py:142
  116.0 0.5 broadcast.38
  116.5 0.8 reduce.5
  117.3 0.7 reshape.92
  118.0 3.5 %all-to-all-start.3 = ((bf16[16,2,432]{2,1,0:T(2,128)(2,1)}), bf16[16,2,432]{2,1,0:T(2,128)(2,1)S(1)}, u32[]{:S(2)}, u32[]{:S(2)}) async-start(bf16[16,2,432]{2,1,0:T(2,128)(2,1)} %reshape.92), calls=%async_computation.3 | async-start | bytes 65536 | tf_op jit(solution)/shard_map/all_to_all | solution.py:148
  121.5 9.1 %input_pairs.1 = bf16[32,128,128]{2,1,0:T(8,128)(2,1)} custom-call(s32[288,3]{1,0:T(8,128)} %bitcast.52, s32[1]{0:T(128)} %bitcast.39.inner_live_ref, s32[32,3]{1,0:T(8,128)} %bitcast.54, s32[1]{0:T(128)} %bitcast.41.outer_live_ref, bf16[32,128,128]{2,1,0:T(8,128)(2,1)} %bitcast.50, bf16[24,128,128]{2,1,0:T(8,128)(2,1)} %copy-done.2, ...), custom_call_target="tpu_custom_call" | custom-call | flops 1342177280 | bytes 6291456 | tf_op jit(solution)/shard_map/input_pairs/pallas_call | solution.py:127
  130.6 4.7 %all-to-all-done.3 = bf16[16,2,432]{2,1,0:T(2,128)(2,1)S(1)} async-done(((bf16[16,2,432]{2,1,0:T(2,128)(2,1)}), bf16[16,2,432]{2,1,0:T(2,128)(2,1)S(1)}, u32[]{:S(2)}, u32[]{:S(2)}) %all-to-all-start.3) | async-done | bytes 27680 | tf_op jit(solution)/shard_map/all_to_all | solution.py:148
  135.3 0.1 reshape.93
  135.4 0.2 reduce.3
  135.5 0.1 reshape.87
  135.7 11.2 %all-gather = bf16[4,1,13824]{2,1,0:T(2,128)(2,1)S(1)} all-gather(bf16[1,1,13824]{2,1,0:T(2,128)(2,1)S(1)} %reshape.87), channel_id=1, replica_groups=mesh['gx'=16,'gy'=8,'gz'=4] {'gz'}, dimensions={0}, use_global_device_ids=true | all-gather | bytes 138240 | tf_op jit(solution)/shard_map/all_gather | solution.py:149
  146.9 0.7 reduce.4
  147.6 21.5 %all_gather.7 = bf16[442368]{0:T(1024)(128)(2,1)S(1)} all-gather(bf16[55296]{0:T(1024)(128)(2,1)S(1)} %reshape.88), channel_id=1, replica_groups=mesh['gx'=16,'gy'=8,'gz'=4] {'gy'}, dimensions={0}, use_global_device_ids=true | all-gather | bytes 995328 | tf_op jit(solution)/shard_map/all_gather | solution.py:150
  169.1 0.9 copy.50
  (16 shorter events, 0.3 us)
Async XLA Ops:
  0.6 17.7 %copy-start.4 = (s32[1,1,1,288,3]{3,2,4,1,0:T(1,128)S(1)}, s32[1,1,1,288,3]{3,2,4,1,0:T(1,128)}, u32[]{:S(2)}) copy-start(s32[1,1,1,288,3]{3,2,4,1,0:T(1,128)} %param.11) | copy-start | bytes 10372
  0.6 18.5 %copy-start.5 = (s32[1,1,1,32,3]{3,2,4,1,0:T(1,128)S(1)}, s32[1,1,1,32,3]{3,2,4,1,0:T(1,128)}, u32[]{:S(2)}) copy-start(s32[1,1,1,32,3]{3,2,4,1,0:T(1,128)} %param.12) | copy-start | bytes 1156
  0.7 20.5 %copy-start = (bf16[1,1,1,4096,128]{4,3,2,1,0:T(8,128)(2,1)S(1)}, bf16[1,1,1,4096,128]{4,3,2,1,0:T(8,128)(2,1)}, u32[]{:S(2)}) copy-start(bf16[1,1,1,4096,128]{4,3,2,1,0:T(8,128)(2,1)} %param.8) | copy-start | bytes 3145732
  3.5 18.9 %collective-permute-start = (bf16[1,4,128,128]{3,2,1,0:T(8,128)(2,1)S(1)}, bf16[1,4,128,128]{3,2,1,0:T(8,128)(2,1)S(1)}, u32[]{:S(2)}, u32[]{:S(2)}) collective-permute-start(bf16[1,4,128,128]{3,2,1,0:T(8,128)(2,1)S(1)} %get-tuple-element.7), channel_id=1, source_target_pairs={{0,32},{32,64},{64,96},{96,128},{128,160},{160,192},{192,224},{224... | collective-permute-start | bytes 393224 | tf_op jit(solution)/shard_map/ppermute | solution.py:25
  7.5 16.3 %collective-permute-start.1 = (bf16[1,4,128,128]{3,2,1,0:T(8,128)(2,1)S(1)}, bf16[1,4,128,128]{3,2,1,0:T(8,128)(2,1)S(1)}, u32[]{:S(2)}, u32[]{:S(2)}) collective-permute-start(bf16[1,4,128,128]{3,2,1,0:T(8,128)(2,1)S(1)} %get-tuple-element.6), channel_id=1, source_target_pairs={{32,0},{64,32},{96,64},{128,96},{160,128},{192,160},{224,192},{256... | collective-permute-start | bytes 393224 | tf_op jit(solution)/shard_map/ppermute | solution.py:26
  8.8 15.0 %collective-permute-start.2 = (bf16[1,4,128,128]{3,2,1,0:T(8,128)(2,1)S(1)}, bf16[1,4,128,128]{3,2,1,0:T(8,128)(2,1)S(1)}, u32[]{:S(2)}, u32[]{:S(2)}) collective-permute-start(bf16[1,4,128,128]{3,2,1,0:T(8,128)(2,1)S(1)} %get-tuple-element.5), channel_id=1, source_target_pairs={{0,4},{4,8},{8,12},{12,16},{16,20},{20,24},{24,28},{1,5},{5,9},{9,... | collective-permute-start | bytes 393224 | tf_op jit(solution)/shard_map/ppermute | solution.py:25
  12.9 11.0 %collective-permute-start.3 = (bf16[1,4,128,128]{3,2,1,0:T(8,128)(2,1)S(1)}, bf16[1,4,128,128]{3,2,1,0:T(8,128)(2,1)S(1)}, u32[]{:S(2)}, u32[]{:S(2)}) collective-permute-start(bf16[1,4,128,128]{3,2,1,0:T(8,128)(2,1)S(1)} %get-tuple-element.4), channel_id=1, source_target_pairs={{4,0},{8,4},{12,8},{16,12},{20,16},{24,20},{28,24},{5,1},{9,5},{13... | collective-permute-start | bytes 393224 | tf_op jit(solution)/shard_map/ppermute | solution.py:26
  16.2 7.6 %collective-permute-start.4 = (bf16[1,4,128,128]{3,2,1,0:T(8,128)(2,1)S(1)}, bf16[1,4,128,128]{3,2,1,0:T(8,128)(2,1)S(1)}, u32[]{:S(2)}, u32[]{:S(2)}) collective-permute-start(bf16[1,4,128,128]{3,2,1,0:T(8,128)(2,1)S(1)} %get-tuple-element.3), channel_id=1, source_target_pairs={{0,1},{1,2},{2,3},{4,5},{5,6},{6,7},{8,9},{9,10},{10,11},{12,13},{... | collective-permute-start | bytes 393224 | tf_op jit(solution)/shard_map/ppermute | solution.py:25
  22.5 6.2 %collective-permute-start.5 = (bf16[1,4,128,128]{3,2,1,0:T(8,128)(2,1)S(1)}, bf16[1,4,128,128]{3,2,1,0:T(8,128)(2,1)S(1)}, u32[]{:S(2)}, u32[]{:S(2)}) collective-permute-start(bf16[1,4,128,128]{3,2,1,0:T(8,128)(2,1)S(1)} %get-tuple-element.2), channel_id=1, source_target_pairs={{1,0},{2,1},{3,2},{5,4},{6,5},{7,6},{9,8},{10,9},{11,10},{13,12},{... | collective-permute-start | bytes 393224 | tf_op jit(solution)/shard_map/ppermute | solution.py:26
  28.6 0.9 copy-start.2
  70.3 31.7 %copy-start.1 = (bf16[27,128,128]{2,1,0:T(8,128)(2,1)S(1)}, bf16[27,128,128]{2,1,0:T(8,128)(2,1)}, u32[]{:S(2)}) copy-start(bf16[27,128,128]{2,1,0:T(8,128)(2,1)} %param.10) | copy-start | bytes 2654212
  88.1 27.8 %all-to-all-start.2 = ((f32[16,1,864]{2,1,0:T(1,128)}), f32[16,1,864]{2,1,0:T(1,128)S(1)}, u32[]{:S(2)}, u32[]{:S(2)}) async-start(f32[16,1,864]{2,1,0:T(1,128)} %all_to_all.26), calls=%async_computation.2 | async-start | bytes 114688 | tf_op jit(solution)/shard_map/all_to_all | solution.py:142
  115.9 5.6 %copy-start.3 = (f32[864]{0:T(1024)}, f32[864]{0:T(1024)S(1)}, u32[]{:S(2)}) copy-start(f32[864]{0:T(1024)S(1)} %reduce_sum.29.after_ref) | copy-start | bytes 10372
  118.0 17.2 %all-to-all-start.3 = ((bf16[16,2,432]{2,1,0:T(2,128)(2,1)}), bf16[16,2,432]{2,1,0:T(2,128)(2,1)S(1)}, u32[]{:S(2)}, u32[]{:S(2)}) async-start(bf16[16,2,432]{2,1,0:T(2,128)(2,1)} %reshape.92), calls=%async_computation.3 | async-start | bytes 65536 | tf_op jit(solution)/shard_map/all_to_all | solution.py:148

commit v9 on v8

--- a/solution.py
+++ b/solution.py
@@ -5,6 +5,7 @@
 from jax import lax
 from jax.experimental import pallas as pl
 from jax.experimental.pallas import tpu as pltpu
+from jax.sharding import Mesh
 from jax.sharding import PartitionSpec as P
 
 C = 128
@@ -13,6 +14,9 @@
 PI = 288
 PB = 32
 UNROLL = 16
+GX = ("zh", "x")
+GY = ("y", "c")
+ZZ = ("zh", "gz")
 
 
 def extended(shard, sides, width):
@@ -30,8 +34,8 @@
 
 def received_blocks(local_grads, face_lists):
     faces = local_grads[face_lists.reshape(-1)].reshape(3, 2, 4, BLOCK, C)
-    got_x = extended(faces[0], (("gx", 0),), 1)
-    got_y = extended(faces[1], (("gy", 0),), 1)
+    got_x = extended(faces[0], ((GX, 0),), 1)
+    got_y = extended(faces[1], ((GY, 0),), 1)
     got_z = extended(faces[2], (("gz", 0),), 1)
     return jnp.concatenate(
         [got_x[0], got_x[3], got_y[0], got_y[3], got_z[0], got_z[3]], axis=0
@@ -137,17 +141,17 @@
 
 def reduce_weights(weight_acc, grad_scale):
     flat = weight_acc.reshape(-1)
-    for axis in ("gy", "gz", "gx"):
+    for axis in (GY, "x", ZZ):
         n = lax.axis_size(axis)
         parts = lax.all_to_all(flat.reshape(n, -1), axis, 0, 0, tiled=True)
         flat = parts.reshape(n, -1).sum(axis=0)
     after = flat
     piece = (flat * grad_scale).astype(jnp.bfloat16)
-    n = lax.axis_size("gx")
+    n = lax.axis_size(ZZ)
     copies = jnp.broadcast_to(piece[None], (n,) + piece.shape)
-    piece = lax.all_to_all(copies, "gx", 0, 0, tiled=True).reshape(-1)
-    piece = lax.all_gather(piece, "gz", tiled=True)
-    piece = lax.all_gather(piece, "gy", tiled=True)
+    piece = lax.all_to_all(copies, ZZ, 0, 0, tiled=True).reshape(-1)
+    piece = lax.all_gather(piece, "x", tiled=True)
+    piece = lax.all_gather(piece, GY, tiled=True)
     return piece.reshape(weight_acc.shape), after
 
 
@@ -161,7 +165,7 @@
     outer_n = outer_live[0, 0]
     received = received_blocks(local_grads, face_blocks[0, 0, 0])
     acc_w = run_weights(inner_pairs, inner_n, outer_pairs, outer_n, local_grads, received, feats_t)
-    bricks_all = lax.axis_size("gx") * lax.axis_size("gy") * lax.axis_size("gz")
+    bricks_all = lax.axis_size(GX) * lax.axis_size(GY) * lax.axis_size("gz")
     grad_scale = math.sqrt(27.0 / (bricks_all * PI * BLOCK))
     weight_grad, after = reduce_weights(acc_w, grad_scale)
     input_grad = run_inputs(
@@ -171,15 +175,23 @@
 
 
 def solution(mesh):
+    gx, gy, gz = (mesh.shape[name] for name in ("gx", "gy", "gz"))
+    along_x = len({device.coords[0] for device in mesh.devices.flat})
+    cores = gy // len({device.coords[1] for device in mesh.devices.flat})
+    fine = Mesh(
+        mesh.devices.reshape(gx // along_x, along_x, gy // cores, cores, gz),
+        ("zh", "x", "y", "c", "gz"),
+    )
+    brick = P(GX, GY, "gz", None, None)
     in_specs = (
-        P("gx", "gy", "gz", None, None),
-        P("gx", "gy", "gz", None, None),
+        brick,
+        brick,
         P(),
-        P("gx", "gy", "gz", None, None),
-        P("gx", "gy", "gz", None, None),
-        P("gx", "gy", "gz", None, None, None),
-        P("gx", "gy", "gz"),
-        P("gx", "gy", "gz"),
+        brick,
+        brick,
+        P(GX, GY, "gz", None, None, None),
+        P(GX, GY, "gz"),
+        P(GX, GY, "gz"),
     )
-    out_specs = (P("gx", "gy", "gz", None, None), P())
-    return jax.shard_map(body, mesh=mesh, in_specs=in_specs, out_specs=out_specs, check_vma=False)
+    out_specs = (brick, P())
+    return jax.shard_map(body, mesh=fine, in_specs=in_specs, out_specs=out_specs, check_vma=False)

time: 171 us -> 163 us (0.953)
  blocking collectives: 79.9 us -> 72.3 us
  Pallas kernels: 18.3 us -> 25.7 us
  waiting for transfers between devices: 21.6 us -> 14.7 us
    all_to_all x1, waiting for transfers between devices: 4.65 us -> 0.01 us  [reduce_weights(): piece = lax.all_to_all(copies, ZZ, 0, 0, tiled=True).reshape(-1)]
    all_gather x2, blocking collectives: 32.7 us -> 28.8 us  [the longest x1 19.5 us: reduce_weights(): piece = lax.all_gather(piece, GY, tiled=True)]
    pallas_call x1, Pallas kernels: 9.08 us -> 12.8 us  [run_inputs(): pl.pallas_call(input_kernel, out_shape=jax.ShapeDtypeStruct((NB, BLOCK, C...]
    pallas_call x1, Pallas kernels: 9.18 us -> 12.9 us  [run_weights(): pl.pallas_call(weight_kernel, out_shape=jax.ShapeDtypeStruct((27, C, C),...]
    all_to_all x2, blocking collectives: 47.2 us -> 43.5 us  [reduce_weights(): parts = lax.all_to_all(flat.reshape(n, -1), axis, 0, 0, tiled=True)]
    all_to_all x1, waiting for transfers between devices: 12.3 us -> 9.99 us  [reduce_weights(): parts = lax.all_to_all(flat.reshape(n, -1), axis, 0, 0, tiled=True)]
  transfers between devices with their start and end apart: 8 -> 8, of which waited for: 3 -> 2; matrix products, arithmetic and copies ran while one was open for 3% -> 3% of each run, Pallas kernels for 5% -> 8%
where the time goes in v9:
time: 163 us
  blocking collectives  72.3 us (44%)
  starting transfers between devices  33 us (20%)
  Pallas kernels  25.7 us (16%)
  waiting for transfers between devices  14.7 us (9%)
  local copies, waits for them, and re-layouts  11.4 us (7%)
  other arithmetic  3.19 us (2%)
  between operations  2.22 us (1%)
    all_to_all x2, blocking collectives, reduce_weights(): parts = lax.all_to_all(flat.reshape(n, -1), axis, 0, 0, tiled=True)  43.5 us
    all_gather x1, blocking collectives, reduce_weights(): piece = lax.all_gather(piece, GY, tiled=True)  19.5 us
    all_to_all x1, starting transfers between devices, reduce_weights(): parts = lax.all_to_all(flat.reshape(n, -1), axis, 0, 0, tiled=True)  13.5 us
    pallas_call x1, Pallas kernels, run_weights(): pl.pallas_call(weight_kernel, out_shape=jax.ShapeDtypeStruct((27, C, C),...  12.9 us
    pallas_call x1, Pallas kernels, run_inputs(): pl.pallas_call(input_kernel, out_shape=jax.ShapeDtypeStruct((NB, BLOCK, C...  12.8 us
    ppermute x3, starting transfers between devices, extended(): before = lax.ppermute(last, axis, up)  10.1 us
    all_to_all x1, waiting for transfers between devices, reduce_weights(): parts = lax.all_to_all(flat.reshape(n, -1), axis, 0, 0, tiled=True)  9.99 us
    all_gather x1, blocking collectives, reduce_weights(): piece = lax.all_gather(piece, 'x', tiled=True)  9.3 us
  transfers between devices with their start and end apart: 8, of which 2 were waited for; matrix products, arithmetic and copies ran while one was open for 3% of the time, Pallas kernels for 8%

profile of v9, /device:TPU:1, one launch (start us, length us, event | category | flops | bytes accessed | tf_op | source)
XLA Modules:
  0.0 162.6 jit_solution(7537071293299509578)
XLA Ops:
  0.6 0.0 copy-start.4
  0.6 0.0 copy-start.5
  0.7 0.0 copy-start
  0.7 0.9 reshape_squeeze.10
  1.5 1.9 %gather_fusion = bf16[24,128,128]{2,1,0:T(8,128)(2,1)S(1)} fusion(bf16[32,128,128]{2,1,0:T(8,128)(2,1)} %bitcast.48, s32[1024]{0:T(1024)S(1)} %pad_clamp_fusion), kind=kCustom, calls=%fused_computation | custom fusion | bytes 1572960 | tf_op jit(solution)/shard_map/gather | solution.py:36
  3.5 0.1 slice_bitcast_fusion
  3.5 4.0 %collective-permute-start = (bf16[1,4,128,128]{3,2,1,0:T(8,128)(2,1)S(1)}, bf16[1,4,128,128]{3,2,1,0:T(8,128)(2,1)S(1)}, u32[]{:S(2)}, u32[]{:S(2)}) collective-permute-start(bf16[1,4,128,128]{3,2,1,0:T(8,128)(2,1)S(1)} %get-tuple-element.7), channel_id=1, source_target_pairs={{0,32},{32,64},{64,96},{96,128},{128,160},{160,192},{192,224},{224... | collective-permute-start | bytes 393224 | tf_op jit(solution)/shard_map/ppermute | solution.py:29
  7.5 1.3 collective-permute-start.1
  8.8 4.0 %collective-permute-start.2 = (bf16[1,4,128,128]{3,2,1,0:T(8,128)(2,1)S(1)}, bf16[1,4,128,128]{3,2,1,0:T(8,128)(2,1)S(1)}, u32[]{:S(2)}, u32[]{:S(2)}) collective-permute-start(bf16[1,4,128,128]{3,2,1,0:T(8,128)(2,1)S(1)} %get-tuple-element.5), channel_id=1, source_target_pairs={{0,4},{4,8},{8,12},{12,16},{16,20},{20,24},{24,28},{1,5},{5,9},{9,... | collective-permute-start | bytes 393224 | tf_op jit(solution)/shard_map/ppermute | solution.py:29
  12.9 3.4 %collective-permute-start.3 = (bf16[1,4,128,128]{3,2,1,0:T(8,128)(2,1)S(1)}, bf16[1,4,128,128]{3,2,1,0:T(8,128)(2,1)S(1)}, u32[]{:S(2)}, u32[]{:S(2)}) collective-permute-start(bf16[1,4,128,128]{3,2,1,0:T(8,128)(2,1)S(1)} %get-tuple-element.4), channel_id=1, source_target_pairs={{4,0},{8,4},{12,8},{16,12},{20,16},{24,20},{28,24},{5,1},{9,5},{13... | collective-permute-start | bytes 393224 | tf_op jit(solution)/shard_map/ppermute | solution.py:30
  16.2 2.1 %collective-permute-start.4 = (bf16[1,4,128,128]{3,2,1,0:T(8,128)(2,1)S(1)}, bf16[1,4,128,128]{3,2,1,0:T(8,128)(2,1)S(1)}, u32[]{:S(2)}, u32[]{:S(2)}) collective-permute-start(bf16[1,4,128,128]{3,2,1,0:T(8,128)(2,1)S(1)} %get-tuple-element.3), channel_id=1, source_target_pairs={{0,1},{1,2},{2,3},{4,5},{5,6},{6,7},{8,9},{9,10},{10,11},{12,13},{... | collective-permute-start | bytes 393224 | tf_op jit(solution)/shard_map/ppermute | solution.py:29
  18.3 0.0 copy-done.4
  18.3 0.8 copy.31
  19.1 0.0 copy-done.5
  19.2 0.7 copy.39
  21.1 0.0 copy-done
  21.1 1.3 copy.33
  22.5 0.0 collective-permute-done
  22.5 1.3 collective-permute-start.5
  23.8 0.0 collective-permute-done.1
  23.8 0.0 collective-permute-done.2
  23.8 0.0 collective-permute-done.3
  23.9 0.0 collective-permute-done.4
  23.9 4.7 %collective-permute-done.5 = bf16[1,4,128,128]{3,2,1,0:T(8,128)(2,1)S(1)} collective-permute-done((bf16[1,4,128,128]{3,2,1,0:T(8,128)(2,1)S(1)}, bf16[1,4,128,128]{3,2,1,0:T(8,128)(2,1)S(1)}, u32[]{:S(2)}, u32[]{:S(2)}) %collective-permute-start.5) | collective-permute-done | bytes 131104 | tf_op jit(solution)/shard_map/ppermute | solution.py:30
  28.6 0.0 copy-start.2
  28.7 0.9 copy-done.2
  29.5 12.9 %weight_pairs.1 = f32[27,128,128]{2,1,0:T(8,128)} custom-call(s32[288,3]{1,0:T(8,128)} %bitcast.51, s32[1]{0:T(128)} %bitcast.38.inner_live_ref, s32[32,3]{1,0:T(8,128)} %bitcast.53, s32[1]{0:T(128)} %bitcast.40.outer_live_ref, bf16[32,128,128]{2,1,0:T(8,128)(2,1)} %bitcast.49, bf16[24,128,128]{2,1,0:T(8,128)(2,1)} %copy-done.2, bf16[32,128,128]{2,1,0:T(8,128)(2,1)} %bitcast.45), custom_call_target="tpu_custom_call" | custom-call | flops 1342177280 | bytes 6291456 | tf_op jit(solution)/shard_map/weight_pairs/pallas_call | solution.py:120
  42.4 28.6 %all_to_all.33 = f32[8,1,55296]{2,1,0:T(1,128)S(1)} all-to-all(f32[8,1,55296]{2,1,0:T(1,128)} %bitcast.43), channel_id=1, replica_groups=mesh['zh'=4,'x'=4,'y'=4,'c'=2,'gz'=4] {'y','c'}, dimensions={0} | all-to-all | bytes 3538944 | tf_op jit(solution)/shard_map/all_to_all | solution.py:146
  71.0 1.3 reduce_sum.27
  72.3 14.9 %all_to_all.34 = f32[4,1,13824]{2,1,0:T(1,128)S(1)} all-to-all(f32[4,1,13824]{2,1,0:T(1,128)S(1)} %bitcast.46), channel_id=1, replica_groups=mesh['zh'=4,'x'=4,'y'=4,'c'=2,'gz'=4] {'x'}, dimensions={0} | all-to-all | bytes 442368 | tf_op jit(solution)/shard_map/all_to_all | solution.py:146
  87.2 0.2 reduce_sum.28
  87.4 0.7 all_to_all.26
  88.1 13.5 %all-to-all-start.2 = ((f32[16,1,864]{2,1,0:T(1,128)}), f32[16,1,864]{2,1,0:T(1,128)S(1)}, u32[]{:S(2)}, u32[]{:S(2)}) async-start(f32[16,1,864]{2,1,0:T(1,128)} %all_to_all.26), calls=%async_computation.2 | async-start | bytes 114688 | tf_op jit(solution)/shard_map/all_to_all | solution.py:146
  101.7 1.6 %copy.32 = bf16[27,128,128]{1,2,0:T(8,128)(2,1)} copy(bf16[27,128,128]{2,1,0:T(8,128)(2,1)S(1)} %copy-done.1) | data formatting | bytes 1769472 | tf_op args[2]
  103.3 10.0 %all-to-all-done.2 = f32[16,1,864]{2,1,0:T(1,128)S(1)} async-done(((f32[16,1,864]{2,1,0:T(1,128)}), f32[16,1,864]{2,1,0:T(1,128)S(1)}, u32[]{:S(2)}, u32[]{:S(2)}) %all-to-all-start.2) | async-done | bytes 55328 | tf_op jit(solution)/shard_map/all_to_all | solution.py:146
  113.4 0.5 broadcast.38
  113.9 0.8 reduce.5
  114.7 0.7 reshape.92
  115.4 3.5 %all-to-all-start.3 = ((bf16[16,2,432]{2,1,0:T(2,128)(2,1)}), bf16[16,2,432]{2,1,0:T(2,128)(2,1)S(1)}, u32[]{:S(2)}, u32[]{:S(2)}) async-start(bf16[16,2,432]{2,1,0:T(2,128)(2,1)} %reshape.92), calls=%async_computation.3 | async-start | bytes 65536 | tf_op jit(solution)/shard_map/all_to_all | solution.py:152
  119.0 12.8 %input_pairs.1 = bf16[32,128,128]{2,1,0:T(8,128)(2,1)} custom-call(s32[288,3]{1,0:T(8,128)} %bitcast.52, s32[1]{0:T(128)} %bitcast.39.inner_live_ref, s32[32,3]{1,0:T(8,128)} %bitcast.54, s32[1]{0:T(128)} %bitcast.41.outer_live_ref, bf16[32,128,128]{2,1,0:T(8,128)(2,1)} %bitcast.50, bf16[24,128,128]{2,1,0:T(8,128)(2,1)} %copy-done.2, ...), custom_call_target="tpu_custom_call" | custom-call | flops 1342177280 | bytes 6291456 | tf_op jit(solution)/shard_map/input_pairs/pallas_call | solution.py:131
  131.8 0.0 all-to-all-done.3
  131.8 0.1 reshape.93
  131.9 0.2 reduce.3
  132.0 0.1 reshape.87
  132.2 9.3 %all-gather = bf16[4,1,13824]{2,1,0:T(2,128)(2,1)S(1)} all-gather(bf16[1,1,13824]{2,1,0:T(2,128)(2,1)S(1)} %reshape.87), channel_id=1, replica_groups=mesh['zh'=4,'x'=4,'y'=4,'c'=2,'gz'=4] {'x'}, dimensions={0}, use_global_device_ids=true | all-gather | bytes 138240 | tf_op jit(solution)/shard_map/all_gather | solution.py:153
  141.5 0.7 reduce.4
  142.2 19.5 %all_gather.7 = bf16[442368]{0:T(1024)(128)(2,1)S(1)} all-gather(bf16[55296]{0:T(1024)(128)(2,1)S(1)} %reshape.88), channel_id=1, replica_groups=mesh['zh'=4,'x'=4,'y'=4,'c'=2,'gz'=4] {'y','c'}, dimensions={0}, use_global_device_ids=true | all-gather | bytes 995328 | tf_op jit(solution)/shard_map/all_gather | solution.py:154
  161.7 0.9 copy.50
  (16 shorter events, 0.3 us)
Async XLA Ops:
  0.6 17.7 %copy-start.4 = (s32[1,1,1,288,3]{3,2,4,1,0:T(1,128)S(1)}, s32[1,1,1,288,3]{3,2,4,1,0:T(1,128)}, u32[]{:S(2)}) copy-start(s32[1,1,1,288,3]{3,2,4,1,0:T(1,128)} %param.11) | copy-start | bytes 10372
  0.6 18.5 %copy-start.5 = (s32[1,1,1,32,3]{3,2,4,1,0:T(1,128)S(1)}, s32[1,1,1,32,3]{3,2,4,1,0:T(1,128)}, u32[]{:S(2)}) copy-start(s32[1,1,1,32,3]{3,2,4,1,0:T(1,128)} %param.12) | copy-start | bytes 1156
  0.7 20.5 %copy-start = (bf16[1,1,1,4096,128]{4,3,2,1,0:T(8,128)(2,1)S(1)}, bf16[1,1,1,4096,128]{4,3,2,1,0:T(8,128)(2,1)}, u32[]{:S(2)}) copy-start(bf16[1,1,1,4096,128]{4,3,2,1,0:T(8,128)(2,1)} %param.8) | copy-start | bytes 3145732
  3.5 18.9 %collective-permute-start = (bf16[1,4,128,128]{3,2,1,0:T(8,128)(2,1)S(1)}, bf16[1,4,128,128]{3,2,1,0:T(8,128)(2,1)S(1)}, u32[]{:S(2)}, u32[]{:S(2)}) collective-permute-start(bf16[1,4,128,128]{3,2,1,0:T(8,128)(2,1)S(1)} %get-tuple-element.7), channel_id=1, source_target_pairs={{0,32},{32,64},{64,96},{96,128},{128,160},{160,192},{192,224},{224... | collective-permute-start | bytes 393224 | tf_op jit(solution)/shard_map/ppermute | solution.py:29
  7.5 16.3 %collective-permute-start.1 = (bf16[1,4,128,128]{3,2,1,0:T(8,128)(2,1)S(1)}, bf16[1,4,128,128]{3,2,1,0:T(8,128)(2,1)S(1)}, u32[]{:S(2)}, u32[]{:S(2)}) collective-permute-start(bf16[1,4,128,128]{3,2,1,0:T(8,128)(2,1)S(1)} %get-tuple-element.6), channel_id=1, source_target_pairs={{32,0},{64,32},{96,64},{128,96},{160,128},{192,160},{224,192},{256... | collective-permute-start | bytes 393224 | tf_op jit(solution)/shard_map/ppermute | solution.py:30
  8.8 15.0 %collective-permute-start.2 = (bf16[1,4,128,128]{3,2,1,0:T(8,128)(2,1)S(1)}, bf16[1,4,128,128]{3,2,1,0:T(8,128)(2,1)S(1)}, u32[]{:S(2)}, u32[]{:S(2)}) collective-permute-start(bf16[1,4,128,128]{3,2,1,0:T(8,128)(2,1)S(1)} %get-tuple-element.5), channel_id=1, source_target_pairs={{0,4},{4,8},{8,12},{12,16},{16,20},{20,24},{24,28},{1,5},{5,9},{9,... | collective-permute-start | bytes 393224 | tf_op jit(solution)/shard_map/ppermute | solution.py:29
  12.9 11.0 %collective-permute-start.3 = (bf16[1,4,128,128]{3,2,1,0:T(8,128)(2,1)S(1)}, bf16[1,4,128,128]{3,2,1,0:T(8,128)(2,1)S(1)}, u32[]{:S(2)}, u32[]{:S(2)}) collective-permute-start(bf16[1,4,128,128]{3,2,1,0:T(8,128)(2,1)S(1)} %get-tuple-element.4), channel_id=1, source_target_pairs={{4,0},{8,4},{12,8},{16,12},{20,16},{24,20},{28,24},{5,1},{9,5},{13... | collective-permute-start | bytes 393224 | tf_op jit(solution)/shard_map/ppermute | solution.py:30
  16.2 7.6 %collective-permute-start.4 = (bf16[1,4,128,128]{3,2,1,0:T(8,128)(2,1)S(1)}, bf16[1,4,128,128]{3,2,1,0:T(8,128)(2,1)S(1)}, u32[]{:S(2)}, u32[]{:S(2)}) collective-permute-start(bf16[1,4,128,128]{3,2,1,0:T(8,128)(2,1)S(1)} %get-tuple-element.3), channel_id=1, source_target_pairs={{0,1},{1,2},{2,3},{4,5},{5,6},{6,7},{8,9},{9,10},{10,11},{12,13},{... | collective-permute-start | bytes 393224 | tf_op jit(solution)/shard_map/ppermute | solution.py:29
  22.5 6.2 %collective-permute-start.5 = (bf16[1,4,128,128]{3,2,1,0:T(8,128)(2,1)S(1)}, bf16[1,4,128,128]{3,2,1,0:T(8,128)(2,1)S(1)}, u32[]{:S(2)}, u32[]{:S(2)}) collective-permute-start(bf16[1,4,128,128]{3,2,1,0:T(8,128)(2,1)S(1)} %get-tuple-element.2), channel_id=1, source_target_pairs={{1,0},{2,1},{3,2},{5,4},{6,5},{7,6},{9,8},{10,9},{11,10},{13,12},{... | collective-permute-start | bytes 393224 | tf_op jit(solution)/shard_map/ppermute | solution.py:30
  28.6 0.9 copy-start.2
  71.0 30.7 %copy-start.1 = (bf16[27,128,128]{2,1,0:T(8,128)(2,1)S(1)}, bf16[27,128,128]{2,1,0:T(8,128)(2,1)}, u32[]{:S(2)}) copy-start(bf16[27,128,128]{2,1,0:T(8,128)(2,1)} %param.10) | copy-start | bytes 2654212
  88.1 25.1 %all-to-all-start.2 = ((f32[16,1,864]{2,1,0:T(1,128)}), f32[16,1,864]{2,1,0:T(1,128)S(1)}, u32[]{:S(2)}, u32[]{:S(2)}) async-start(f32[16,1,864]{2,1,0:T(1,128)} %all_to_all.26), calls=%async_computation.2 | async-start | bytes 114688 | tf_op jit(solution)/shard_map/all_to_all | solution.py:146
  113.3 5.6 %copy-start.3 = (f32[864]{0:T(1024)}, f32[864]{0:T(1024)S(1)}, u32[]{:S(2)}) copy-start(f32[864]{0:T(1024)S(1)} %reduce_sum.29.after_ref) | copy-start | bytes 10372
  115.4 16.3 %all-to-all-start.3 = ((bf16[16,2,432]{2,1,0:T(2,128)(2,1)}), bf16[16,2,432]{2,1,0:T(2,128)(2,1)S(1)}, u32[]{:S(2)}, u32[]{:S(2)}) async-start(bf16[16,2,432]{2,1,0:T(2,128)(2,1)} %reshape.92), calls=%async_computation.3 | async-start | bytes 65536 | tf_op jit(solution)/shard_map/all_to_all | solution.py:152

commit v10 on v9

--- a/solution.py
+++ b/solution.py
@@ -13,7 +13,7 @@
 NB = 32
 PI = 288
 PB = 32
-UNROLL = 16
+UNROLL = 32
 GX = ("zh", "x")
 GY = ("y", "c")
 ZZ = ("zh", "gz")

time: 163 us -> 168 us (1.031)
  blocking collectives: 72.3 us -> 75.2 us
  starting transfers between devices: 33 us -> 35.3 us
    all_to_all x1, starting transfers between devices: 13.5 us -> 15.7 us  [reduce_weights(): parts = lax.all_to_all(flat.reshape(n, -1), axis, 0, 0, tiled=True)]
    all_to_all x2, blocking collectives: 43.5 us -> 45.4 us  [reduce_weights(): parts = lax.all_to_all(flat.reshape(n, -1), axis, 0, 0, tiled=True)]
where the time goes in v10:
time: 168 us; the launch traced here: 167 us
  blocking collectives  75.2 us (45%)
  starting transfers between devices  35.3 us (21%)
  Pallas kernels  25.2 us (15%)
  waiting for transfers between devices  14.7 us (9%)
  local copies, waits for them, and re-layouts  11.4 us (7%)
  other arithmetic  3.19 us (2%)
  between operations  2.22 us (1%)
    all_to_all x2, blocking collectives, reduce_weights(): parts = lax.all_to_all(flat.reshape(n, -1), axis, 0, 0, tiled=True)  45.4 us
    all_gather x1, blocking collectives, reduce_weights(): piece = lax.all_gather(piece, GY, tiled=True)  19 us
    all_to_all x1, starting transfers between devices, reduce_weights(): parts = lax.all_to_all(flat.reshape(n, -1), axis, 0, 0, tiled=True)  15.7 us
    pallas_call x1, Pallas kernels, run_weights(): pl.pallas_call(weight_kernel, out_shape=jax.ShapeDtypeStruct((27, C, C),...  12.7 us
    pallas_call x1, Pallas kernels, run_inputs(): pl.pallas_call(input_kernel, out_shape=jax.ShapeDtypeStruct((NB, BLOCK, C...  12.5 us
    all_gather x1, blocking collectives, reduce_weights(): piece = lax.all_gather(piece, 'x', tiled=True)  10.8 us
    ppermute x3, starting transfers between devices, extended(): before = lax.ppermute(last, axis, up)  10.1 us
    all_to_all x1, waiting for transfers between devices, reduce_weights(): parts = lax.all_to_all(flat.reshape(n, -1), axis, 0, 0, tiled=True)  9.99 us
  transfers between devices with their start and end apart: 8, of which 2 were waited for; matrix products, arithmetic and copies ran while one was open for 3% of the time, Pallas kernels for 8%

profile of v10, /device:TPU:1, one launch (start us, length us, event | category | flops | bytes accessed | tf_op | source)
XLA Modules:
  0.0 167.2 jit_solution(13984646904302588789)
XLA Ops:
  0.6 0.0 copy-start.4
  0.6 0.0 copy-start.5
  0.7 0.0 copy-start
  0.7 0.9 reshape_squeeze.10
  1.5 1.9 %gather_fusion = bf16[24,128,128]{2,1,0:T(8,128)(2,1)S(1)} fusion(bf16[32,128,128]{2,1,0:T(8,128)(2,1)} %bitcast.48, s32[1024]{0:T(1024)S(1)} %pad_clamp_fusion), kind=kCustom, calls=%fused_computation | custom fusion | bytes 1572960 | tf_op jit(solution)/shard_map/gather | solution.py:36
  3.5 0.1 slice_bitcast_fusion
  3.5 4.0 %collective-permute-start = (bf16[1,4,128,128]{3,2,1,0:T(8,128)(2,1)S(1)}, bf16[1,4,128,128]{3,2,1,0:T(8,128)(2,1)S(1)}, u32[]{:S(2)}, u32[]{:S(2)}) collective-permute-start(bf16[1,4,128,128]{3,2,1,0:T(8,128)(2,1)S(1)} %get-tuple-element.7), channel_id=1, source_target_pairs={{0,32},{32,64},{64,96},{96,128},{128,160},{160,192},{192,224},{224... | collective-permute-start | bytes 393224 | tf_op jit(solution)/shard_map/ppermute | solution.py:29
  7.5 1.3 collective-permute-start.1
  8.8 4.0 %collective-permute-start.2 = (bf16[1,4,128,128]{3,2,1,0:T(8,128)(2,1)S(1)}, bf16[1,4,128,128]{3,2,1,0:T(8,128)(2,1)S(1)}, u32[]{:S(2)}, u32[]{:S(2)}) collective-permute-start(bf16[1,4,128,128]{3,2,1,0:T(8,128)(2,1)S(1)} %get-tuple-element.5), channel_id=1, source_target_pairs={{0,4},{4,8},{8,12},{12,16},{16,20},{20,24},{24,28},{1,5},{5,9},{9,... | collective-permute-start | bytes 393224 | tf_op jit(solution)/shard_map/ppermute | solution.py:29
  12.9 3.4 %collective-permute-start.3 = (bf16[1,4,128,128]{3,2,1,0:T(8,128)(2,1)S(1)}, bf16[1,4,128,128]{3,2,1,0:T(8,128)(2,1)S(1)}, u32[]{:S(2)}, u32[]{:S(2)}) collective-permute-start(bf16[1,4,128,128]{3,2,1,0:T(8,128)(2,1)S(1)} %get-tuple-element.4), channel_id=1, source_target_pairs={{4,0},{8,4},{12,8},{16,12},{20,16},{24,20},{28,24},{5,1},{9,5},{13... | collective-permute-start | bytes 393224 | tf_op jit(solution)/shard_map/ppermute | solution.py:30
  16.2 2.1 %collective-permute-start.4 = (bf16[1,4,128,128]{3,2,1,0:T(8,128)(2,1)S(1)}, bf16[1,4,128,128]{3,2,1,0:T(8,128)(2,1)S(1)}, u32[]{:S(2)}, u32[]{:S(2)}) collective-permute-start(bf16[1,4,128,128]{3,2,1,0:T(8,128)(2,1)S(1)} %get-tuple-element.3), channel_id=1, source_target_pairs={{0,1},{1,2},{2,3},{4,5},{5,6},{6,7},{8,9},{9,10},{10,11},{12,13},{... | collective-permute-start | bytes 393224 | tf_op jit(solution)/shard_map/ppermute | solution.py:29
  18.3 0.0 copy-done.4
  18.3 0.8 copy.31
  19.1 0.0 copy-done.5
  19.2 0.7 copy.39
  21.1 0.0 copy-done
  21.1 1.3 copy.33
  22.5 0.0 collective-permute-done
  22.5 1.3 collective-permute-start.5
  23.8 0.0 collective-permute-done.1
  23.8 0.0 collective-permute-done.2
  23.8 0.0 collective-permute-done.3
  23.9 0.0 collective-permute-done.4
  23.9 4.7 %collective-permute-done.5 = bf16[1,4,128,128]{3,2,1,0:T(8,128)(2,1)S(1)} collective-permute-done((bf16[1,4,128,128]{3,2,1,0:T(8,128)(2,1)S(1)}, bf16[1,4,128,128]{3,2,1,0:T(8,128)(2,1)S(1)}, u32[]{:S(2)}, u32[]{:S(2)}) %collective-permute-start.5) | collective-permute-done | bytes 131104 | tf_op jit(solution)/shard_map/ppermute | solution.py:30
  28.6 0.0 copy-start.2
  28.7 0.9 copy-done.2
  29.5 12.7 %weight_pairs.1 = f32[27,128,128]{2,1,0:T(8,128)} custom-call(s32[288,3]{1,0:T(8,128)} %bitcast.51, s32[1]{0:T(128)} %bitcast.38.inner_live_ref, s32[32,3]{1,0:T(8,128)} %bitcast.53, s32[1]{0:T(128)} %bitcast.40.outer_live_ref, bf16[32,128,128]{2,1,0:T(8,128)(2,1)} %bitcast.49, bf16[24,128,128]{2,1,0:T(8,128)(2,1)} %copy-done.2, bf16[32,128,128]{2,1,0:T(8,128)(2,1)} %bitcast.45), custom_call_target="tpu_custom_call" | custom-call | flops 1342177280 | bytes 6291456 | tf_op jit(solution)/shard_map/weight_pairs/pallas_call | solution.py:120
  42.2 30.4 %all_to_all.33 = f32[8,1,55296]{2,1,0:T(1,128)S(1)} all-to-all(f32[8,1,55296]{2,1,0:T(1,128)} %bitcast.43), channel_id=1, replica_groups=mesh['zh'=4,'x'=4,'y'=4,'c'=2,'gz'=4] {'y','c'}, dimensions={0} | all-to-all | bytes 3538944 | tf_op jit(solution)/shard_map/all_to_all | solution.py:146
  72.6 1.3 reduce_sum.27
  73.9 15.0 %all_to_all.34 = f32[4,1,13824]{2,1,0:T(1,128)S(1)} all-to-all(f32[4,1,13824]{2,1,0:T(1,128)S(1)} %bitcast.46), channel_id=1, replica_groups=mesh['zh'=4,'x'=4,'y'=4,'c'=2,'gz'=4] {'x'}, dimensions={0} | all-to-all | bytes 442368 | tf_op jit(solution)/shard_map/all_to_all | solution.py:146
  88.9 0.2 reduce_sum.28
  89.1 0.7 all_to_all.26
  89.8 15.7 %all-to-all-start.2 = ((f32[16,1,864]{2,1,0:T(1,128)}), f32[16,1,864]{2,1,0:T(1,128)S(1)}, u32[]{:S(2)}, u32[]{:S(2)}) async-start(f32[16,1,864]{2,1,0:T(1,128)} %all_to_all.26), calls=%async_computation.2 | async-start | bytes 114688 | tf_op jit(solution)/shard_map/all_to_all | solution.py:146
  105.6 1.6 copy.32
  107.2 10.0 %all-to-all-done.2 = f32[16,1,864]{2,1,0:T(1,128)S(1)} async-done(((f32[16,1,864]{2,1,0:T(1,128)}), f32[16,1,864]{2,1,0:T(1,128)S(1)}, u32[]{:S(2)}, u32[]{:S(2)}) %all-to-all-start.2) | async-done | bytes 55328 | tf_op jit(solution)/shard_map/all_to_all | solution.py:146
  117.3 0.5 broadcast.38
  117.8 0.8 reduce.5
  118.6 0.7 reshape.92
  119.3 3.5 %all-to-all-start.3 = ((bf16[16,2,432]{2,1,0:T(2,128)(2,1)}), bf16[16,2,432]{2,1,0:T(2,128)(2,1)S(1)}, u32[]{:S(2)}, u32[]{:S(2)}) async-start(bf16[16,2,432]{2,1,0:T(2,128)(2,1)} %reshape.92), calls=%async_computation.3 | async-start | bytes 65536 | tf_op jit(solution)/shard_map/all_to_all | solution.py:152
  122.9 12.5 %input_pairs.1 = bf16[32,128,128]{2,1,0:T(8,128)(2,1)} custom-call(s32[288,3]{1,0:T(8,128)} %bitcast.52, s32[1]{0:T(128)} %bitcast.39.inner_live_ref, s32[32,3]{1,0:T(8,128)} %bitcast.54, s32[1]{0:T(128)} %bitcast.41.outer_live_ref, bf16[32,128,128]{2,1,0:T(8,128)(2,1)} %bitcast.50, bf16[24,128,128]{2,1,0:T(8,128)(2,1)} %copy-done.2, ...), custom_call_target="tpu_custom_call" | custom-call | flops 1342177280 | bytes 6291456 | tf_op jit(solution)/shard_map/input_pairs/pallas_call | solution.py:131
  135.4 0.0 all-to-all-done.3
  135.4 0.1 reshape.93
  135.5 0.2 reduce.3
  135.7 0.1 reshape.87
  135.8 10.8 %all-gather = bf16[4,1,13824]{2,1,0:T(2,128)(2,1)S(1)} all-gather(bf16[1,1,13824]{2,1,0:T(2,128)(2,1)S(1)} %reshape.87), channel_id=1, replica_groups=mesh['zh'=4,'x'=4,'y'=4,'c'=2,'gz'=4] {'x'}, dimensions={0}, use_global_device_ids=true | all-gather | bytes 138240 | tf_op jit(solution)/shard_map/all_gather | solution.py:153
  146.6 0.7 reduce.4
  147.3 19.0 %all_gather.7 = bf16[442368]{0:T(1024)(128)(2,1)S(1)} all-gather(bf16[55296]{0:T(1024)(128)(2,1)S(1)} %reshape.88), channel_id=1, replica_groups=mesh['zh'=4,'x'=4,'y'=4,'c'=2,'gz'=4] {'y','c'}, dimensions={0}, use_global_device_ids=true | all-gather | bytes 995328 | tf_op jit(solution)/shard_map/all_gather | solution.py:154
  166.3 0.9 copy.50
  (16 shorter events, 0.3 us)
Async XLA Ops:
  0.6 17.7 %copy-start.4 = (s32[1,1,1,288,3]{3,2,4,1,0:T(1,128)S(1)}, s32[1,1,1,288,3]{3,2,4,1,0:T(1,128)}, u32[]{:S(2)}) copy-start(s32[1,1,1,288,3]{3,2,4,1,0:T(1,128)} %param.11) | copy-start | bytes 10372
  0.6 18.5 %copy-start.5 = (s32[1,1,1,32,3]{3,2,4,1,0:T(1,128)S(1)}, s32[1,1,1,32,3]{3,2,4,1,0:T(1,128)}, u32[]{:S(2)}) copy-start(s32[1,1,1,32,3]{3,2,4,1,0:T(1,128)} %param.12) | copy-start | bytes 1156
  0.7 20.5 %copy-start = (bf16[1,1,1,4096,128]{4,3,2,1,0:T(8,128)(2,1)S(1)}, bf16[1,1,1,4096,128]{4,3,2,1,0:T(8,128)(2,1)}, u32[]{:S(2)}) copy-start(bf16[1,1,1,4096,128]{4,3,2,1,0:T(8,128)(2,1)} %param.8) | copy-start | bytes 3145732
  3.5 18.9 %collective-permute-start = (bf16[1,4,128,128]{3,2,1,0:T(8,128)(2,1)S(1)}, bf16[1,4,128,128]{3,2,1,0:T(8,128)(2,1)S(1)}, u32[]{:S(2)}, u32[]{:S(2)}) collective-permute-start(bf16[1,4,128,128]{3,2,1,0:T(8,128)(2,1)S(1)} %get-tuple-element.7), channel_id=1, source_target_pairs={{0,32},{32,64},{64,96},{96,128},{128,160},{160,192},{192,224},{224... | collective-permute-start | bytes 393224 | tf_op jit(solution)/shard_map/ppermute | solution.py:29
  7.5 16.3 %collective-permute-start.1 = (bf16[1,4,128,128]{3,2,1,0:T(8,128)(2,1)S(1)}, bf16[1,4,128,128]{3,2,1,0:T(8,128)(2,1)S(1)}, u32[]{:S(2)}, u32[]{:S(2)}) collective-permute-start(bf16[1,4,128,128]{3,2,1,0:T(8,128)(2,1)S(1)} %get-tuple-element.6), channel_id=1, source_target_pairs={{32,0},{64,32},{96,64},{128,96},{160,128},{192,160},{224,192},{256... | collective-permute-start | bytes 393224 | tf_op jit(solution)/shard_map/ppermute | solution.py:30
  8.8 15.0 %collective-permute-start.2 = (bf16[1,4,128,128]{3,2,1,0:T(8,128)(2,1)S(1)}, bf16[1,4,128,128]{3,2,1,0:T(8,128)(2,1)S(1)}, u32[]{:S(2)}, u32[]{:S(2)}) collective-permute-start(bf16[1,4,128,128]{3,2,1,0:T(8,128)(2,1)S(1)} %get-tuple-element.5), channel_id=1, source_target_pairs={{0,4},{4,8},{8,12},{12,16},{16,20},{20,24},{24,28},{1,5},{5,9},{9,... | collective-permute-start | bytes 393224 | tf_op jit(solution)/shard_map/ppermute | solution.py:29
  12.9 11.0 %collective-permute-start.3 = (bf16[1,4,128,128]{3,2,1,0:T(8,128)(2,1)S(1)}, bf16[1,4,128,128]{3,2,1,0:T(8,128)(2,1)S(1)}, u32[]{:S(2)}, u32[]{:S(2)}) collective-permute-start(bf16[1,4,128,128]{3,2,1,0:T(8,128)(2,1)S(1)} %get-tuple-element.4), channel_id=1, source_target_pairs={{4,0},{8,4},{12,8},{16,12},{20,16},{24,20},{28,24},{5,1},{9,5},{13... | collective-permute-start | bytes 393224 | tf_op jit(solution)/shard_map/ppermute | solution.py:30
  16.2 7.6 %collective-permute-start.4 = (bf16[1,4,128,128]{3,2,1,0:T(8,128)(2,1)S(1)}, bf16[1,4,128,128]{3,2,1,0:T(8,128)(2,1)S(1)}, u32[]{:S(2)}, u32[]{:S(2)}) collective-permute-start(bf16[1,4,128,128]{3,2,1,0:T(8,128)(2,1)S(1)} %get-tuple-element.3), channel_id=1, source_target_pairs={{0,1},{1,2},{2,3},{4,5},{5,6},{6,7},{8,9},{9,10},{10,11},{12,13},{... | collective-permute-start | bytes 393224 | tf_op jit(solution)/shard_map/ppermute | solution.py:29
  22.5 6.2 %collective-permute-start.5 = (bf16[1,4,128,128]{3,2,1,0:T(8,128)(2,1)S(1)}, bf16[1,4,128,128]{3,2,1,0:T(8,128)(2,1)S(1)}, u32[]{:S(2)}, u32[]{:S(2)}) collective-permute-start(bf16[1,4,128,128]{3,2,1,0:T(8,128)(2,1)S(1)} %get-tuple-element.2), channel_id=1, source_target_pairs={{1,0},{2,1},{3,2},{5,4},{6,5},{7,6},{9,8},{10,9},{11,10},{13,12},{... | collective-permute-start | bytes 393224 | tf_op jit(solution)/shard_map/ppermute | solution.py:30
  28.6 0.9 copy-start.2
  72.6 32.9 %copy-start.1 = (bf16[27,128,128]{2,1,0:T(8,128)(2,1)S(1)}, bf16[27,128,128]{2,1,0:T(8,128)(2,1)}, u32[]{:S(2)}) copy-start(bf16[27,128,128]{2,1,0:T(8,128)(2,1)} %param.10) | copy-start | bytes 2654212
  89.8 27.4 %all-to-all-start.2 = ((f32[16,1,864]{2,1,0:T(1,128)}), f32[16,1,864]{2,1,0:T(1,128)S(1)}, u32[]{:S(2)}, u32[]{:S(2)}) async-start(f32[16,1,864]{2,1,0:T(1,128)} %all_to_all.26), calls=%async_computation.2 | async-start | bytes 114688 | tf_op jit(solution)/shard_map/all_to_all | solution.py:146
  117.2 5.6 %copy-start.3 = (f32[864]{0:T(1024)}, f32[864]{0:T(1024)S(1)}, u32[]{:S(2)}) copy-start(f32[864]{0:T(1024)S(1)} %reduce_sum.29.after_ref) | copy-start | bytes 10372
  119.3 16.1 %all-to-all-start.3 = ((bf16[16,2,432]{2,1,0:T(2,128)(2,1)}), bf16[16,2,432]{2,1,0:T(2,128)(2,1)S(1)}, u32[]{:S(2)}, u32[]{:S(2)}) async-start(bf16[16,2,432]{2,1,0:T(2,128)(2,1)} %reshape.92), calls=%async_computation.3 | async-start | bytes 65536 | tf_op jit(solution)/shard_map/all_to_all | solution.py:152

commit v11 on v9

--- a/solution.py
+++ b/solution.py
@@ -46,43 +46,51 @@
     def pair_ids(i):
         return (pairs_ref[i, 0], pairs_ref[i, 1] - table_base, pairs_ref[i, 2])
 
+    live = jnp.clip(live_ref[0], 0, pairs_ref.shape[0])
+
+    def group_at(group, masked):
+        rows = [group * UNROLL + j for j in range(UNROLL)]
+        ids = [pair_ids(row) for row in rows]
+        grads = [table_ref[a] for _, a, _ in ids]
+        update(ids, grads, [row < live for row in rows] if masked else None)
+
     def one_group(group, carry):
-        ids = [pair_ids(group * UNROLL + j) for j in range(UNROLL)]
-        grads = [table_ref[a] for _, a, _ in ids]
-        update(ids, grads)
+        group_at(group, False)
         return carry
 
-    def one_pair(i, carry):
-        k, a, b = pair_ids(i)
-        update([(k, a, b)], [table_ref[a]])
+    def last_group(group, carry):
+        group_at(group, True)
         return carry
 
-    live = jnp.clip(live_ref[0], 0, pairs_ref.shape[0])
     groups = live // UNROLL
     lax.fori_loop(0, groups, one_group, 0)
-    lax.fori_loop(groups * UNROLL, live, one_pair, 0)
+    lax.fori_loop(groups, (live + UNROLL - 1) // UNROLL, last_group, 0)
+
+
+def keep(term, valid):
+    return term if valid is None else jnp.where(valid, term, jnp.zeros_like(term))
 
 
 def weight_updater(ft_ref, acc_w):
-    def update(ids, grads):
+    def update(ids, grads, valid):
         terms = [
             jnp.dot(ft_ref[b], g, preferred_element_type=jnp.float32)
             for g, (_, _, b) in zip(grads, ids)
         ]
-        for (k, _, _), term in zip(ids, terms):
-            acc_w[k] += term
+        for j, ((k, _, _), term) in enumerate(zip(ids, terms)):
+            acc_w[k] += keep(term, None if valid is None else valid[j])
 
     return update
 
 
 def input_updater(kt_ref, acc_in):
-    def update(ids, grads):
+    def update(ids, grads, valid):
         terms = [
             jnp.dot(g, kt_ref[k], preferred_element_type=jnp.float32)
             for g, (k, _, _) in zip(grads, ids)
         ]
-        for (_, _, b), term in zip(ids, terms):
-            acc_in[b] += term
+        for j, ((_, _, b), term) in enumerate(zip(ids, terms)):
+            acc_in[b] += keep(term, None if valid is None else valid[j])
 
     return update
 

time: 163 us -> 160 us (0.982)
  Pallas kernels: 25.7 us -> 21.7 us
    pallas_call x1, Pallas kernels: 12.8 us -> 10.8 us  [run_inputs(): pl.pallas_call(input_kernel, out_shape=jax.ShapeDtypeStruct((NB, BLOCK, C...]
    pallas_call x1, Pallas kernels: 12.9 us -> 10.9 us  [run_weights(): pl.pallas_call(weight_kernel, out_shape=jax.ShapeDtypeStruct((27, C, C),...]
    all_to_all x2, blocking collectives: 43.5 us -> 41.7 us  [reduce_weights(): parts = lax.all_to_all(flat.reshape(n, -1), axis, 0, 0, tiled=True)]
  transfers between devices with their start and end apart: 8 -> 8, of which waited for: 2 -> 3; matrix products, arithmetic and copies ran while one was open for 3% -> 3% of each run, Pallas kernels for 8% -> 7%
where the time goes in v11:
time: 160 us
  blocking collectives  72 us (45%)
  starting transfers between devices  33.7 us (21%)
  Pallas kernels  21.7 us (14%)
  waiting for transfers between devices  15.2 us (10%)
  local copies, waits for them, and re-layouts  11.4 us (7%)
  other arithmetic  3.19 us (2%)
  between operations  2.21 us (1%)
    all_to_all x2, blocking collectives, reduce_weights(): parts = lax.all_to_all(flat.reshape(n, -1), axis, 0, 0, tiled=True)  41.7 us
    all_gather x1, blocking collectives, reduce_weights(): piece = lax.all_gather(piece, GY, tiled=True)  21 us
    all_to_all x1, starting transfers between devices, reduce_weights(): parts = lax.all_to_all(flat.reshape(n, -1), axis, 0, 0, tiled=True)  14.2 us
    pallas_call x1, Pallas kernels, run_weights(): pl.pallas_call(weight_kernel, out_shape=jax.ShapeDtypeStruct((27, C, C),...  10.9 us
    pallas_call x1, Pallas kernels, run_inputs(): pl.pallas_call(input_kernel, out_shape=jax.ShapeDtypeStruct((NB, BLOCK, C...  10.8 us
    ppermute x3, starting transfers between devices, extended(): before = lax.ppermute(last, axis, up)  10.1 us
    all_to_all x1, waiting for transfers between devices, reduce_weights(): parts = lax.all_to_all(flat.reshape(n, -1), axis, 0, 0, tiled=True)  9.99 us
    all_gather x1, blocking collectives, reduce_weights(): piece = lax.all_gather(piece, 'x', tiled=True)  9.3 us
  transfers between devices with their start and end apart: 8, of which 3 were waited for; matrix products, arithmetic and copies ran while one was open for 3% of the time, Pallas kernels for 7%

profile of v11, /device:TPU:1, one launch (start us, length us, event | category | flops | bytes accessed | tf_op | source)
XLA Modules:
  0.0 159.5 jit_solution(12088626750154712042)
XLA Ops:
  0.6 0.0 copy-start.4
  0.6 0.0 copy-start.5
  0.7 0.0 copy-start
  0.7 0.9 reshape_squeeze.10
  1.5 1.9 %gather_fusion = bf16[24,128,128]{2,1,0:T(8,128)(2,1)S(1)} fusion(bf16[32,128,128]{2,1,0:T(8,128)(2,1)} %bitcast.48, s32[1024]{0:T(1024)S(1)} %pad_clamp_fusion), kind=kCustom, calls=%fused_computation | custom fusion | bytes 1572960 | tf_op jit(solution)/shard_map/gather | solution.py:36
  3.5 0.1 slice_bitcast_fusion
  3.5 4.0 %collective-permute-start = (bf16[1,4,128,128]{3,2,1,0:T(8,128)(2,1)S(1)}, bf16[1,4,128,128]{3,2,1,0:T(8,128)(2,1)S(1)}, u32[]{:S(2)}, u32[]{:S(2)}) collective-permute-start(bf16[1,4,128,128]{3,2,1,0:T(8,128)(2,1)S(1)} %get-tuple-element.7), channel_id=1, source_target_pairs={{0,32},{32,64},{64,96},{96,128},{128,160},{160,192},{192,224},{224... | collective-permute-start | bytes 393224 | tf_op jit(solution)/shard_map/ppermute | solution.py:29
  7.5 1.3 collective-permute-start.1
  8.8 4.0 %collective-permute-start.2 = (bf16[1,4,128,128]{3,2,1,0:T(8,128)(2,1)S(1)}, bf16[1,4,128,128]{3,2,1,0:T(8,128)(2,1)S(1)}, u32[]{:S(2)}, u32[]{:S(2)}) collective-permute-start(bf16[1,4,128,128]{3,2,1,0:T(8,128)(2,1)S(1)} %get-tuple-element.5), channel_id=1, source_target_pairs={{0,4},{4,8},{8,12},{12,16},{16,20},{20,24},{24,28},{1,5},{5,9},{9,... | collective-permute-start | bytes 393224 | tf_op jit(solution)/shard_map/ppermute | solution.py:29
  12.9 3.4 %collective-permute-start.3 = (bf16[1,4,128,128]{3,2,1,0:T(8,128)(2,1)S(1)}, bf16[1,4,128,128]{3,2,1,0:T(8,128)(2,1)S(1)}, u32[]{:S(2)}, u32[]{:S(2)}) collective-permute-start(bf16[1,4,128,128]{3,2,1,0:T(8,128)(2,1)S(1)} %get-tuple-element.4), channel_id=1, source_target_pairs={{4,0},{8,4},{12,8},{16,12},{20,16},{24,20},{28,24},{5,1},{9,5},{13... | collective-permute-start | bytes 393224 | tf_op jit(solution)/shard_map/ppermute | solution.py:30
  16.2 2.1 %collective-permute-start.4 = (bf16[1,4,128,128]{3,2,1,0:T(8,128)(2,1)S(1)}, bf16[1,4,128,128]{3,2,1,0:T(8,128)(2,1)S(1)}, u32[]{:S(2)}, u32[]{:S(2)}) collective-permute-start(bf16[1,4,128,128]{3,2,1,0:T(8,128)(2,1)S(1)} %get-tuple-element.3), channel_id=1, source_target_pairs={{0,1},{1,2},{2,3},{4,5},{5,6},{6,7},{8,9},{9,10},{10,11},{12,13},{... | collective-permute-start | bytes 393224 | tf_op jit(solution)/shard_map/ppermute | solution.py:29
  18.3 0.0 copy-done.4
  18.3 0.8 copy.31
  19.1 0.0 copy-done.5
  19.2 0.7 copy.39
  21.1 0.0 copy-done
  21.1 1.3 copy.33
  22.5 0.0 collective-permute-done
  22.5 1.3 collective-permute-start.5
  23.8 0.0 collective-permute-done.1
  23.8 0.0 collective-permute-done.2
  23.8 0.0 collective-permute-done.3
  23.9 0.0 collective-permute-done.4
  23.9 4.7 %collective-permute-done.5 = bf16[1,4,128,128]{3,2,1,0:T(8,128)(2,1)S(1)} collective-permute-done((bf16[1,4,128,128]{3,2,1,0:T(8,128)(2,1)S(1)}, bf16[1,4,128,128]{3,2,1,0:T(8,128)(2,1)S(1)}, u32[]{:S(2)}, u32[]{:S(2)}) %collective-permute-start.5) | collective-permute-done | bytes 131104 | tf_op jit(solution)/shard_map/ppermute | solution.py:30
  28.7 0.9 copy-done.2
  29.5 10.9 %weight_pairs.1 = f32[27,128,128]{2,1,0:T(8,128)} custom-call(s32[288,3]{1,0:T(8,128)} %bitcast.51, s32[1]{0:T(128)} %bitcast.38.inner_live_ref, s32[32,3]{1,0:T(8,128)} %bitcast.53, s32[1]{0:T(128)} %bitcast.40.outer_live_ref, bf16[32,128,128]{2,1,0:T(8,128)(2,1)} %bitcast.49, bf16[24,128,128]{2,1,0:T(8,128)(2,1)} %copy-done.2, bf16[32,128,128]{2,1,0:T(8,128)(2,1)} %bitcast.45), custom_call_target="tpu_custom_call" | custom-call | flops 1342177280 | bytes 6291456 | tf_op jit(solution)/shard_map/weight_pairs/pallas_call | solution.py:128
  40.4 27.0 %all_to_all.33 = f32[8,1,55296]{2,1,0:T(1,128)S(1)} all-to-all(f32[8,1,55296]{2,1,0:T(1,128)} %bitcast.43), channel_id=1, replica_groups=mesh['zh'=4,'x'=4,'y'=4,'c'=2,'gz'=4] {'y','c'}, dimensions={0} | all-to-all | bytes 3538944 | tf_op jit(solution)/shard_map/all_to_all | solution.py:154
  67.5 1.3 reduce_sum.27
  68.7 14.7 %all_to_all.34 = f32[4,1,13824]{2,1,0:T(1,128)S(1)} all-to-all(f32[4,1,13824]{2,1,0:T(1,128)S(1)} %bitcast.46), channel_id=1, replica_groups=mesh['zh'=4,'x'=4,'y'=4,'c'=2,'gz'=4] {'x'}, dimensions={0} | all-to-all | bytes 442368 | tf_op jit(solution)/shard_map/all_to_all | solution.py:154
  83.4 0.2 reduce_sum.28
  83.6 0.7 all_to_all.26
  84.4 14.2 %all-to-all-start.2 = ((f32[16,1,864]{2,1,0:T(1,128)}), f32[16,1,864]{2,1,0:T(1,128)S(1)}, u32[]{:S(2)}, u32[]{:S(2)}) async-start(f32[16,1,864]{2,1,0:T(1,128)} %all_to_all.26), calls=%async_computation.2 | async-start | bytes 114688 | tf_op jit(solution)/shard_map/all_to_all | solution.py:154
  98.6 1.6 %copy.32 = bf16[27,128,128]{1,2,0:T(8,128)(2,1)} copy(bf16[27,128,128]{2,1,0:T(8,128)(2,1)S(1)} %copy-done.1) | data formatting | bytes 1769472 | tf_op args[2]
  100.2 10.0 %all-to-all-done.2 = f32[16,1,864]{2,1,0:T(1,128)S(1)} async-done(((f32[16,1,864]{2,1,0:T(1,128)}), f32[16,1,864]{2,1,0:T(1,128)S(1)}, u32[]{:S(2)}, u32[]{:S(2)}) %all-to-all-start.2) | async-done | bytes 55328 | tf_op jit(solution)/shard_map/all_to_all | solution.py:154
  110.3 0.5 broadcast.38
  110.8 0.8 reduce.5
  111.7 0.7 reshape.92
  112.4 3.5 %all-to-all-start.3 = ((bf16[16,2,432]{2,1,0:T(2,128)(2,1)}), bf16[16,2,432]{2,1,0:T(2,128)(2,1)S(1)}, u32[]{:S(2)}, u32[]{:S(2)}) async-start(bf16[16,2,432]{2,1,0:T(2,128)(2,1)} %reshape.92), calls=%async_computation.3 | async-start | bytes 65536 | tf_op jit(solution)/shard_map/all_to_all | solution.py:160
  115.9 0.0 copy-done.3
  115.9 10.8 %input_pairs.1 = bf16[32,128,128]{2,1,0:T(8,128)(2,1)} custom-call(s32[288,3]{1,0:T(8,128)} %bitcast.52, s32[1]{0:T(128)} %bitcast.39.inner_live_ref, s32[32,3]{1,0:T(8,128)} %bitcast.54, s32[1]{0:T(128)} %bitcast.41.outer_live_ref, bf16[32,128,128]{2,1,0:T(8,128)(2,1)} %bitcast.50, bf16[24,128,128]{2,1,0:T(8,128)(2,1)} %copy-done.2, ...), custom_call_target="tpu_custom_call" | custom-call | flops 1342177280 | bytes 6291456 | tf_op jit(solution)/shard_map/input_pairs/pallas_call | solution.py:139
  126.7 0.5 all-to-all-done.3
  127.2 0.1 reshape.93
  127.3 0.2 reduce.3
  127.5 0.1 reshape.87
  127.6 9.3 %all-gather = bf16[4,1,13824]{2,1,0:T(2,128)(2,1)S(1)} all-gather(bf16[1,1,13824]{2,1,0:T(2,128)(2,1)S(1)} %reshape.87), channel_id=1, replica_groups=mesh['zh'=4,'x'=4,'y'=4,'c'=2,'gz'=4] {'x'}, dimensions={0}, use_global_device_ids=true | all-gather | bytes 138240 | tf_op jit(solution)/shard_map/all_gather | solution.py:161
  136.9 0.7 reduce.4
  137.6 21.0 %all_gather.7 = bf16[442368]{0:T(1024)(128)(2,1)S(1)} all-gather(bf16[55296]{0:T(1024)(128)(2,1)S(1)} %reshape.88), channel_id=1, replica_groups=mesh['zh'=4,'x'=4,'y'=4,'c'=2,'gz'=4] {'y','c'}, dimensions={0}, use_global_device_ids=true | all-gather | bytes 995328 | tf_op jit(solution)/shard_map/all_gather | solution.py:162
  158.6 0.9 copy.50
  (16 shorter events, 0.3 us)
Async XLA Ops:
  0.6 17.7 %copy-start.4 = (s32[1,1,1,288,3]{3,2,4,1,0:T(1,128)S(1)}, s32[1,1,1,288,3]{3,2,4,1,0:T(1,128)}, u32[]{:S(2)}) copy-start(s32[1,1,1,288,3]{3,2,4,1,0:T(1,128)} %param.11) | copy-start | bytes 10372
  0.6 18.5 %copy-start.5 = (s32[1,1,1,32,3]{3,2,4,1,0:T(1,128)S(1)}, s32[1,1,1,32,3]{3,2,4,1,0:T(1,128)}, u32[]{:S(2)}) copy-start(s32[1,1,1,32,3]{3,2,4,1,0:T(1,128)} %param.12) | copy-start | bytes 1156
  0.7 20.5 %copy-start = (bf16[1,1,1,4096,128]{4,3,2,1,0:T(8,128)(2,1)S(1)}, bf16[1,1,1,4096,128]{4,3,2,1,0:T(8,128)(2,1)}, u32[]{:S(2)}) copy-start(bf16[1,1,1,4096,128]{4,3,2,1,0:T(8,128)(2,1)} %param.8) | copy-start | bytes 3145732
  3.5 18.9 %collective-permute-start = (bf16[1,4,128,128]{3,2,1,0:T(8,128)(2,1)S(1)}, bf16[1,4,128,128]{3,2,1,0:T(8,128)(2,1)S(1)}, u32[]{:S(2)}, u32[]{:S(2)}) collective-permute-start(bf16[1,4,128,128]{3,2,1,0:T(8,128)(2,1)S(1)} %get-tuple-element.7), channel_id=1, source_target_pairs={{0,32},{32,64},{64,96},{96,128},{128,160},{160,192},{192,224},{224... | collective-permute-start | bytes 393224 | tf_op jit(solution)/shard_map/ppermute | solution.py:29
  7.5 16.3 %collective-permute-start.1 = (bf16[1,4,128,128]{3,2,1,0:T(8,128)(2,1)S(1)}, bf16[1,4,128,128]{3,2,1,0:T(8,128)(2,1)S(1)}, u32[]{:S(2)}, u32[]{:S(2)}) collective-permute-start(bf16[1,4,128,128]{3,2,1,0:T(8,128)(2,1)S(1)} %get-tuple-element.6), channel_id=1, source_target_pairs={{32,0},{64,32},{96,64},{128,96},{160,128},{192,160},{224,192},{256... | collective-permute-start | bytes 393224 | tf_op jit(solution)/shard_map/ppermute | solution.py:30
  8.8 15.0 %collective-permute-start.2 = (bf16[1,4,128,128]{3,2,1,0:T(8,128)(2,1)S(1)}, bf16[1,4,128,128]{3,2,1,0:T(8,128)(2,1)S(1)}, u32[]{:S(2)}, u32[]{:S(2)}) collective-permute-start(bf16[1,4,128,128]{3,2,1,0:T(8,128)(2,1)S(1)} %get-tuple-element.5), channel_id=1, source_target_pairs={{0,4},{4,8},{8,12},{12,16},{16,20},{20,24},{24,28},{1,5},{5,9},{9,... | collective-permute-start | bytes 393224 | tf_op jit(solution)/shard_map/ppermute | solution.py:29
  12.9 11.0 %collective-permute-start.3 = (bf16[1,4,128,128]{3,2,1,0:T(8,128)(2,1)S(1)}, bf16[1,4,128,128]{3,2,1,0:T(8,128)(2,1)S(1)}, u32[]{:S(2)}, u32[]{:S(2)}) collective-permute-start(bf16[1,4,128,128]{3,2,1,0:T(8,128)(2,1)S(1)} %get-tuple-element.4), channel_id=1, source_target_pairs={{4,0},{8,4},{12,8},{16,12},{20,16},{24,20},{28,24},{5,1},{9,5},{13... | collective-permute-start | bytes 393224 | tf_op jit(solution)/shard_map/ppermute | solution.py:30
  16.2 7.6 %collective-permute-start.4 = (bf16[1,4,128,128]{3,2,1,0:T(8,128)(2,1)S(1)}, bf16[1,4,128,128]{3,2,1,0:T(8,128)(2,1)S(1)}, u32[]{:S(2)}, u32[]{:S(2)}) collective-permute-start(bf16[1,4,128,128]{3,2,1,0:T(8,128)(2,1)S(1)} %get-tuple-element.3), channel_id=1, source_target_pairs={{0,1},{1,2},{2,3},{4,5},{5,6},{6,7},{8,9},{9,10},{10,11},{12,13},{... | collective-permute-start | bytes 393224 | tf_op jit(solution)/shard_map/ppermute | solution.py:29
  22.5 6.2 %collective-permute-start.5 = (bf16[1,4,128,128]{3,2,1,0:T(8,128)(2,1)S(1)}, bf16[1,4,128,128]{3,2,1,0:T(8,128)(2,1)S(1)}, u32[]{:S(2)}, u32[]{:S(2)}) collective-permute-start(bf16[1,4,128,128]{3,2,1,0:T(8,128)(2,1)S(1)} %get-tuple-element.2), channel_id=1, source_target_pairs={{1,0},{2,1},{3,2},{5,4},{6,5},{7,6},{9,8},{10,9},{11,10},{13,12},{... | collective-permute-start | bytes 393224 | tf_op jit(solution)/shard_map/ppermute | solution.py:30
  28.6 0.9 copy-start.2
  67.4 31.1 %copy-start.1 = (bf16[27,128,128]{2,1,0:T(8,128)(2,1)S(1)}, bf16[27,128,128]{2,1,0:T(8,128)(2,1)}, u32[]{:S(2)}) copy-start(bf16[27,128,128]{2,1,0:T(8,128)(2,1)} %param.10) | copy-start | bytes 2654212
  84.4 25.8 %all-to-all-start.2 = ((f32[16,1,864]{2,1,0:T(1,128)}), f32[16,1,864]{2,1,0:T(1,128)S(1)}, u32[]{:S(2)}, u32[]{:S(2)}) async-start(f32[16,1,864]{2,1,0:T(1,128)} %all_to_all.26), calls=%async_computation.2 | async-start | bytes 114688 | tf_op jit(solution)/shard_map/all_to_all | solution.py:154
  110.3 5.6 %copy-start.3 = (f32[864]{0:T(1024)}, f32[864]{0:T(1024)S(1)}, u32[]{:S(2)}) copy-start(f32[864]{0:T(1024)S(1)} %reduce_sum.29.after_ref) | copy-start | bytes 10372
  112.4 14.9 %all-to-all-start.3 = ((bf16[16,2,432]{2,1,0:T(2,128)(2,1)}), bf16[16,2,432]{2,1,0:T(2,128)(2,1)S(1)}, u32[]{:S(2)}, u32[]{:S(2)}) async-start(bf16[16,2,432]{2,1,0:T(2,128)(2,1)} %reshape.92), calls=%async_computation.3 | async-start | bytes 65536 | tf_op jit(solution)/shard_map/all_to_all | solution.py:160

commit v12 on v11

--- a/solution.py
+++ b/solution.py
@@ -95,7 +95,12 @@
     return update
 
 
-def weight_kernel(inner_ref, inner_live_ref, outer_ref, outer_live_ref, local_ref, received_ref, ft_ref, acc_w):
+def weight_kernel(inner_ref, inner_live_ref, outer_ref, outer_live_ref, local_ref, received_ref, f_ref, acc_w, ft_ref):
+    def transpose_block(b, carry):
+        ft_ref[b] = f_ref[b].T
+        return carry
+
+    lax.fori_loop(0, NB, transpose_block, 0)
     acc_w[...] = jnp.zeros_like(acc_w)
     update = weight_updater(ft_ref, acc_w)
     pair_loop(inner_ref, inner_live_ref, local_ref, 0, update)
@@ -130,6 +135,7 @@
         out_shape=jax.ShapeDtypeStruct((27, C, C), jnp.float32),
         in_specs=[smem(), smem(), smem(), smem(), vmem(), vmem(), vmem()],
         out_specs=vmem(),
+        scratch_shapes=[pltpu.VMEM((NB, C, BLOCK), jnp.bfloat16)],
         cost_estimate=cost(PI + PB),
         name="weight_pairs",
     )(inner_pairs, inner_n, outer_pairs, outer_n, local, received, ft)
@@ -165,14 +171,14 @@
 
 def body(features, output_grad, kernel, inner_map, outer_map, face_blocks, inner_live, outer_live):
     local_grads = output_grad[0, 0, 0].reshape(NB, BLOCK, C)
-    feats_t = jnp.swapaxes(features[0, 0, 0].reshape(NB, BLOCK, C), 1, 2)
+    feats = features[0, 0, 0].reshape(NB, BLOCK, C)
     kernel_t = jnp.swapaxes(kernel, 1, 2)
     inner_pairs = inner_map[0, 0, 0]
     outer_pairs = outer_map[0, 0, 0]
     inner_n = inner_live[0, 0]
     outer_n = outer_live[0, 0]
     received = received_blocks(local_grads, face_blocks[0, 0, 0])
-    acc_w = run_weights(inner_pairs, inner_n, outer_pairs, outer_n, local_grads, received, feats_t)
+    acc_w = run_weights(inner_pairs, inner_n, outer_pairs, outer_n, local_grads, received, feats)
     bricks_all = lax.axis_size(GX) * lax.axis_size(GY) * lax.axis_size("gz")
     grad_scale = math.sqrt(27.0 / (bricks_all * PI * BLOCK))
     weight_grad, after = reduce_weights(acc_w, grad_scale)

time: 160 us -> 162 us (1.012)
  blocking collectives: 72 us -> 75.8 us
  waiting for transfers between devices: 15.2 us -> 18.2 us
  Pallas kernels: 21.7 us -> 19.1 us
    all_to_all x2, blocking collectives: 41.7 us -> 45.5 us  [reduce_weights(): parts = lax.all_to_all(flat.reshape(n, -1), axis, 0, 0, tiled=True)]
    all_to_all x1, waiting for transfers between devices: 0.54 us -> 2.98 us  [reduce_weights(): piece = lax.all_to_all(copies, ZZ, 0, 0, tiled=True).reshape(-1)]
    pallas_call x1, Pallas kernels: 10.8 us -> 8.36 us  [run_inputs(): pl.pallas_call(input_kernel, out_shape=jax.ShapeDtypeStruct((NB, BLOCK, C...]
    unnamed x24 -> x22, local copies, waits for them, and re-layouts: 5.29 us -> 5.29 us
  transfers between devices with their start and end apart: 8 -> 8, of which waited for: 3 -> 3; matrix products, arithmetic and copies ran while one was open for 3% -> 2% of each run, Pallas kernels for 7% -> 5%
where the time goes in v12:
time: 162 us
  blocking collectives  75.8 us (47%)
  starting transfers between devices  33.3 us (21%)
  Pallas kernels  19.1 us (12%)
  waiting for transfers between devices  18.2 us (11%)
  local copies, waits for them, and re-layouts  10.1 us (6%)
  other arithmetic  3.19 us (2%)
  between operations  2.21 us (1%)
    all_to_all x2, blocking collectives, reduce_weights(): parts = lax.all_to_all(flat.reshape(n, -1), axis, 0, 0, tiled=True)  45.5 us
    all_gather x1, blocking collectives, reduce_weights(): piece = lax.all_gather(piece, GY, tiled=True)  21 us
    all_to_all x1, starting transfers between devices, reduce_weights(): parts = lax.all_to_all(flat.reshape(n, -1), axis, 0, 0, tiled=True)  13.8 us
    pallas_call x1, Pallas kernels, run_weights(): pl.pallas_call(weight_kernel, out_shape=jax.ShapeDtypeStruct((27, C, C),...  10.8 us
    ppermute x3, starting transfers between devices, extended(): before = lax.ppermute(last, axis, up)  10.1 us
    all_to_all x1, waiting for transfers between devices, reduce_weights(): parts = lax.all_to_all(flat.reshape(n, -1), axis, 0, 0, tiled=True)  9.99 us
    all_gather x1, blocking collectives, reduce_weights(): piece = lax.all_gather(piece, 'x', tiled=True)  9.3 us
    pallas_call x1, Pallas kernels, run_inputs(): pl.pallas_call(input_kernel, out_shape=jax.ShapeDtypeStruct((NB, BLOCK, C...  8.36 us
  transfers between devices with their start and end apart: 8, of which 3 were waited for; matrix products, arithmetic and copies ran while one was open for 2% of the time, Pallas kernels for 5%

profile of v12, /device:TPU:1, one launch (start us, length us, event | category | flops | bytes accessed | tf_op | source)
XLA Modules:
  0.0 161.8 jit_solution(16061036185881742252)
XLA Ops:
  0.6 0.0 copy-start.3
  0.6 0.0 copy-start.4
  0.7 0.8 reshape_squeeze.10
  1.4 1.9 %gather_fusion = bf16[24,128,128]{2,1,0:T(8,128)(2,1)S(1)} fusion(bf16[32,128,128]{2,1,0:T(8,128)(2,1)} %bitcast.45, s32[1024]{0:T(1024)S(1)} %pad_clamp_fusion), kind=kCustom, calls=%fused_computation | custom fusion | bytes 1572960 | tf_op jit(solution)/shard_map/gather | solution.py:36
  3.4 0.1 slice_bitcast_fusion
  3.5 4.0 %collective-permute-start = (bf16[1,4,128,128]{3,2,1,0:T(8,128)(2,1)S(1)}, bf16[1,4,128,128]{3,2,1,0:T(8,128)(2,1)S(1)}, u32[]{:S(2)}, u32[]{:S(2)}) collective-permute-start(bf16[1,4,128,128]{3,2,1,0:T(8,128)(2,1)S(1)} %get-tuple-element.7), channel_id=1, source_target_pairs={{0,32},{32,64},{64,96},{96,128},{128,160},{160,192},{192,224},{224... | collective-permute-start | bytes 393224 | tf_op jit(solution)/shard_map/ppermute | solution.py:29
  7.4 1.3 collective-permute-start.1
  8.7 4.0 %collective-permute-start.2 = (bf16[1,4,128,128]{3,2,1,0:T(8,128)(2,1)S(1)}, bf16[1,4,128,128]{3,2,1,0:T(8,128)(2,1)S(1)}, u32[]{:S(2)}, u32[]{:S(2)}) collective-permute-start(bf16[1,4,128,128]{3,2,1,0:T(8,128)(2,1)S(1)} %get-tuple-element.5), channel_id=1, source_target_pairs={{0,4},{4,8},{8,12},{12,16},{16,20},{20,24},{24,28},{1,5},{5,9},{9,... | collective-permute-start | bytes 393224 | tf_op jit(solution)/shard_map/ppermute | solution.py:29
  12.8 3.4 %collective-permute-start.3 = (bf16[1,4,128,128]{3,2,1,0:T(8,128)(2,1)S(1)}, bf16[1,4,128,128]{3,2,1,0:T(8,128)(2,1)S(1)}, u32[]{:S(2)}, u32[]{:S(2)}) collective-permute-start(bf16[1,4,128,128]{3,2,1,0:T(8,128)(2,1)S(1)} %get-tuple-element.4), channel_id=1, source_target_pairs={{4,0},{8,4},{12,8},{16,12},{20,16},{24,20},{28,24},{5,1},{9,5},{13... | collective-permute-start | bytes 393224 | tf_op jit(solution)/shard_map/ppermute | solution.py:30
  16.2 2.1 %collective-permute-start.4 = (bf16[1,4,128,128]{3,2,1,0:T(8,128)(2,1)S(1)}, bf16[1,4,128,128]{3,2,1,0:T(8,128)(2,1)S(1)}, u32[]{:S(2)}, u32[]{:S(2)}) collective-permute-start(bf16[1,4,128,128]{3,2,1,0:T(8,128)(2,1)S(1)} %get-tuple-element.3), channel_id=1, source_target_pairs={{0,1},{1,2},{2,3},{4,5},{5,6},{6,7},{8,9},{9,10},{10,11},{12,13},{... | collective-permute-start | bytes 393224 | tf_op jit(solution)/shard_map/ppermute | solution.py:29
  18.3 0.0 copy-done.3
  18.3 0.8 copy.28
  19.1 0.0 copy-done.4
  19.1 0.7 copy.35
  21.0 0.0 collective-permute-done
  21.1 1.3 collective-permute-start.5
  22.4 0.0 collective-permute-done.1
  22.4 0.0 collective-permute-done.2
  22.4 0.0 collective-permute-done.3
  22.5 0.0 collective-permute-done.4
  22.5 5.2 %collective-permute-done.5 = bf16[1,4,128,128]{3,2,1,0:T(8,128)(2,1)S(1)} collective-permute-done((bf16[1,4,128,128]{3,2,1,0:T(8,128)(2,1)S(1)}, bf16[1,4,128,128]{3,2,1,0:T(8,128)(2,1)S(1)}, u32[]{:S(2)}, u32[]{:S(2)}) %collective-permute-start.5) | collective-permute-done | bytes 131104 | tf_op jit(solution)/shard_map/ppermute | solution.py:30
  27.7 0.0 copy-start.1
  27.7 0.9 copy-done.1
  28.6 10.8 %weight_pairs.1 = f32[27,128,128]{2,1,0:T(8,128)} custom-call(s32[288,3]{1,0:T(8,128)} %bitcast.48, s32[1]{0:T(128)} %bitcast.37.inner_live_ref, s32[32,3]{1,0:T(8,128)} %bitcast.50, s32[1]{0:T(128)} %bitcast.39.outer_live_ref, bf16[32,128,128]{2,1,0:T(8,128)(2,1)} %bitcast.46, bf16[24,128,128]{2,1,0:T(8,128)(2,1)} %copy-done.1, bf16[32,128,128]{2,1,0:T(8,128)(2,1)} %bitcast.52), custom_call_target="tpu_custom_call" | custom-call | flops 1342177280 | bytes 6291456 | tf_op jit(solution)/shard_map/weight_pairs/pallas_call | solution.py:133
  39.3 29.3 %all_to_all.33 = f32[8,1,55296]{2,1,0:T(1,128)S(1)} all-to-all(f32[8,1,55296]{2,1,0:T(1,128)} %bitcast.42), channel_id=1, replica_groups=mesh['zh'=4,'x'=4,'y'=4,'c'=2,'gz'=4] {'y','c'}, dimensions={0} | all-to-all | bytes 3538944 | tf_op jit(solution)/shard_map/all_to_all | solution.py:160
  68.7 0.0 copy-start
  68.7 1.3 reduce_sum.27
  69.9 16.1 %all_to_all.34 = f32[4,1,13824]{2,1,0:T(1,128)S(1)} all-to-all(f32[4,1,13824]{2,1,0:T(1,128)S(1)} %bitcast.43), channel_id=1, replica_groups=mesh['zh'=4,'x'=4,'y'=4,'c'=2,'gz'=4] {'x'}, dimensions={0} | all-to-all | bytes 442368 | tf_op jit(solution)/shard_map/all_to_all | solution.py:160
  86.1 0.2 reduce_sum.28
  86.3 0.7 all_to_all.26
  87.0 13.8 %all-to-all-start.2 = ((f32[16,1,864]{2,1,0:T(1,128)}), f32[16,1,864]{2,1,0:T(1,128)S(1)}, u32[]{:S(2)}, u32[]{:S(2)}) async-start(f32[16,1,864]{2,1,0:T(1,128)} %all_to_all.26), calls=%async_computation.2 | async-start | bytes 114688 | tf_op jit(solution)/shard_map/all_to_all | solution.py:160
  100.8 0.0 copy-done
  100.8 1.6 %copy.29 = bf16[27,128,128]{1,2,0:T(8,128)(2,1)} copy(bf16[27,128,128]{2,1,0:T(8,128)(2,1)S(1)} %copy-done) | data formatting | bytes 1769472 | tf_op args[2]
  102.4 10.0 %all-to-all-done.2 = f32[16,1,864]{2,1,0:T(1,128)S(1)} async-done(((f32[16,1,864]{2,1,0:T(1,128)}), f32[16,1,864]{2,1,0:T(1,128)S(1)}, u32[]{:S(2)}, u32[]{:S(2)}) %all-to-all-start.2) | async-done | bytes 55328 | tf_op jit(solution)/shard_map/all_to_all | solution.py:160
  112.5 0.5 broadcast.38
  113.1 0.8 reduce.5
  113.9 0.7 reshape.92
  114.6 3.5 %all-to-all-start.3 = ((bf16[16,2,432]{2,1,0:T(2,128)(2,1)}), bf16[16,2,432]{2,1,0:T(2,128)(2,1)S(1)}, u32[]{:S(2)}, u32[]{:S(2)}) async-start(bf16[16,2,432]{2,1,0:T(2,128)(2,1)} %reshape.92), calls=%async_computation.3 | async-start | bytes 65536 | tf_op jit(solution)/shard_map/all_to_all | solution.py:166
  118.1 0.0 copy-done.2
  118.1 8.4 %input_pairs.1 = bf16[32,128,128]{2,1,0:T(8,128)(2,1)} custom-call(s32[288,3]{1,0:T(8,128)} %bitcast.49, s32[1]{0:T(128)} %bitcast.38.inner_live_ref, s32[32,3]{1,0:T(8,128)} %bitcast.51, s32[1]{0:T(128)} %bitcast.40.outer_live_ref, bf16[32,128,128]{2,1,0:T(8,128)(2,1)} %bitcast.47, bf16[24,128,128]{2,1,0:T(8,128)(2,1)} %copy-done.1, ...), custom_call_target="tpu_custom_call" | custom-call | flops 1342177280 | bytes 6291456 | tf_op jit(solution)/shard_map/input_pairs/pallas_call | solution.py:145
  126.5 3.0 %all-to-all-done.3 = bf16[16,2,432]{2,1,0:T(2,128)(2,1)S(1)} async-done(((bf16[16,2,432]{2,1,0:T(2,128)(2,1)}), bf16[16,2,432]{2,1,0:T(2,128)(2,1)S(1)}, u32[]{:S(2)}, u32[]{:S(2)}) %all-to-all-start.3) | async-done | bytes 27680 | tf_op jit(solution)/shard_map/all_to_all | solution.py:166
  129.4 0.1 reshape.93
  129.6 0.2 reduce.3
  129.7 0.1 reshape.87
  129.8 9.3 %all-gather = bf16[4,1,13824]{2,1,0:T(2,128)(2,1)S(1)} all-gather(bf16[1,1,13824]{2,1,0:T(2,128)(2,1)S(1)} %reshape.87), channel_id=1, replica_groups=mesh['zh'=4,'x'=4,'y'=4,'c'=2,'gz'=4] {'x'}, dimensions={0}, use_global_device_ids=true | all-gather | bytes 138240 | tf_op jit(solution)/shard_map/all_gather | solution.py:167
  139.1 0.7 reduce.4
  139.9 21.0 %all_gather.7 = bf16[442368]{0:T(1024)(128)(2,1)S(1)} all-gather(bf16[55296]{0:T(1024)(128)(2,1)S(1)} %reshape.88), channel_id=1, replica_groups=mesh['zh'=4,'x'=4,'y'=4,'c'=2,'gz'=4] {'y','c'}, dimensions={0}, use_global_device_ids=true | all-gather | bytes 995328 | tf_op jit(solution)/shard_map/all_gather | solution.py:168
  160.9 0.9 copy.46
  (13 shorter events, 0.3 us)
Async XLA Ops:
  0.6 17.6 %copy-start.3 = (s32[1,1,1,288,3]{3,2,4,1,0:T(1,128)S(1)}, s32[1,1,1,288,3]{3,2,4,1,0:T(1,128)}, u32[]{:S(2)}) copy-start(s32[1,1,1,288,3]{3,2,4,1,0:T(1,128)} %param.11) | copy-start | bytes 10372
  0.6 18.4 %copy-start.4 = (s32[1,1,1,32,3]{3,2,4,1,0:T(1,128)S(1)}, s32[1,1,1,32,3]{3,2,4,1,0:T(1,128)}, u32[]{:S(2)}) copy-start(s32[1,1,1,32,3]{3,2,4,1,0:T(1,128)} %param.12) | copy-start | bytes 1156
  3.5 17.6 %collective-permute-start = (bf16[1,4,128,128]{3,2,1,0:T(8,128)(2,1)S(1)}, bf16[1,4,128,128]{3,2,1,0:T(8,128)(2,1)S(1)}, u32[]{:S(2)}, u32[]{:S(2)}) collective-permute-start(bf16[1,4,128,128]{3,2,1,0:T(8,128)(2,1)S(1)} %get-tuple-element.7), channel_id=1, source_target_pairs={{0,32},{32,64},{64,96},{96,128},{128,160},{160,192},{192,224},{224... | collective-permute-start | bytes 393224 | tf_op jit(solution)/shard_map/ppermute | solution.py:29
  7.4 15.0 %collective-permute-start.1 = (bf16[1,4,128,128]{3,2,1,0:T(8,128)(2,1)S(1)}, bf16[1,4,128,128]{3,2,1,0:T(8,128)(2,1)S(1)}, u32[]{:S(2)}, u32[]{:S(2)}) collective-permute-start(bf16[1,4,128,128]{3,2,1,0:T(8,128)(2,1)S(1)} %get-tuple-element.6), channel_id=1, source_target_pairs={{32,0},{64,32},{96,64},{128,96},{160,128},{192,160},{224,192},{256... | collective-permute-start | bytes 393224 | tf_op jit(solution)/shard_map/ppermute | solution.py:30
  8.7 13.7 %collective-permute-start.2 = (bf16[1,4,128,128]{3,2,1,0:T(8,128)(2,1)S(1)}, bf16[1,4,128,128]{3,2,1,0:T(8,128)(2,1)S(1)}, u32[]{:S(2)}, u32[]{:S(2)}) collective-permute-start(bf16[1,4,128,128]{3,2,1,0:T(8,128)(2,1)S(1)} %get-tuple-element.5), channel_id=1, source_target_pairs={{0,4},{4,8},{8,12},{12,16},{16,20},{20,24},{24,28},{1,5},{5,9},{9,... | collective-permute-start | bytes 393224 | tf_op jit(solution)/shard_map/ppermute | solution.py:29
  12.8 9.7 %collective-permute-start.3 = (bf16[1,4,128,128]{3,2,1,0:T(8,128)(2,1)S(1)}, bf16[1,4,128,128]{3,2,1,0:T(8,128)(2,1)S(1)}, u32[]{:S(2)}, u32[]{:S(2)}) collective-permute-start(bf16[1,4,128,128]{3,2,1,0:T(8,128)(2,1)S(1)} %get-tuple-element.4), channel_id=1, source_target_pairs={{4,0},{8,4},{12,8},{16,12},{20,16},{24,20},{28,24},{5,1},{9,5},{13... | collective-permute-start | bytes 393224 | tf_op jit(solution)/shard_map/ppermute | solution.py:30
  16.2 6.3 %collective-permute-start.4 = (bf16[1,4,128,128]{3,2,1,0:T(8,128)(2,1)S(1)}, bf16[1,4,128,128]{3,2,1,0:T(8,128)(2,1)S(1)}, u32[]{:S(2)}, u32[]{:S(2)}) collective-permute-start(bf16[1,4,128,128]{3,2,1,0:T(8,128)(2,1)S(1)} %get-tuple-element.3), channel_id=1, source_target_pairs={{0,1},{1,2},{2,3},{4,5},{5,6},{6,7},{8,9},{9,10},{10,11},{12,13},{... | collective-permute-start | bytes 393224 | tf_op jit(solution)/shard_map/ppermute | solution.py:29
  21.1 6.6 %collective-permute-start.5 = (bf16[1,4,128,128]{3,2,1,0:T(8,128)(2,1)S(1)}, bf16[1,4,128,128]{3,2,1,0:T(8,128)(2,1)S(1)}, u32[]{:S(2)}, u32[]{:S(2)}) collective-permute-start(bf16[1,4,128,128]{3,2,1,0:T(8,128)(2,1)S(1)} %get-tuple-element.2), channel_id=1, source_target_pairs={{1,0},{2,1},{3,2},{5,4},{6,5},{7,6},{9,8},{10,9},{11,10},{13,12},{... | collective-permute-start | bytes 393224 | tf_op jit(solution)/shard_map/ppermute | solution.py:30
  27.7 0.9 copy-start.1
  68.7 32.1 %copy-start = (bf16[27,128,128]{2,1,0:T(8,128)(2,1)S(1)}, bf16[27,128,128]{2,1,0:T(8,128)(2,1)}, u32[]{:S(2)}) copy-start(bf16[27,128,128]{2,1,0:T(8,128)(2,1)} %param.10) | copy-start | bytes 2654212
  87.0 25.4 %all-to-all-start.2 = ((f32[16,1,864]{2,1,0:T(1,128)}), f32[16,1,864]{2,1,0:T(1,128)S(1)}, u32[]{:S(2)}, u32[]{:S(2)}) async-start(f32[16,1,864]{2,1,0:T(1,128)} %all_to_all.26), calls=%async_computation.2 | async-start | bytes 114688 | tf_op jit(solution)/shard_map/all_to_all | solution.py:160
  112.5 5.6 %copy-start.2 = (f32[864]{0:T(1024)}, f32[864]{0:T(1024)S(1)}, u32[]{:S(2)}) copy-start(f32[864]{0:T(1024)S(1)} %reduce_sum.29.after_ref) | copy-start | bytes 10372
  114.6 14.9 %all-to-all-start.3 = ((bf16[16,2,432]{2,1,0:T(2,128)(2,1)}), bf16[16,2,432]{2,1,0:T(2,128)(2,1)S(1)}, u32[]{:S(2)}, u32[]{:S(2)}) async-start(bf16[16,2,432]{2,1,0:T(2,128)(2,1)} %reshape.92), calls=%async_computation.3 | async-start | bytes 65536 | tf_op jit(solution)/shard_map/all_to_all | solution.py:166
